TPU v7x, 512 devices: a whole 4x8x8 slice. The times are simulated.
512 devices in a mesh: seq: 64 (over z, y), chan: 8 (over x, core).
Axes of the slice: x: 4, y: 8, z: 8, core: 2. Of those that a mesh axis runs over, the one named last changes fastest.
Arguments:
- tokens: bfloat16 [8192, 4096], P('seq', 'chan'), may hold values from -6 to 6
- conv_taps: float32 [4, 4096], P(None, 'chan'), may hold values from -12 to 12
- log_rate: float32 [4096], P('chan'), may hold values from 4.8828125e-06 to 0.034
- rotation: float32 [4096], P('chan'), may hold values from 0 to 0.2
- in_proj: bfloat16 [64, 64, 128], P('chan'), may hold values from -0.75 to 0.75
- out_proj: bfloat16 [64, 64, 128], P('chan'), may hold values from -0.5 to 0.5
- skip_gain: float32 [4096], P('chan'), may hold values from 0.25 to 1.5
- norm_gain: float32 [4096], P('chan'), may hold values from 0.25 to 1.75
- retention: float32 [8192], P('seq'), may hold values from 0.5 to 1
- cotangent: bfloat16 [8192, 4096], P('seq', 'chan'), may hold values from -6 to 6
Outputs:
- normed: bfloat16 [8192, 4096], P('seq', 'chan')
- tokens_grad: bfloat16 [8192, 4096], P('seq', 'chan')
- in_grad: float32 [64, 64, 128], P('chan')
- out_grad: float32 [64, 64, 128], P('chan')
- taps_grad: float32 [4, 4096], P(None, 'chan')
All inputs are finite; a program needn't handle non-finite values.
Results may differ from a plain program's by a relative error of at most 0.011.
Values may be sent and summed in bfloat16 or wider, within the bound.
No kernel may reach another device: no remote copies, remote signals or barrier semaphores. Data moves between devices by JAX's collectives and lax.ppermute only.
A program may use at most 64 MiB of HBM per device.

v0:
```python
import jax
import jax.numpy as jnp
from jax import lax
from jax.sharding import PartitionSpec as P


def from_behind(value, axis, by):
    length = lax.axis_size(axis)
    pairs = [(i, i + by) for i in range(length) if 0 <= i + by < length]
    return lax.ppermute(value, axis, pairs)


def carried_in(part, axis, combine, identity, reverse):
    count = lax.axis_size(axis)
    place = lax.axis_index(axis)
    ahead = count - 1 - place if reverse else place
    step = -1 if reverse else 1
    packed = jnp.stack(part)
    unit = jnp.stack([jnp.zeros_like(a) + jnp.asarray(e, a.dtype) for a, e in zip(part, identity)])
    state = jnp.where(ahead >= 1, from_behind(packed, axis, step), unit)
    reach = 1
    while reach < count:
        earlier = from_behind(state, axis, step * reach)
        joined = jnp.stack(combine(tuple(earlier), tuple(state)))
        state = jnp.where(ahead >= reach, joined, state)
        reach *= 2
    return tuple(state)


def linear_run(drive_re, drive_im, decay_rate, turn_rate, log_keep):
    seq_len, num_cols = drive_re.shape
    block_len = min(64, seq_len)
    block_count = seq_len // block_len
    offsets = jnp.arange(block_len, dtype=jnp.float32)
    keep_cum = jnp.cumsum(log_keep.reshape(block_count, block_len), axis=1)[:, :, None]
    angles = offsets[:, None] * turn_rate[None, :]
    cosine = jnp.cos(angles)
    sine = jnp.sin(angles)
    growth = jnp.exp(offsets[None, :, None] * decay_rate[None, None, :] - keep_cum)
    blk_re = drive_re.reshape(block_count, block_len, num_cols)
    blk_im = drive_im.reshape(block_count, block_len, num_cols)
    pre_re = growth * (blk_re * cosine + blk_im * sine)
    pre_im = growth * (blk_im * cosine - blk_re * sine)
    lower_ones = (offsets[:, None] >= offsets[None, :]).astype(jnp.float32)
    summed = jnp.einsum(
        "ji,abik->abjk", lower_ones, jnp.stack([pre_re, pre_im]), precision=lax.Precision.HIGHEST
    )
    shrink = jnp.exp(keep_cum - offsets[None, :, None] * decay_rate[None, None, :])
    state_re = shrink * (summed[0] * cosine - summed[1] * sine)
    state_im = shrink * (summed[0] * sine + summed[1] * cosine)
    step_mag = jnp.exp(keep_cum[:, -1] - block_len * decay_rate[None, :])
    step_re = step_mag * jnp.cos(block_len * turn_rate)[None, :]
    step_im = step_mag * jnp.sin(block_len * turn_rate)[None, :]

    def advance(carried, inputs):
        carry_re, carry_im = carried
        mult_re, mult_im, end_re, end_im = inputs
        next_re = mult_re * carry_re - mult_im * carry_im + end_re
        next_im = mult_re * carry_im + mult_im * carry_re + end_im
        return ((next_re, next_im), (carry_re, carry_im))

    zeros_col = jnp.zeros((num_cols,), jnp.float32)
    enter_re, enter_im = lax.scan(
        advance, (zeros_col, zeros_col), (step_re, step_im, state_re[:, -1], state_im[:, -1])
    )[1]
    ahead = offsets + 1.0
    lift = jnp.exp(keep_cum - ahead[None, :, None] * decay_rate[None, None, :])
    lift_re = lift * jnp.cos(ahead[:, None] * turn_rate[None, :])
    lift_im = lift * jnp.sin(ahead[:, None] * turn_rate[None, :])
    state_re = state_re + lift_re * enter_re[:, None] - lift_im * enter_im[:, None]
    state_im = state_im + lift_re * enter_im[:, None] + lift_im * enter_re[:, None]
    return (state_re.reshape(seq_len, num_cols), state_im.reshape(seq_len, num_cols))


def carry_combine(earlier, later):
    early_re, early_im, early_sre, early_sim = earlier
    late_re, late_im, late_sre, late_sim = later
    joined_re = early_re * late_re - early_im * late_im
    joined_im = early_re * late_im + early_im * late_re
    joined_sre = late_re * early_sre - late_im * early_sim + late_sre
    joined_sim = late_re * early_sim + late_im * early_sre + late_sim
    return (joined_re, joined_im, joined_sre, joined_sim)


def per_device(
    tokens,
    conv_taps,
    log_rate,
    rotation,
    in_proj,
    out_proj,
    skip_gain,
    norm_gain,
    retention,
    cotangent,
):
    seq_len, local_width = tokens.shape
    tap_count = conv_taps.shape[0]
    local_heads, head_width, double_state = in_proj.shape
    state_size = double_state // 2
    num_cols = local_heads * state_size
    lead_rows = from_behind(tokens[seq_len - (tap_count - 1) :], "seq", 1)
    padded = jnp.concatenate([lead_rows, tokens], axis=0).astype(jnp.float32)
    conv_sum = conv_taps[0][None, :] * padded[tap_count - 1 :]
    for offset in range(1, tap_count):
        conv_sum = (
            conv_sum
            + conv_taps[offset][None, :]
            * padded[tap_count - 1 - offset : tap_count - 1 - offset + seq_len]
        )
    mixed_in = conv_sum.astype(jnp.bfloat16)
    by_head = mixed_in.reshape(seq_len, local_heads, head_width)
    projected = jnp.einsum("thc,hck->thk", by_head, in_proj, preferred_element_type=jnp.float32)
    in_scale = jnp.sqrt(-jnp.expm1(-2.0 * log_rate))
    drive_re = projected[:, :, :state_size].reshape(seq_len, num_cols) * in_scale
    drive_im = projected[:, :, state_size:].reshape(seq_len, num_cols) * in_scale
    log_keep = jnp.log(retention)
    state_re, state_im = linear_run(drive_re, drive_im, log_rate, rotation, log_keep)
    keep_total = jnp.sum(log_keep)
    total_mag = jnp.exp(keep_total - seq_len * log_rate)
    total_re = total_mag * jnp.cos(seq_len * rotation)
    total_im = total_mag * jnp.sin(seq_len * rotation)
    unit_ones = jnp.ones((num_cols,), jnp.float32)
    zeros_col = jnp.zeros((num_cols,), jnp.float32)
    chained = carried_in(
        (total_re, total_im, state_re[-1], state_im[-1]),
        "seq",
        carry_combine,
        (unit_ones, zeros_col, zeros_col, zeros_col),
        False,
    )
    enter_re, enter_im = (chained[2], chained[3])
    positions = jnp.arange(seq_len, dtype=jnp.float32)
    ahead = positions + 1.0
    lift = jnp.exp(jnp.cumsum(log_keep)[:, None] - ahead[:, None] * log_rate[None, :])
    lift_re = lift * jnp.cos(ahead[:, None] * rotation[None, :])
    lift_im = lift * jnp.sin(ahead[:, None] * rotation[None, :])
    state_re = state_re + lift_re * enter_re[None, :] - lift_im * enter_im[None, :]
    state_im = state_im + lift_re * enter_im[None, :] + lift_im * enter_re[None, :]
    state_bf = jnp.concatenate(
        [
            state_re.reshape(seq_len, local_heads, state_size),
            state_im.reshape(seq_len, local_heads, state_size),
        ],
        axis=2,
    ).astype(jnp.bfloat16)
    mixed = jnp.einsum(
        "thk,hck->thc", state_bf, out_proj, preferred_element_type=jnp.float32
    ).reshape(seq_len, local_width)
    mixed = mixed + skip_gain * mixed_in.astype(jnp.float32)
    squares = jnp.sum(mixed * mixed, axis=1)
    scaled = cotangent.astype(jnp.float32) * norm_gain
    dots = jnp.sum(scaled * mixed, axis=1)
    squares = lax.psum(squares, "chan")
    model_width = local_width * lax.axis_size("chan")
    inverse = lax.rsqrt(squares / model_width + 1e-06)
    normed = (mixed * inverse[:, None] * norm_gain).astype(jnp.bfloat16)
    dots = lax.psum(dots, "chan")
    mixed_grad = inverse[:, None] * (
        scaled - mixed * (inverse * inverse * dots / model_width)[:, None]
    )
    grad_bf = mixed_grad.astype(jnp.bfloat16).reshape(seq_len, local_heads, head_width)
    state_grad = jnp.einsum("thc,hck->thk", grad_bf, out_proj, preferred_element_type=jnp.float32)
    out_grad = jnp.einsum("thc,thk->hck", grad_bf, state_bf, preferred_element_type=jnp.float32)
    back_keep = jnp.concatenate([jnp.zeros((1,), jnp.float32), log_keep[::-1][:-1]])
    grad_re = state_grad[:, :, :state_size].reshape(seq_len, num_cols)[::-1]
    grad_im = state_grad[:, :, state_size:].reshape(seq_len, num_cols)[::-1]
    adj_re, adj_im = linear_run(grad_re, grad_im, log_rate, -rotation, back_keep)
    first_mag = jnp.exp(log_keep[0] - log_rate)
    cos_turn = jnp.cos(rotation)
    sin_turn = jnp.sin(rotation)
    first_re = first_mag * (cos_turn * adj_re[-1] + sin_turn * adj_im[-1])
    first_im = first_mag * (cos_turn * adj_im[-1] - sin_turn * adj_re[-1])
    back_chained = carried_in(
        (total_re, -total_im, first_re, first_im),
        "seq",
        carry_combine,
        (unit_ones, zeros_col, zeros_col, zeros_col),
        True,
    )
    later_re, later_im = (back_chained[2], back_chained[3])
    back_lift = jnp.exp(jnp.cumsum(back_keep)[:, None] - positions[:, None] * log_rate[None, :])
    back_re = back_lift * jnp.cos(positions[:, None] * rotation[None, :])
    back_im = -back_lift * jnp.sin(positions[:, None] * rotation[None, :])
    adj_re = adj_re + back_re * later_re[None, :] - back_im * later_im[None, :]
    adj_im = adj_im + back_re * later_im[None, :] + back_im * later_re[None, :]
    adj_re = adj_re[::-1]
    adj_im = adj_im[::-1]
    drive_grad = jnp.concatenate(
        [
            (in_scale * adj_re).reshape(seq_len, local_heads, state_size),
            (in_scale * adj_im).reshape(seq_len, local_heads, state_size),
        ],
        axis=2,
    ).astype(jnp.bfloat16)
    in_grad = jnp.einsum("thc,thk->hck", by_head, drive_grad, preferred_element_type=jnp.float32)
    input_grad = jnp.einsum(
        "thk,hck->thc", drive_grad, in_proj, preferred_element_type=jnp.float32
    ).reshape(seq_len, local_width)
    input_grad = input_grad + skip_gain * mixed_grad
    trail_rows = from_behind(input_grad[: tap_count - 1], "seq", -1)
    tail = jnp.concatenate([input_grad, trail_rows], axis=0)
    tokens_grad = conv_taps[0][None, :] * tail[:seq_len]
    for offset in range(1, tap_count):
        tokens_grad = tokens_grad + conv_taps[offset][None, :] * tail[offset : offset + seq_len]
    taps_grad = jnp.stack(
        [
            jnp.sum(
                input_grad * padded[tap_count - 1 - offset : tap_count - 1 - offset + seq_len],
                axis=0,
            )
            for offset in range(tap_count)
        ]
    )
    in_grad, out_grad, taps_grad = lax.psum((in_grad, out_grad, taps_grad), "seq")
    return (normed, tokens_grad.astype(jnp.bfloat16), in_grad, out_grad, taps_grad)


def solution(mesh):
    in_specs = (
        P("seq", "chan"),
        P(None, "chan"),
        P("chan"),
        P("chan"),
        P("chan", None, None),
        P("chan", None, None),
        P("chan"),
        P("chan"),
        P("seq"),
        P("seq", "chan"),
    )
    out_specs = (
        P("seq", "chan"),
        P("seq", "chan"),
        P("chan", None, None),
        P("chan", None, None),
        P(None, "chan"),
    )
    return jax.shard_map(
        per_device, mesh=mesh, in_specs=in_specs, out_specs=out_specs, check_vma=False
    )
```

profile of v0, /device:TPU:56, one launch (start us, length us, event | category | flops | bytes accessed | tf_op | source)
XLA Modules:
  0.0 358.1 jit_solution(17775567052841719686)
XLA Ops:
  7.2 0.7 slice.117
  8.2 3.5 collective-permute-start
  14.8 1.3 fusion.68
  16.1 2.5 multiply_cosine_fusion.1
  18.7 0.8 subtract_exponential_fusion.1
  21.0 1.1 fusion.18
  26.5 0.8 multiply_subtract_fusion.13
  27.3 3.5 collective-permute-start.1
  30.8 2.0 collective-permute-done.1
  32.8 5.6 %collective-permute-start.2 = (f32[4,512]{1,0:T(4,128)S(1)}, f32[4,512]{1,0:T(4,128)S(1)}, u32[]{:S(2)}, u32[]{:S(2)}) collective-permute-start(f32[4,512]{1,0:T(4,128)S(1)} %broadcast_select_fusion.5), channel_id=1, source_target_pairs={{0,8},{8,16},{16,24},{24,32},{32,40},{40,48},{48,56},{56,64},{64,7... | collective-permute-start | bytes 24584 | tf_op jit(solution)/shard_map/ppermute | solution.py:10
  38.4 1.3 collective-permute-done.2
  39.8 3.6 %collective-permute-start.3 = (f32[4,512]{1,0:T(4,128)S(1)}, f32[4,512]{1,0:T(4,128)S(1)}, u32[]{:S(2)}, u32[]{:S(2)}) collective-permute-start(f32[4,512]{1,0:T(4,128)S(1)} %maximum_select_fusion), channel_id=1, source_target_pairs={{0,16},{8,24},{16,32},{24,40},{32,48},{40,56},{48,64},{56,72},{64,... | collective-permute-start | bytes 24584 | tf_op jit(solution)/shard_map/ppermute | solution.py:10
  43.5 2.8 collective-permute-done.3
  46.4 6.3 %collective-permute-start.4 = (f32[4,512]{1,0:T(4,128)S(1)}, f32[4,512]{1,0:T(4,128)S(1)}, u32[]{:S(2)}, u32[]{:S(2)}) collective-permute-start(f32[4,512]{1,0:T(4,128)S(1)} %maximum_select_fusion.1), channel_id=1, source_target_pairs={{0,32},{8,40},{16,48},{24,56},{32,64},{40,72},{48,80},{56,88},{64,... | collective-permute-start | bytes 24584 | tf_op jit(solution)/shard_map/ppermute | solution.py:10
  52.7 3.1 collective-permute-done.4
  55.9 4.3 %collective-permute-start.5 = (f32[4,512]{1,0:T(4,128)S(1)}, f32[4,512]{1,0:T(4,128)S(1)}, u32[]{:S(2)}, u32[]{:S(2)}) collective-permute-start(f32[4,512]{1,0:T(4,128)S(1)} %maximum_select_fusion.2), channel_id=1, source_target_pairs={{0,64},{8,72},{16,80},{24,88},{32,96},{40,104},{48,112},{56,120},{... | collective-permute-start | bytes 24584 | tf_op jit(solution)/shard_map/ppermute | solution.py:10
  60.2 1.3 collective-permute-done.5
  61.6 8.5 %collective-permute-start.6 = (f32[4,512]{1,0:T(4,128)S(1)}, f32[4,512]{1,0:T(4,128)S(1)}, u32[]{:S(2)}, u32[]{:S(2)}) collective-permute-start(f32[4,512]{1,0:T(4,128)S(1)} %maximum_select_fusion.3), channel_id=1, source_target_pairs={{0,128},{8,136},{16,144},{24,152},{32,160},{40,168},{48,176},{56,1... | collective-permute-start | bytes 24584 | tf_op jit(solution)/shard_map/ppermute | solution.py:10
  70.2 1.3 collective-permute-done.6
  72.8 9.7 %collective-permute-start.7 = (f32[4,512]{1,0:T(4,128)}, f32[4,512]{1,0:T(4,128)}, u32[]{:S(2)}, u32[]{:S(2)}) collective-permute-start(f32[4,512]{1,0:T(4,128)} %maximum_select_fusion.4), channel_id=1, source_target_pairs={{0,256},{8,264},{16,272},{24,280},{32,288},{40,296},{48,304},{56,3... | collective-permute-start | bytes 24584 | tf_op jit(solution)/shard_map/ppermute | solution.py:10
  85.2 0.8 sub.356
  85.9 1.1 sub.357
  87.0 0.9 copy.130
  88.0 0.9 copy.136
  88.9 0.9 copy.138
  90.0 0.9 copy.139
  91.1 0.9 copy.140
  92.2 0.9 copy.142
  95.5 0.8 copy-done.2
  96.4 0.8 copy-done.5
  97.4 1.1 squeeze.79
  98.5 0.9 copy.141
  99.4 0.9 copy.143
  100.3 0.9 copy.135
  101.6 1.0 multiply_subtract_fusion.7
  104.1 2.7 subtract_convert_fusion
  108.2 12.6 %all-reduce.1 = (f32[128]{0:T(128)S(1)}, f32[128]{0:T(128)S(1)}) all-reduce(f32[128]{0:T(128)S(1)} %get-tuple-element.185, f32[128]{0:T(128)S(1)} %get-tuple-element.184), channel_id=1, replica_groups=mesh['seq'=64,'chan'=8] {'chan'}, use_global_device_ids=true, to_apply=%region_6.7 | all-reduce | flops 256 | bytes 2048 | tf_op jit(solution)/shard_map/psum | solution.py:154
  123.9 0.8 add_multiply_fusion.2
  128.2 5.4 %collective-permute-start.8 = (f32[4,512]{1,0:T(4,128)S(1)}, f32[4,512]{1,0:T(4,128)S(1)}, u32[]{:S(2)}, u32[]{:S(2)}) collective-permute-start(f32[4,512]{1,0:T(4,128)S(1)} %fusion.50), channel_id=1, source_target_pairs={{8,0},{16,8},{24,16},{32,24},{40,32},{48,40},{56,48},{64,56},{72,6... | collective-permute-start | bytes 24584 | tf_op jit(solution)/shard_map/ppermute | solution.py:10
  133.6 7.6 %collective-permute-done.8 = f32[4,512]{1,0:T(4,128)S(1)} collective-permute-done((f32[4,512]{1,0:T(4,128)S(1)}, f32[4,512]{1,0:T(4,128)S(1)}, u32[]{:S(2)}, u32[]{:S(2)}) %collective-permute-start.8) | collective-permute-done | bytes 8224 | tf_op jit(solution)/shard_map/ppermute | solution.py:10
  141.2 1.9 collective-permute-start.9
  143.1 5.7 %collective-permute-done.9 = f32[4,512]{1,0:T(4,128)S(1)} collective-permute-done((f32[4,512]{1,0:T(4,128)S(1)}, f32[4,512]{1,0:T(4,128)S(1)}, u32[]{:S(2)}, u32[]{:S(2)}) %collective-permute-start.9) | collective-permute-done | bytes 8224 | tf_op jit(solution)/shard_map/ppermute | solution.py:10
  148.9 1.9 collective-permute-start.10
  150.8 6.6 %collective-permute-done.10 = f32[4,512]{1,0:T(4,128)S(1)} collective-permute-done((f32[4,512]{1,0:T(4,128)S(1)}, f32[4,512]{1,0:T(4,128)S(1)}, u32[]{:S(2)}, u32[]{:S(2)}) %collective-permute-start.10) | collective-permute-done | bytes 8224 | tf_op jit(solution)/shard_map/ppermute | solution.py:10
  157.5 1.9 collective-permute-start.11
  159.4 8.4 %collective-permute-done.11 = f32[4,512]{1,0:T(4,128)S(1)} collective-permute-done((f32[4,512]{1,0:T(4,128)S(1)}, f32[4,512]{1,0:T(4,128)S(1)}, u32[]{:S(2)}, u32[]{:S(2)}) %collective-permute-start.11) | collective-permute-done | bytes 8224 | tf_op jit(solution)/shard_map/ppermute | solution.py:10
  167.9 1.3 collective-permute-start.12
  169.2 4.2 %collective-permute-done.12 = f32[4,512]{1,0:T(4,128)S(1)} collective-permute-done((f32[4,512]{1,0:T(4,128)S(1)}, f32[4,512]{1,0:T(4,128)S(1)}, u32[]{:S(2)}, u32[]{:S(2)}) %collective-permute-start.12) | collective-permute-done | bytes 8224 | tf_op jit(solution)/shard_map/ppermute | solution.py:10
  173.5 1.3 collective-permute-start.13
  175.8 4.1 %collective-permute-done.13 = f32[4,512]{1,0:T(4,128)S(1)} collective-permute-done((f32[4,512]{1,0:T(4,128)S(1)}, f32[4,512]{1,0:T(4,128)S(1)}, u32[]{:S(2)}, u32[]{:S(2)}) %collective-permute-start.13) | collective-permute-done | bytes 8224 | tf_op jit(solution)/shard_map/ppermute | solution.py:10
  180.0 1.3 collective-permute-start.14
  181.3 1.0 fusion.35
  182.3 7.2 %collective-permute-done.14 = f32[4,512]{1,0:T(4,128)S(1)} collective-permute-done((f32[4,512]{1,0:T(4,128)S(1)}, f32[4,512]{1,0:T(4,128)S(1)}, u32[]{:S(2)}, u32[]{:S(2)}) %collective-permute-start.14) | collective-permute-done | bytes 8224 | tf_op jit(solution)/shard_map/ppermute | solution.py:10
  190.2 1.1 multiply_subtract_fusion
  192.9 0.7 copy-done.10
  193.9 1.0 fusion.42
  195.0 0.7 multiply_reduce_fusion.3
  195.7 1.9 collective-permute-start.15
  197.6 0.8 copy.162
  198.4 130.4 %psum.39 = f32[4,512]{1,0:T(4,128)} all-reduce(f32[4,512]{1,0:T(4,128)S(1)} %pad_maximum_fusion.9), channel_id=1, replica_groups=mesh['seq'=64,'chan'=8] {'seq'}, use_global_device_ids=true, to_apply=%region_19.20 | all-reduce | flops 2048 | bytes 16384 | tf_op jit(solution)/shard_map/psum | solution.py:215
  328.8 0.7 fusion.28
  329.6 0.8 copy.163
  330.4 18.4 %all-reduce.4.cloned.1.call-done = (f32[8,64,128]{2,1,0:T(8,128)}, f32[8,64,128]{2,1,0:T(8,128)}) async-done(((f32[8,64,128]{2,1,0:T(8,128)}, f32[8,64,128]{2,1,0:T(8,128)}), (f32[8,64,128]{2,1,0:T(8,128)}, f32[8,64,128]{2,1,0:T(8,128)})) %all-reduce.4.cloned.1.call-update) | async-done | bytes 524304 | tf_op jit(solution)/shard_map/psum | solution.py:215
  348.8 1.7 copy.219
  (337 shorter events, 30.5 us)
Async XLA Ops:
  7.2 99.6 %copy-start = (bf16[8,64,128]{2,1,0:T(8,128)(2,1)S(1)}, bf16[8,64,128]{2,1,0:T(8,128)(2,1)}, u32[]{:S(2)}) copy-start(bf16[8,64,128]{2,1,0:T(8,128)(2,1)} %param.19) | copy-start | bytes 393220
  7.2 341.6 %all-reduce.4.cloned.1.call-start = ((), (), s32[]{:S(2)}) async-start(), calls=%async_computation | async-start | bytes 1048576 | tf_op jit(solution)/shard_map/psum | solution.py:215
  8.1 3.5 copy-start.88
  8.2 13.9 %collective-permute-start = (bf16[3,512]{0,1:T(8,128)(2,1)S(1)}, bf16[3,512]{0,1:T(8,128)(2,1)S(1)}, u32[]{:S(2)}, u32[]{:S(2)}) collective-permute-start(bf16[3,512]{0,1:T(8,128)(2,1)S(1)} %copy.131), channel_id=1, source_target_pairs={{0,8},{8,16},{16,24},{24,32},{32,40},{40,48},{48,56},{56,64},{64,7... | collective-permute-start | bytes 9224 | tf_op jit(solution)/shard_map/ppermute | solution.py:10
  14.1 70.4 %copy-start.72 = (f32[2,64]{1,0:T(2,128)}, f32[2,64]{1,0:T(2,128)S(1)}, u32[]{:S(2)}) copy-start(f32[2,64]{1,0:T(2,128)S(1)} %reduce.6) | copy-start | bytes 1540
  16.1 8.5 %copy-start.57 = (f32[512]{0:T(512)}, f32[512]{0:T(512)S(1)}, u32[]{:S(2)}) copy-start(f32[512]{0:T(512)S(1)} %get-tuple-element.354) | copy-start | bytes 6148
  16.1 11.1 %copy-start.59 = (f32[512]{0:T(512)}, f32[512]{0:T(512)S(1)}, u32[]{:S(2)}) copy-start(f32[512]{0:T(512)S(1)} %get-tuple-element.350) | copy-start | bytes 6148
  18.7 1.5 copy-start.14
  20.2 2.1 copy-start.49
  20.2 2.1 copy-start.51
  20.2 2.1 copy-start.53
  20.2 2.1 copy-start.55
  27.3 5.6 %copy-start.16 = (f32[4,512]{1,0:T(4,128)S(1)}, f32[4,512]{1,0:T(4,128)}, u32[]{:S(2)}) copy-start(f32[4,512]{1,0:T(4,128)} %constant.73.clone.1) | copy-start | bytes 24580
  27.3 5.5 %collective-permute-start.1 = (f32[4,512]{1,0:T(4,128)S(1)}, f32[4,512]{1,0:T(4,128)S(1)}, u32[]{:S(2)}, u32[]{:S(2)}) collective-permute-start(f32[4,512]{1,0:T(4,128)S(1)} %fusion.48), channel_id=1, source_target_pairs={{0,8},{8,16},{16,24},{24,32},{32,40},{40,48},{48,56},{56,64},{64,7... | collective-permute-start | bytes 24584 | tf_op jit(solution)/shard_map/ppermute | solution.py:10
  32.8 6.9 %collective-permute-start.2 = (f32[4,512]{1,0:T(4,128)S(1)}, f32[4,512]{1,0:T(4,128)S(1)}, u32[]{:S(2)}, u32[]{:S(2)}) collective-permute-start(f32[4,512]{1,0:T(4,128)S(1)} %broadcast_select_fusion.5), channel_id=1, source_target_pairs={{0,8},{8,16},{16,24},{24,32},{32,40},{40,48},{48,56},{56,64},{64,7... | collective-permute-start | bytes 24584 | tf_op jit(solution)/shard_map/ppermute | solution.py:10
  39.8 6.4 %collective-permute-start.3 = (f32[4,512]{1,0:T(4,128)S(1)}, f32[4,512]{1,0:T(4,128)S(1)}, u32[]{:S(2)}, u32[]{:S(2)}) collective-permute-start(f32[4,512]{1,0:T(4,128)S(1)} %maximum_select_fusion), channel_id=1, source_target_pairs={{0,16},{8,24},{16,32},{24,40},{32,48},{40,56},{48,64},{56,72},{64,... | collective-permute-start | bytes 24584 | tf_op jit(solution)/shard_map/ppermute | solution.py:10
  46.3 25.3 %copy-start.17 = (f32[1,512]{1,0:T(1,128)}, f32[1,512]{1,0:T(1,128)S(1)}, u32[]{:S(2)}) copy-start(f32[1,512]{1,0:T(1,128)S(1)} %get-tuple-element.317) | copy-start | bytes 6148
  46.3 25.3 %copy-start.19 = (f32[1,512]{1,0:T(1,128)}, f32[1,512]{1,0:T(1,128)S(1)}, u32[]{:S(2)}) copy-start(f32[1,512]{1,0:T(1,128)S(1)} %get-tuple-element.318) | copy-start | bytes 6148
  46.3 25.3 %copy-start.21 = (f32[1,512]{1,0:T(1,128)}, f32[1,512]{1,0:T(1,128)S(1)}, u32[]{:S(2)}) copy-start(f32[1,512]{1,0:T(1,128)S(1)} %get-tuple-element.319) | copy-start | bytes 6148
  46.3 25.3 %copy-start.23 = (f32[1,512]{1,0:T(1,128)}, f32[1,512]{1,0:T(1,128)S(1)}, u32[]{:S(2)}) copy-start(f32[1,512]{1,0:T(1,128)S(1)} %get-tuple-element.320) | copy-start | bytes 6148
  46.4 9.5 %collective-permute-start.4 = (f32[4,512]{1,0:T(4,128)S(1)}, f32[4,512]{1,0:T(4,128)S(1)}, u32[]{:S(2)}, u32[]{:S(2)}) collective-permute-start(f32[4,512]{1,0:T(4,128)S(1)} %maximum_select_fusion.1), channel_id=1, source_target_pairs={{0,32},{8,40},{16,48},{24,56},{32,64},{40,72},{48,80},{56,88},{64,... | collective-permute-start | bytes 24584 | tf_op jit(solution)/shard_map/ppermute | solution.py:10
  55.8 15.8 %copy-start.29 = (f32[1,512]{1,0:T(1,128)}, f32[1,512]{1,0:T(1,128)S(1)}, u32[]{:S(2)}) copy-start(f32[1,512]{1,0:T(1,128)S(1)} %get-tuple-element.313) | copy-start | bytes 6148
  55.8 15.8 %copy-start.31 = (f32[1,512]{1,0:T(1,128)}, f32[1,512]{1,0:T(1,128)S(1)}, u32[]{:S(2)}) copy-start(f32[1,512]{1,0:T(1,128)S(1)} %get-tuple-element.314) | copy-start | bytes 6148
  55.8 15.8 %copy-start.33 = (f32[1,512]{1,0:T(1,128)}, f32[1,512]{1,0:T(1,128)S(1)}, u32[]{:S(2)}) copy-start(f32[1,512]{1,0:T(1,128)S(1)} %get-tuple-element.315) | copy-start | bytes 6148
  55.9 15.8 %copy-start.35 = (f32[1,512]{1,0:T(1,128)}, f32[1,512]{1,0:T(1,128)S(1)}, u32[]{:S(2)}) copy-start(f32[1,512]{1,0:T(1,128)S(1)} %get-tuple-element.316) | copy-start | bytes 6148
  55.9 5.6 %collective-permute-start.5 = (f32[4,512]{1,0:T(4,128)S(1)}, f32[4,512]{1,0:T(4,128)S(1)}, u32[]{:S(2)}, u32[]{:S(2)}) collective-permute-start(f32[4,512]{1,0:T(4,128)S(1)} %maximum_select_fusion.2), channel_id=1, source_target_pairs={{0,64},{8,72},{16,80},{24,88},{32,96},{40,104},{48,112},{56,120},{... | collective-permute-start | bytes 24584 | tf_op jit(solution)/shard_map/ppermute | solution.py:10
  61.6 10.1 %copy-start.41 = (f32[1,512]{1,0:T(1,128)}, f32[1,512]{1,0:T(1,128)S(1)}, u32[]{:S(2)}) copy-start(f32[1,512]{1,0:T(1,128)S(1)} %get-tuple-element.309) | copy-start | bytes 6148
  61.6 10.1 %copy-start.43 = (f32[1,512]{1,0:T(1,128)}, f32[1,512]{1,0:T(1,128)S(1)}, u32[]{:S(2)}) copy-start(f32[1,512]{1,0:T(1,128)S(1)} %get-tuple-element.310) | copy-start | bytes 6148
  61.6 10.1 %copy-start.45 = (f32[1,512]{1,0:T(1,128)}, f32[1,512]{1,0:T(1,128)S(1)}, u32[]{:S(2)}) copy-start(f32[1,512]{1,0:T(1,128)S(1)} %get-tuple-element.311) | copy-start | bytes 6148
  61.6 10.1 %copy-start.47 = (f32[1,512]{1,0:T(1,128)}, f32[1,512]{1,0:T(1,128)S(1)}, u32[]{:S(2)}) copy-start(f32[1,512]{1,0:T(1,128)S(1)} %get-tuple-element.312) | copy-start | bytes 6148
  61.6 9.9 %collective-permute-start.6 = (f32[4,512]{1,0:T(4,128)S(1)}, f32[4,512]{1,0:T(4,128)S(1)}, u32[]{:S(2)}, u32[]{:S(2)}) collective-permute-start(f32[4,512]{1,0:T(4,128)S(1)} %maximum_select_fusion.3), channel_id=1, source_target_pairs={{0,128},{8,136},{16,144},{24,152},{32,160},{40,168},{48,176},{56,1... | collective-permute-start | bytes 24584 | tf_op jit(solution)/shard_map/ppermute | solution.py:10
  71.5 1.2 copy-start.67
  72.8 28.7 %collective-permute-start.7 = (f32[4,512]{1,0:T(4,128)}, f32[4,512]{1,0:T(4,128)}, u32[]{:S(2)}, u32[]{:S(2)}) collective-permute-start(f32[4,512]{1,0:T(4,128)} %maximum_select_fusion.4), channel_id=1, source_target_pairs={{0,256},{8,264},{16,272},{24,280},{32,288},{40,296},{48,304},{56,3... | collective-permute-start | bytes 24584 | tf_op jit(solution)/shard_map/ppermute | solution.py:10
  95.3 0.9 copy-start.2
  96.3 0.9 copy-start.5
  100.3 2.3 copy-start.68
  101.2 2.2 copy-start.6
  101.2 2.2 copy-start.7
  101.2 2.2 copy-start.8
  101.5 1.1 copy-start.22
  101.5 1.1 copy-start.24
  101.5 1.1 copy-start.30
  101.5 1.1 copy-start.32
  101.5 1.1 copy-start.34
  101.5 1.1 copy-start.36
  101.5 1.1 copy-start.42
  101.5 1.1 copy-start.44
  101.5 1.1 copy-start.46
  101.6 1.1 copy-start.48
  101.6 1.1 copy-start.62
  101.6 1.1 copy-start.64
  101.6 1.1 copy-start.66
  123.1 1.7 copy-start.38
  123.1 2.7 copy-start.11
  123.1 2.7 copy-start.12
  128.2 13.0 %collective-permute-start.8 = (f32[4,512]{1,0:T(4,128)S(1)}, f32[4,512]{1,0:T(4,128)S(1)}, u32[]{:S(2)}, u32[]{:S(2)}) collective-permute-start(f32[4,512]{1,0:T(4,128)S(1)} %fusion.50), channel_id=1, source_target_pairs={{8,0},{16,8},{24,16},{32,24},{40,32},{48,40},{56,48},{64,56},{72,6... | collective-permute-start | bytes 24584 | tf_op jit(solution)/shard_map/ppermute | solution.py:10
  141.2 7.6 %collective-permute-start.9 = (f32[4,512]{1,0:T(4,128)S(1)}, f32[4,512]{1,0:T(4,128)S(1)}, u32[]{:S(2)}, u32[]{:S(2)}) collective-permute-start(f32[4,512]{1,0:T(4,128)S(1)} %broadcast_select_fusion.4), channel_id=1, source_target_pairs={{8,0},{16,8},{24,16},{32,24},{40,32},{48,40},{56,48},{64,56},{72,6... | collective-permute-start | bytes 24584 | tf_op jit(solution)/shard_map/ppermute | solution.py:10
  148.9 8.6 %collective-permute-start.10 = (f32[4,512]{1,0:T(4,128)S(1)}, f32[4,512]{1,0:T(4,128)S(1)}, u32[]{:S(2)}, u32[]{:S(2)}) collective-permute-start(f32[4,512]{1,0:T(4,128)S(1)} %maximum_select_fusion.6), channel_id=1, source_target_pairs={{16,0},{24,8},{32,16},{40,24},{48,32},{56,40},{64,48},{72,56},{80,... | collective-permute-start | bytes 24584 | tf_op jit(solution)/shard_map/ppermute | solution.py:10
  157.5 10.4 %collective-permute-start.11 = (f32[4,512]{1,0:T(4,128)S(1)}, f32[4,512]{1,0:T(4,128)S(1)}, u32[]{:S(2)}, u32[]{:S(2)}) collective-permute-start(f32[4,512]{1,0:T(4,128)S(1)} %maximum_select_fusion.7), channel_id=1, source_target_pairs={{32,0},{40,8},{48,16},{56,24},{64,32},{72,40},{80,48},{88,56},{96,... | collective-permute-start | bytes 24584 | tf_op jit(solution)/shard_map/ppermute | solution.py:10
  167.9 5.5 %collective-permute-start.12 = (f32[4,512]{1,0:T(4,128)S(1)}, f32[4,512]{1,0:T(4,128)S(1)}, u32[]{:S(2)}, u32[]{:S(2)}) collective-permute-start(f32[4,512]{1,0:T(4,128)S(1)} %maximum_select_fusion.8), channel_id=1, source_target_pairs={{64,0},{72,8},{80,16},{88,24},{96,32},{104,40},{112,48},{120,56},{... | collective-permute-start | bytes 24584 | tf_op jit(solution)/shard_map/ppermute | solution.py:10
  173.5 6.4 %collective-permute-start.13 = (f32[4,512]{1,0:T(4,128)S(1)}, f32[4,512]{1,0:T(4,128)S(1)}, u32[]{:S(2)}, u32[]{:S(2)}) collective-permute-start(f32[4,512]{1,0:T(4,128)S(1)} %maximum_select_fusion.9), channel_id=1, source_target_pairs={{128,0},{136,8},{144,16},{152,24},{160,32},{168,40},{176,48},{184,... | collective-permute-start | bytes 24584 | tf_op jit(solution)/shard_map/ppermute | solution.py:10
  180.0 9.5 %collective-permute-start.14 = (f32[4,512]{1,0:T(4,128)S(1)}, f32[4,512]{1,0:T(4,128)S(1)}, u32[]{:S(2)}, u32[]{:S(2)}) collective-permute-start(f32[4,512]{1,0:T(4,128)S(1)} %maximum_select_fusion.10), channel_id=1, source_target_pairs={{256,0},{264,8},{272,16},{280,24},{288,32},{296,40},{304,48},{312,... | collective-permute-start | bytes 24584 | tf_op jit(solution)/shard_map/ppermute | solution.py:10
  195.7 133.2 %collective-permute-start.15 = (f32[3,512]{0,1:T(8,128)S(1)}, f32[3,512]{0,1:T(8,128)S(1)}, u32[]{:S(2)}, u32[]{:S(2)}) collective-permute-start(f32[3,512]{0,1:T(8,128)S(1)} %bitcast.242), channel_id=1, source_target_pairs={{8,0},{16,8},{24,16},{32,24},{40,32},{48,40},{56,48},{64,56},{72,6... | collective-permute-start | bytes 18440 | tf_op jit(solution)/shard_map/ppermute | solution.py:10
  348.8 1.7 copy-start.13
  (43 other events, 29.4 us)
Sparse Core Ops, SparseCore 0:
  195.1 153.6 all-reduce.3
where the time goes:
time: 361 us; the launch traced here: 358 us
  blocking collectives  143 us (40%)
  waiting for transfers between devices  74.3 us (21%)
  starting transfers between devices  62 us (17%)
  local copies, waits for them, and re-layouts  38.1 us (11%)
  other arithmetic  20.8 us (6%)
  between operations  15.7 us (4%)
  matrix products  3.88 us (1%)
    psum x1, blocking collectives, per_device(): lax.psum((in_grad, out_grad, taps_grad), 'seq')  130 us
    ppermute x16, starting transfers between devices, from_behind(): return lax.ppermute(value, axis, pairs)  61.9 us
    ppermute x16, waiting for transfers between devices, from_behind(): return lax.ppermute(value, axis, pairs)  55.9 us
    psum x1, waiting for transfers between devices, per_device(): lax.psum((in_grad, out_grad, taps_grad), 'seq')  18.4 us
    unnamed x189, local copies, waits for them, and re-layouts  17 us
    psum x1, blocking collectives, per_device(): squares = lax.psum(squares, 'chan')  12.6 us
  transfers between devices with their start and end apart: 17, of which 14 were waited for; matrix products, arithmetic and copies ran while one was open for 9% of the time, Pallas kernels for 0%

commit v1 on v0

--- a/solution.py
+++ b/solution.py
@@ -1,7 +1,9 @@
 import jax
 import jax.numpy as jnp
 from jax import lax
-from jax.sharding import PartitionSpec as P
+from jax.sharding import Mesh, PartitionSpec as P
+
+SEQ = ("z", "y")
 
 
 def from_behind(value, axis, by):
@@ -99,7 +101,7 @@
     local_heads, head_width, double_state = in_proj.shape
     state_size = double_state // 2
     num_cols = local_heads * state_size
-    lead_rows = from_behind(tokens[seq_len - (tap_count - 1) :], "seq", 1)
+    lead_rows = from_behind(tokens[seq_len - (tap_count - 1) :], SEQ, 1)
     padded = jnp.concatenate([lead_rows, tokens], axis=0).astype(jnp.float32)
     conv_sum = conv_taps[0][None, :] * padded[tap_count - 1 :]
     for offset in range(1, tap_count):
@@ -124,7 +126,7 @@
     zeros_col = jnp.zeros((num_cols,), jnp.float32)
     chained = carried_in(
         (total_re, total_im, state_re[-1], state_im[-1]),
-        "seq",
+        SEQ,
         carry_combine,
         (unit_ones, zeros_col, zeros_col, zeros_col),
         False,
@@ -162,6 +164,7 @@
     grad_bf = mixed_grad.astype(jnp.bfloat16).reshape(seq_len, local_heads, head_width)
     state_grad = jnp.einsum("thc,hck->thk", grad_bf, out_proj, preferred_element_type=jnp.float32)
     out_grad = jnp.einsum("thc,thk->hck", grad_bf, state_bf, preferred_element_type=jnp.float32)
+    out_grad = lax.psum(lax.psum(out_grad, "y"), "z")
     back_keep = jnp.concatenate([jnp.zeros((1,), jnp.float32), log_keep[::-1][:-1]])
     grad_re = state_grad[:, :, :state_size].reshape(seq_len, num_cols)[::-1]
     grad_im = state_grad[:, :, state_size:].reshape(seq_len, num_cols)[::-1]
@@ -173,7 +176,7 @@
     first_im = first_mag * (cos_turn * adj_im[-1] - sin_turn * adj_re[-1])
     back_chained = carried_in(
         (total_re, -total_im, first_re, first_im),
-        "seq",
+        SEQ,
         carry_combine,
         (unit_ones, zeros_col, zeros_col, zeros_col),
         True,
@@ -198,7 +201,7 @@
         "thk,hck->thc", drive_grad, in_proj, preferred_element_type=jnp.float32
     ).reshape(seq_len, local_width)
     input_grad = input_grad + skip_gain * mixed_grad
-    trail_rows = from_behind(input_grad[: tap_count - 1], "seq", -1)
+    trail_rows = from_behind(input_grad[: tap_count - 1], SEQ, -1)
     tail = jnp.concatenate([input_grad, trail_rows], axis=0)
     tokens_grad = conv_taps[0][None, :] * tail[:seq_len]
     for offset in range(1, tap_count):
@@ -212,13 +215,22 @@
             for offset in range(tap_count)
         ]
     )
-    in_grad, out_grad, taps_grad = lax.psum((in_grad, out_grad, taps_grad), "seq")
+    packed = jnp.concatenate([in_grad.reshape(-1), taps_grad.reshape(-1)])
+    packed = lax.psum(lax.psum(packed, "y"), "z")
+    in_grad = packed[: in_grad.size].reshape(in_grad.shape)
+    taps_grad = packed[in_grad.size :].reshape(taps_grad.shape)
     return (normed, tokens_grad.astype(jnp.bfloat16), in_grad, out_grad, taps_grad)
 
 
 def solution(mesh):
+    seq_count, chan_count = mesh.devices.shape
+    inner = 1
+    while inner * inner < seq_count:
+        inner *= 2
+    devices = mesh.devices.reshape(seq_count // inner, inner, chan_count)
+    mesh = Mesh(devices, SEQ + ("chan",))
     in_specs = (
-        P("seq", "chan"),
+        P(SEQ, "chan"),
         P(None, "chan"),
         P("chan"),
         P("chan"),
@@ -226,12 +238,12 @@
         P("chan", None, None),
         P("chan"),
         P("chan"),
-        P("seq"),
-        P("seq", "chan"),
+        P(SEQ),
+        P(SEQ, "chan"),
     )
     out_specs = (
-        P("seq", "chan"),
-        P("seq", "chan"),
+        P(SEQ, "chan"),
+        P(SEQ, "chan"),
         P("chan", None, None),
         P("chan", None, None),
         P(None, "chan"),

time: 361 us -> 366 us (1.014)
  waiting for transfers between devices: 74.3 us -> 209 us
  blocking collectives: 143 us -> 12.6 us
    psum x1 -> x0, blocking collectives: 130 us -> none  [per_device(): lax.psum((in_grad, out_grad, taps_grad), 'seq')]
    psum x1 -> x2, waiting for transfers between devices: 18.4 us -> 146 us  [per_device(): packed = lax.psum(lax.psum(packed, 'y'), 'z')]
    ppermute x16, waiting for transfers between devices: 55.9 us -> 62.9 us  [from_behind(): return lax.ppermute(value, axis, pairs)]
  transfers between devices with their start and end apart: 17 -> 18, of which waited for: 14 -> 16; matrix products, arithmetic and copies ran while one was open for 9% -> 8% of each run, Pallas kernels for 0% -> 0%
where the time goes in v1:
time: 366 us; the launch traced here: 364 us
  waiting for transfers between devices  209 us (57%)
  starting transfers between devices  62.6 us (17%)
  local copies, waits for them, and re-layouts  39.3 us (11%)
  other arithmetic  21.6 us (6%)
  between operations  15.8 us (4%)
  blocking collectives  12.6 us (3%)
    psum x2, waiting for transfers between devices, per_device(): packed = lax.psum(lax.psum(packed, 'y'), 'z')  146 us
    ppermute x16, waiting for transfers between devices, from_behind(): return lax.ppermute(value, axis, pairs)  62.9 us
    ppermute x16, starting transfers between devices, from_behind(): return lax.ppermute(value, axis, pairs)  62.5 us
    unnamed x189, local copies, waits for them, and re-layouts  15.2 us
    psum x1, blocking collectives, per_device(): squares = lax.psum(squares, 'chan')  12.6 us
  transfers between devices with their start and end apart: 18, of which 16 were waited for; matrix products, arithmetic and copies ran while one was open for 8% of the time, Pallas kernels for 0%

profile of v1, /device:TPU:56, one launch (start us, length us, event | category | flops | bytes accessed | tf_op | source)
XLA Modules:
  0.0 364.1 jit_solution(13326804845153230500)
XLA Ops:
  7.2 0.7 slice.133
  8.2 3.5 collective-permute-start
  14.9 1.3 fusion.68
  16.2 2.5 multiply_cosine_fusion.1
  18.7 0.8 subtract_exponential_fusion.1
  21.0 1.0 fusion.18
  26.4 0.8 multiply_subtract_fusion.13
  27.2 3.5 collective-permute-start.1
  30.7 2.0 collective-permute-done.1
  32.8 5.6 %collective-permute-start.2 = (f32[4,512]{1,0:T(4,128)S(1)}, f32[4,512]{1,0:T(4,128)S(1)}, u32[]{:S(2)}, u32[]{:S(2)}) collective-permute-start(f32[4,512]{1,0:T(4,128)S(1)} %broadcast_select_fusion.5), channel_id=1, source_target_pairs={{0,8},{8,16},{16,24},{24,32},{32,40},{40,48},{48,56},{56,64},{64,7... | collective-permute-start | bytes 24584 | tf_op jit(solution)/shard_map/ppermute | solution.py:12
  38.4 1.3 collective-permute-done.2
  39.7 3.6 %collective-permute-start.3 = (f32[4,512]{1,0:T(4,128)S(1)}, f32[4,512]{1,0:T(4,128)S(1)}, u32[]{:S(2)}, u32[]{:S(2)}) collective-permute-start(f32[4,512]{1,0:T(4,128)S(1)} %maximum_select_fusion), channel_id=1, source_target_pairs={{0,16},{8,24},{16,32},{24,40},{32,48},{40,56},{48,64},{56,72},{64,... | collective-permute-start | bytes 24584 | tf_op jit(solution)/shard_map/ppermute | solution.py:12
  43.4 2.8 collective-permute-done.3
  46.3 6.3 %collective-permute-start.4 = (f32[4,512]{1,0:T(4,128)S(1)}, f32[4,512]{1,0:T(4,128)S(1)}, u32[]{:S(2)}, u32[]{:S(2)}) collective-permute-start(f32[4,512]{1,0:T(4,128)S(1)} %maximum_select_fusion.1), channel_id=1, source_target_pairs={{0,32},{8,40},{16,48},{24,56},{32,64},{40,72},{48,80},{56,88},{64,... | collective-permute-start | bytes 24584 | tf_op jit(solution)/shard_map/ppermute | solution.py:12
  52.6 3.1 collective-permute-done.4
  55.8 4.3 %collective-permute-start.5 = (f32[4,512]{1,0:T(4,128)S(1)}, f32[4,512]{1,0:T(4,128)S(1)}, u32[]{:S(2)}, u32[]{:S(2)}) collective-permute-start(f32[4,512]{1,0:T(4,128)S(1)} %maximum_select_fusion.2), channel_id=1, source_target_pairs={{0,64},{8,72},{16,80},{24,88},{32,96},{40,104},{48,112},{56,120},{... | collective-permute-start | bytes 24584 | tf_op jit(solution)/shard_map/ppermute | solution.py:12
  60.1 1.3 collective-permute-done.5
  61.6 8.5 %collective-permute-start.6 = (f32[4,512]{1,0:T(4,128)S(1)}, f32[4,512]{1,0:T(4,128)S(1)}, u32[]{:S(2)}, u32[]{:S(2)}) collective-permute-start(f32[4,512]{1,0:T(4,128)S(1)} %maximum_select_fusion.3), channel_id=1, source_target_pairs={{0,128},{8,136},{16,144},{24,152},{32,160},{40,168},{48,176},{56,1... | collective-permute-start | bytes 24584 | tf_op jit(solution)/shard_map/ppermute | solution.py:12
  70.1 1.3 collective-permute-done.6
  72.7 9.6 %collective-permute-start.7 = (f32[4,512]{1,0:T(4,128)}, f32[4,512]{1,0:T(4,128)}, u32[]{:S(2)}, u32[]{:S(2)}) collective-permute-start(f32[4,512]{1,0:T(4,128)} %maximum_select_fusion.4), channel_id=1, source_target_pairs={{0,256},{8,264},{16,272},{24,280},{32,288},{40,296},{48,304},{56,3... | collective-permute-start | bytes 24584 | tf_op jit(solution)/shard_map/ppermute | solution.py:12
  85.2 0.7 sub.356
  85.9 1.1 sub.357
  87.0 0.9 copy.130
  87.9 0.9 copy.136
  88.9 0.9 copy.138
  90.0 0.9 copy.139
  91.0 0.9 copy.140
  92.1 0.9 copy.142
  95.5 0.8 copy-done.2
  96.4 0.8 copy-done.5
  97.4 1.1 squeeze.79
  98.5 0.9 copy.141
  99.4 0.9 copy.143
  100.3 0.9 copy.135
  101.6 0.9 multiply_subtract_fusion.7
  104.1 2.7 subtract_convert_fusion
  108.2 12.6 %all-reduce = (f32[128]{0:T(128)S(1)}, f32[128]{0:T(128)S(1)}) all-reduce(f32[128]{0:T(128)S(1)} %get-tuple-element.185, f32[128]{0:T(128)S(1)} %get-tuple-element.184), channel_id=1, replica_groups=mesh['z'=8,'y'=8,'chan'=8] {'chan'}, use_global_device_ids=true, to_apply=%region_6.7 | all-reduce | flops 256 | bytes 2048 | tf_op jit(solution)/shard_map/psum | solution.py:156
  123.9 0.8 add_multiply_fusion.2
  128.2 5.4 %collective-permute-start.8 = (f32[4,512]{1,0:T(4,128)S(1)}, f32[4,512]{1,0:T(4,128)S(1)}, u32[]{:S(2)}, u32[]{:S(2)}) collective-permute-start(f32[4,512]{1,0:T(4,128)S(1)} %fusion.50), channel_id=1, source_target_pairs={{8,0},{16,8},{24,16},{32,24},{40,32},{48,40},{56,48},{64,56},{72,6... | collective-permute-start | bytes 24584 | tf_op jit(solution)/shard_map/ppermute | solution.py:12
  133.6 7.6 %collective-permute-done.8 = f32[4,512]{1,0:T(4,128)S(1)} collective-permute-done((f32[4,512]{1,0:T(4,128)S(1)}, f32[4,512]{1,0:T(4,128)S(1)}, u32[]{:S(2)}, u32[]{:S(2)}) %collective-permute-start.8) | collective-permute-done | bytes 8224 | tf_op jit(solution)/shard_map/ppermute | solution.py:12
  141.2 1.9 collective-permute-start.9
  143.1 5.7 %collective-permute-done.9 = f32[4,512]{1,0:T(4,128)S(1)} collective-permute-done((f32[4,512]{1,0:T(4,128)S(1)}, f32[4,512]{1,0:T(4,128)S(1)}, u32[]{:S(2)}, u32[]{:S(2)}) %collective-permute-start.9) | collective-permute-done | bytes 8224 | tf_op jit(solution)/shard_map/ppermute | solution.py:12
  148.9 1.9 collective-permute-start.10
  150.8 6.6 %collective-permute-done.10 = f32[4,512]{1,0:T(4,128)S(1)} collective-permute-done((f32[4,512]{1,0:T(4,128)S(1)}, f32[4,512]{1,0:T(4,128)S(1)}, u32[]{:S(2)}, u32[]{:S(2)}) %collective-permute-start.10) | collective-permute-done | bytes 8224 | tf_op jit(solution)/shard_map/ppermute | solution.py:12
  157.5 1.9 collective-permute-start.11
  159.4 8.4 %collective-permute-done.11 = f32[4,512]{1,0:T(4,128)S(1)} collective-permute-done((f32[4,512]{1,0:T(4,128)S(1)}, f32[4,512]{1,0:T(4,128)S(1)}, u32[]{:S(2)}, u32[]{:S(2)}) %collective-permute-start.11) | collective-permute-done | bytes 8224 | tf_op jit(solution)/shard_map/ppermute | solution.py:12
  167.9 1.3 collective-permute-start.12
  169.2 4.2 %collective-permute-done.12 = f32[4,512]{1,0:T(4,128)S(1)} collective-permute-done((f32[4,512]{1,0:T(4,128)S(1)}, f32[4,512]{1,0:T(4,128)S(1)}, u32[]{:S(2)}, u32[]{:S(2)}) %collective-permute-start.12) | collective-permute-done | bytes 8224 | tf_op jit(solution)/shard_map/ppermute | solution.py:12
  173.5 1.3 collective-permute-start.13
  175.8 4.1 %collective-permute-done.13 = f32[4,512]{1,0:T(4,128)S(1)} collective-permute-done((f32[4,512]{1,0:T(4,128)S(1)}, f32[4,512]{1,0:T(4,128)S(1)}, u32[]{:S(2)}, u32[]{:S(2)}) %collective-permute-start.13) | collective-permute-done | bytes 8224 | tf_op jit(solution)/shard_map/ppermute | solution.py:12
  180.0 1.3 collective-permute-start.14
  181.3 1.0 fusion.35
  182.3 7.2 %collective-permute-done.14 = f32[4,512]{1,0:T(4,128)S(1)} collective-permute-done((f32[4,512]{1,0:T(4,128)S(1)}, f32[4,512]{1,0:T(4,128)S(1)}, u32[]{:S(2)}, u32[]{:S(2)}) %collective-permute-start.14) | collective-permute-done | bytes 8224 | tf_op jit(solution)/shard_map/ppermute | solution.py:12
  190.3 1.1 multiply_subtract_fusion
  194.1 0.7 multiply_reduce_fusion.3
  194.9 0.7 pad_maximum_fusion
  195.7 75.9 %all-reduce.6.cloned.1.call-done = (f32[67584]{0:T(1024)}, f32[8,64,128]{2,1,0:T(8,128)}) async-done(((f32[67584]{0:T(1024)}, f32[8,64,128]{2,1,0:T(8,128)}), (f32[67584]{0:T(1024)}, f32[8,64,128]{2,1,0:T(8,128)})) %all-reduce.6.cloned.1.call-update) | async-done | bytes 532496 | tf_op jit(solution)/shard_map/psum | solution.py:219
  271.6 2.5 collective-permute-start.15
  274.1 0.8 copy.162
  274.8 7.1 %collective-permute-done.15 = f32[3,512]{0,1:T(8,128)S(1)} collective-permute-done((f32[3,512]{0,1:T(8,128)S(1)}, f32[3,512]{0,1:T(8,128)S(1)}, u32[]{:S(2)}, u32[]{:S(2)}) %collective-permute-start.15) | collective-permute-done | bytes 6176 | tf_op jit(solution)/shard_map/ppermute | solution.py:12
  282.0 0.7 fusion.28
  282.7 0.8 copy.163
  283.5 70.0 %all-reduce.8.cloned.1.call-done = (f32[67584]{0:T(1024)}, f32[8,64,128]{2,1,0:T(8,128)}) async-done(((f32[67584]{0:T(1024)}, f32[8,64,128]{2,1,0:T(8,128)}), (f32[67584]{0:T(1024)}, f32[8,64,128]{2,1,0:T(8,128)})) %all-reduce.8.cloned.1.call-update) | async-done | bytes 532496 | tf_op jit(solution)/shard_map/psum | solution.py:219
  353.5 1.7 slice.228
  (343 shorter events, 33.0 us)
Async XLA Ops:
  7.2 99.6 %copy-start = (bf16[8,64,128]{2,1,0:T(8,128)(2,1)S(1)}, bf16[8,64,128]{2,1,0:T(8,128)(2,1)}, u32[]{:S(2)}) copy-start(bf16[8,64,128]{2,1,0:T(8,128)(2,1)} %param.19) | copy-start | bytes 393220
  7.2 264.4 %all-reduce.6.cloned.1.call-start = ((), (), s32[]{:S(2)}) async-start(), calls=%async_computation | async-start | bytes 1064960 | tf_op jit(solution)/shard_map/psum | solution.py:219
  8.1 3.5 copy-start.88
  8.2 13.9 %collective-permute-start = (bf16[3,512]{0,1:T(8,128)(2,1)S(1)}, bf16[3,512]{0,1:T(8,128)(2,1)S(1)}, u32[]{:S(2)}, u32[]{:S(2)}) collective-permute-start(bf16[3,512]{0,1:T(8,128)(2,1)S(1)} %copy.131), channel_id=1, source_target_pairs={{0,8},{8,16},{16,24},{24,32},{32,40},{40,48},{48,56},{56,64},{64,7... | collective-permute-start | bytes 9224 | tf_op jit(solution)/shard_map/ppermute | solution.py:12
  14.2 70.4 %copy-start.72 = (f32[2,64]{1,0:T(2,128)}, f32[2,64]{1,0:T(2,128)S(1)}, u32[]{:S(2)}) copy-start(f32[2,64]{1,0:T(2,128)S(1)} %reduce.6) | copy-start | bytes 1540
  16.2 8.3 %copy-start.57 = (f32[512]{0:T(512)}, f32[512]{0:T(512)S(1)}, u32[]{:S(2)}) copy-start(f32[512]{0:T(512)S(1)} %get-tuple-element.356) | copy-start | bytes 6148
  16.2 11.0 %copy-start.59 = (f32[512]{0:T(512)}, f32[512]{0:T(512)S(1)}, u32[]{:S(2)}) copy-start(f32[512]{0:T(512)S(1)} %get-tuple-element.352) | copy-start | bytes 6148
  18.7 1.5 copy-start.14
  20.2 2.0 copy-start.49
  20.2 2.0 copy-start.51
  20.3 2.0 copy-start.53
  20.3 2.0 copy-start.55
  27.2 5.5 %collective-permute-start.1 = (f32[4,512]{1,0:T(4,128)S(1)}, f32[4,512]{1,0:T(4,128)S(1)}, u32[]{:S(2)}, u32[]{:S(2)}) collective-permute-start(f32[4,512]{1,0:T(4,128)S(1)} %fusion.48), channel_id=1, source_target_pairs={{0,8},{8,16},{16,24},{24,32},{32,40},{40,48},{48,56},{56,64},{64,7... | collective-permute-start | bytes 24584 | tf_op jit(solution)/shard_map/ppermute | solution.py:12
  30.7 2.1 copy-start.16
  32.8 6.9 %collective-permute-start.2 = (f32[4,512]{1,0:T(4,128)S(1)}, f32[4,512]{1,0:T(4,128)S(1)}, u32[]{:S(2)}, u32[]{:S(2)}) collective-permute-start(f32[4,512]{1,0:T(4,128)S(1)} %broadcast_select_fusion.5), channel_id=1, source_target_pairs={{0,8},{8,16},{16,24},{24,32},{32,40},{40,48},{48,56},{56,64},{64,7... | collective-permute-start | bytes 24584 | tf_op jit(solution)/shard_map/ppermute | solution.py:12
  39.7 6.4 %collective-permute-start.3 = (f32[4,512]{1,0:T(4,128)S(1)}, f32[4,512]{1,0:T(4,128)S(1)}, u32[]{:S(2)}, u32[]{:S(2)}) collective-permute-start(f32[4,512]{1,0:T(4,128)S(1)} %maximum_select_fusion), channel_id=1, source_target_pairs={{0,16},{8,24},{16,32},{24,40},{32,48},{40,56},{48,64},{56,72},{64,... | collective-permute-start | bytes 24584 | tf_op jit(solution)/shard_map/ppermute | solution.py:12
  46.2 25.3 %copy-start.17 = (f32[1,512]{1,0:T(1,128)}, f32[1,512]{1,0:T(1,128)S(1)}, u32[]{:S(2)}) copy-start(f32[1,512]{1,0:T(1,128)S(1)} %get-tuple-element.319) | copy-start | bytes 6148
  46.2 25.3 %copy-start.19 = (f32[1,512]{1,0:T(1,128)}, f32[1,512]{1,0:T(1,128)S(1)}, u32[]{:S(2)}) copy-start(f32[1,512]{1,0:T(1,128)S(1)} %get-tuple-element.320) | copy-start | bytes 6148
  46.2 25.3 %copy-start.21 = (f32[1,512]{1,0:T(1,128)}, f32[1,512]{1,0:T(1,128)S(1)}, u32[]{:S(2)}) copy-start(f32[1,512]{1,0:T(1,128)S(1)} %get-tuple-element.321) | copy-start | bytes 6148
  46.2 25.3 %copy-start.23 = (f32[1,512]{1,0:T(1,128)}, f32[1,512]{1,0:T(1,128)S(1)}, u32[]{:S(2)}) copy-start(f32[1,512]{1,0:T(1,128)S(1)} %get-tuple-element.322) | copy-start | bytes 6148
  46.3 9.5 %collective-permute-start.4 = (f32[4,512]{1,0:T(4,128)S(1)}, f32[4,512]{1,0:T(4,128)S(1)}, u32[]{:S(2)}, u32[]{:S(2)}) collective-permute-start(f32[4,512]{1,0:T(4,128)S(1)} %maximum_select_fusion.1), channel_id=1, source_target_pairs={{0,32},{8,40},{16,48},{24,56},{32,64},{40,72},{48,80},{56,88},{64,... | collective-permute-start | bytes 24584 | tf_op jit(solution)/shard_map/ppermute | solution.py:12
  55.8 15.8 %copy-start.29 = (f32[1,512]{1,0:T(1,128)}, f32[1,512]{1,0:T(1,128)S(1)}, u32[]{:S(2)}) copy-start(f32[1,512]{1,0:T(1,128)S(1)} %get-tuple-element.315) | copy-start | bytes 6148
  55.8 15.8 %copy-start.31 = (f32[1,512]{1,0:T(1,128)}, f32[1,512]{1,0:T(1,128)S(1)}, u32[]{:S(2)}) copy-start(f32[1,512]{1,0:T(1,128)S(1)} %get-tuple-element.316) | copy-start | bytes 6148
  55.8 15.8 %copy-start.33 = (f32[1,512]{1,0:T(1,128)}, f32[1,512]{1,0:T(1,128)S(1)}, u32[]{:S(2)}) copy-start(f32[1,512]{1,0:T(1,128)S(1)} %get-tuple-element.317) | copy-start | bytes 6148
  55.8 15.8 %copy-start.35 = (f32[1,512]{1,0:T(1,128)}, f32[1,512]{1,0:T(1,128)S(1)}, u32[]{:S(2)}) copy-start(f32[1,512]{1,0:T(1,128)S(1)} %get-tuple-element.318) | copy-start | bytes 6148
  55.8 5.6 %collective-permute-start.5 = (f32[4,512]{1,0:T(4,128)S(1)}, f32[4,512]{1,0:T(4,128)S(1)}, u32[]{:S(2)}, u32[]{:S(2)}) collective-permute-start(f32[4,512]{1,0:T(4,128)S(1)} %maximum_select_fusion.2), channel_id=1, source_target_pairs={{0,64},{8,72},{16,80},{24,88},{32,96},{40,104},{48,112},{56,120},{... | collective-permute-start | bytes 24584 | tf_op jit(solution)/shard_map/ppermute | solution.py:12
  61.5 10.1 %copy-start.41 = (f32[1,512]{1,0:T(1,128)}, f32[1,512]{1,0:T(1,128)S(1)}, u32[]{:S(2)}) copy-start(f32[1,512]{1,0:T(1,128)S(1)} %get-tuple-element.311) | copy-start | bytes 6148
  61.5 10.1 %copy-start.43 = (f32[1,512]{1,0:T(1,128)}, f32[1,512]{1,0:T(1,128)S(1)}, u32[]{:S(2)}) copy-start(f32[1,512]{1,0:T(1,128)S(1)} %get-tuple-element.312) | copy-start | bytes 6148
  61.5 10.1 %copy-start.45 = (f32[1,512]{1,0:T(1,128)}, f32[1,512]{1,0:T(1,128)S(1)}, u32[]{:S(2)}) copy-start(f32[1,512]{1,0:T(1,128)S(1)} %get-tuple-element.313) | copy-start | bytes 6148
  61.5 10.1 %copy-start.47 = (f32[1,512]{1,0:T(1,128)}, f32[1,512]{1,0:T(1,128)S(1)}, u32[]{:S(2)}) copy-start(f32[1,512]{1,0:T(1,128)S(1)} %get-tuple-element.314) | copy-start | bytes 6148
  61.6 9.9 %collective-permute-start.6 = (f32[4,512]{1,0:T(4,128)S(1)}, f32[4,512]{1,0:T(4,128)S(1)}, u32[]{:S(2)}, u32[]{:S(2)}) collective-permute-start(f32[4,512]{1,0:T(4,128)S(1)} %maximum_select_fusion.3), channel_id=1, source_target_pairs={{0,128},{8,136},{16,144},{24,152},{32,160},{40,168},{48,176},{56,1... | collective-permute-start | bytes 24584 | tf_op jit(solution)/shard_map/ppermute | solution.py:12
  71.5 1.2 copy-start.67
  72.7 28.7 %collective-permute-start.7 = (f32[4,512]{1,0:T(4,128)}, f32[4,512]{1,0:T(4,128)}, u32[]{:S(2)}, u32[]{:S(2)}) collective-permute-start(f32[4,512]{1,0:T(4,128)} %maximum_select_fusion.4), channel_id=1, source_target_pairs={{0,256},{8,264},{16,272},{24,280},{32,288},{40,296},{48,304},{56,3... | collective-permute-start | bytes 24584 | tf_op jit(solution)/shard_map/ppermute | solution.py:12
  93.0 1.0 copy-start.15
  100.3 2.2 copy-start.68
  101.2 2.3 copy-start.6
  101.2 2.3 copy-start.7
  101.2 2.3 copy-start.8
  101.4 1.1 copy-start.22
  101.5 1.1 copy-start.24
  101.5 1.1 copy-start.30
  101.5 1.1 copy-start.32
  101.5 1.1 copy-start.34
  101.5 1.1 copy-start.36
  101.5 1.1 copy-start.42
  101.5 1.1 copy-start.44
  101.5 1.1 copy-start.46
  101.5 1.1 copy-start.48
  101.5 1.1 copy-start.62
  101.6 1.1 copy-start.64
  101.6 1.1 copy-start.66
  123.1 1.7 copy-start.38
  123.1 2.7 copy-start.11
  123.1 2.7 copy-start.12
  128.2 13.0 %collective-permute-start.8 = (f32[4,512]{1,0:T(4,128)S(1)}, f32[4,512]{1,0:T(4,128)S(1)}, u32[]{:S(2)}, u32[]{:S(2)}) collective-permute-start(f32[4,512]{1,0:T(4,128)S(1)} %fusion.50), channel_id=1, source_target_pairs={{8,0},{16,8},{24,16},{32,24},{40,32},{48,40},{56,48},{64,56},{72,6... | collective-permute-start | bytes 24584 | tf_op jit(solution)/shard_map/ppermute | solution.py:12
  141.2 7.6 %collective-permute-start.9 = (f32[4,512]{1,0:T(4,128)S(1)}, f32[4,512]{1,0:T(4,128)S(1)}, u32[]{:S(2)}, u32[]{:S(2)}) collective-permute-start(f32[4,512]{1,0:T(4,128)S(1)} %broadcast_select_fusion.4), channel_id=1, source_target_pairs={{8,0},{16,8},{24,16},{32,24},{40,32},{48,40},{56,48},{64,56},{72,6... | collective-permute-start | bytes 24584 | tf_op jit(solution)/shard_map/ppermute | solution.py:12
  148.9 8.6 %collective-permute-start.10 = (f32[4,512]{1,0:T(4,128)S(1)}, f32[4,512]{1,0:T(4,128)S(1)}, u32[]{:S(2)}, u32[]{:S(2)}) collective-permute-start(f32[4,512]{1,0:T(4,128)S(1)} %maximum_select_fusion.6), channel_id=1, source_target_pairs={{16,0},{24,8},{32,16},{40,24},{48,32},{56,40},{64,48},{72,56},{80,... | collective-permute-start | bytes 24584 | tf_op jit(solution)/shard_map/ppermute | solution.py:12
  157.5 10.4 %collective-permute-start.11 = (f32[4,512]{1,0:T(4,128)S(1)}, f32[4,512]{1,0:T(4,128)S(1)}, u32[]{:S(2)}, u32[]{:S(2)}) collective-permute-start(f32[4,512]{1,0:T(4,128)S(1)} %maximum_select_fusion.7), channel_id=1, source_target_pairs={{32,0},{40,8},{48,16},{56,24},{64,32},{72,40},{80,48},{88,56},{96,... | collective-permute-start | bytes 24584 | tf_op jit(solution)/shard_map/ppermute | solution.py:12
  167.9 5.5 %collective-permute-start.12 = (f32[4,512]{1,0:T(4,128)S(1)}, f32[4,512]{1,0:T(4,128)S(1)}, u32[]{:S(2)}, u32[]{:S(2)}) collective-permute-start(f32[4,512]{1,0:T(4,128)S(1)} %maximum_select_fusion.8), channel_id=1, source_target_pairs={{64,0},{72,8},{80,16},{88,24},{96,32},{104,40},{112,48},{120,56},{... | collective-permute-start | bytes 24584 | tf_op jit(solution)/shard_map/ppermute | solution.py:12
  173.5 6.4 %collective-permute-start.13 = (f32[4,512]{1,0:T(4,128)S(1)}, f32[4,512]{1,0:T(4,128)S(1)}, u32[]{:S(2)}, u32[]{:S(2)}) collective-permute-start(f32[4,512]{1,0:T(4,128)S(1)} %maximum_select_fusion.9), channel_id=1, source_target_pairs={{128,0},{136,8},{144,16},{152,24},{160,32},{168,40},{176,48},{184,... | collective-permute-start | bytes 24584 | tf_op jit(solution)/shard_map/ppermute | solution.py:12
  180.0 9.5 %collective-permute-start.14 = (f32[4,512]{1,0:T(4,128)S(1)}, f32[4,512]{1,0:T(4,128)S(1)}, u32[]{:S(2)}, u32[]{:S(2)}) collective-permute-start(f32[4,512]{1,0:T(4,128)S(1)} %maximum_select_fusion.10), channel_id=1, source_target_pairs={{256,0},{264,8},{272,16},{280,24},{288,32},{296,40},{304,48},{312,... | collective-permute-start | bytes 24584 | tf_op jit(solution)/shard_map/ppermute | solution.py:12
  195.6 157.9 %all-reduce.8.cloned.1.call-start = ((), (), s32[]{:S(2)}) async-start(), calls=%async_computation.1 | async-start | bytes 1064960 | tf_op jit(solution)/shard_map/psum | solution.py:219
  271.6 10.4 %collective-permute-start.15 = (f32[3,512]{0,1:T(8,128)S(1)}, f32[3,512]{0,1:T(8,128)S(1)}, u32[]{:S(2)}, u32[]{:S(2)}) collective-permute-start(f32[3,512]{0,1:T(8,128)S(1)} %bitcast.248), channel_id=1, source_target_pairs={{8,0},{16,8},{24,16},{32,24},{40,32},{48,40},{56,48},{64,56},{72,6... | collective-permute-start | bytes 18440 | tf_op jit(solution)/shard_map/ppermute | solution.py:12
  353.5 3.0 copy-start.13
  (44 other events, 30.4 us)
Sparse Core Ops, SparseCore 0:
  195.8 75.7 all-reduce.5
  274.0 79.4 all-reduce.7

commit v2 on v1

--- a/solution.py
+++ b/solution.py
@@ -27,6 +27,33 @@
         state = jnp.where(ahead >= reach, joined, state)
         reach *= 2
     return tuple(state)
+
+
+def tree_sum(value, axis):
+    count = lax.axis_size(axis)
+    place = lax.axis_index(axis)
+    flat = value.reshape(-1)
+    width = -(-flat.size // count)
+    block = jnp.pad(flat, (0, width * count - flat.size)).reshape(count, width)
+    bits = []
+    span = 1
+    while span < count:
+        bits.append(span)
+        span *= 2
+    order = bits[0::3] + bits[1::3] + bits[2::3]
+    for span in order:
+        upper = (place // span) % 2 == 1
+        half = block.shape[0] // 2
+        low, high = block[:half], block[half:]
+        pairs = [(i, i ^ span) for i in range(count)]
+        sent = lax.ppermute(jnp.where(upper, low, high), axis, pairs)
+        block = jnp.where(upper, high, low) + sent
+    for span in order[::-1]:
+        upper = (place // span) % 2 == 1
+        pairs = [(i, i ^ span) for i in range(count)]
+        other = lax.ppermute(block, axis, pairs)
+        block = jnp.where(upper, jnp.concatenate([other, block]), jnp.concatenate([block, other]))
+    return block.reshape(-1)[: flat.size].reshape(value.shape)
 
 
 def linear_run(drive_re, drive_im, decay_rate, turn_rate, log_keep):
@@ -164,7 +191,7 @@
     grad_bf = mixed_grad.astype(jnp.bfloat16).reshape(seq_len, local_heads, head_width)
     state_grad = jnp.einsum("thc,hck->thk", grad_bf, out_proj, preferred_element_type=jnp.float32)
     out_grad = jnp.einsum("thc,thk->hck", grad_bf, state_bf, preferred_element_type=jnp.float32)
-    out_grad = lax.psum(lax.psum(out_grad, "y"), "z")
+    out_grad = tree_sum(out_grad, SEQ)
     back_keep = jnp.concatenate([jnp.zeros((1,), jnp.float32), log_keep[::-1][:-1]])
     grad_re = state_grad[:, :, :state_size].reshape(seq_len, num_cols)[::-1]
     grad_im = state_grad[:, :, state_size:].reshape(seq_len, num_cols)[::-1]
@@ -216,7 +243,7 @@
         ]
     )
     packed = jnp.concatenate([in_grad.reshape(-1), taps_grad.reshape(-1)])
-    packed = lax.psum(lax.psum(packed, "y"), "z")
+    packed = tree_sum(packed, SEQ)
     in_grad = packed[: in_grad.size].reshape(in_grad.shape)
     taps_grad = packed[in_grad.size :].reshape(taps_grad.shape)
     return (normed, tokens_grad.astype(jnp.bfloat16), in_grad, out_grad, taps_grad)

time: 366 us -> 302 us (0.83)
  waiting for transfers between devices: 209 us -> 66.2 us
  starting transfers between devices: 62.6 us -> 153 us
  between operations: 15.8 us -> 3.04 us
    psum x2 -> x0, waiting for transfers between devices: 146 us -> none  [per_device(): packed = lax.psum(lax.psum(packed, 'y'), 'z')]
    ppermute x0 -> x24, starting transfers between devices: none -> 89.5 us  [the longest x12 45.7 us: tree_sum(): sent = lax.ppermute(jnp.where(upper, low, high), axis, pairs)]
    ppermute x0 -> x24, waiting for transfers between devices: none -> 11.7 us  [the longest x12 8.17 us: tree_sum(): sent = lax.ppermute(jnp.where(upper, low, high), axis, pairs)]
    ppermute x16, waiting for transfers between devices: 62.9 us -> 54.5 us  [from_behind(): return lax.ppermute(value, axis, pairs)]
    unnamed x189 -> x186, local copies, waits for them, and re-layouts: 15.2 us -> 14.6 us
  transfers between devices with their start and end apart: 18 -> 40, of which waited for: 16 -> 23; matrix products, arithmetic and copies ran while one was open for 8% -> 11% of each run, Pallas kernels for 0% -> 0%
where the time goes in v2:
time: 302 us; the launch traced here: 297 us
  starting transfers between devices  153 us (51%)
  waiting for transfers between devices  66.2 us (22%)
  local copies, waits for them, and re-layouts  38.4 us (13%)
  other arithmetic  21.3 us (7%)
  blocking collectives  12.6 us (4%)
  between operations  3.04 us (1%)
    ppermute x16, starting transfers between devices, from_behind(): return lax.ppermute(value, axis, pairs)  63.8 us
    ppermute x16, waiting for transfers between devices, from_behind(): return lax.ppermute(value, axis, pairs)  54.5 us
    ppermute x12, starting transfers between devices, tree_sum(): sent = lax.ppermute(jnp.where(upper, low, high), axis, pairs)  45.7 us
    ppermute x12, starting transfers between devices, tree_sum(): other = lax.ppermute(block, axis, pairs)  43.7 us
    unnamed x186, local copies, waits for them, and re-layouts  14.6 us
    psum x1, blocking collectives, per_device(): squares = lax.psum(squares, 'chan')  12.6 us
    ppermute x12, waiting for transfers between devices, tree_sum(): sent = lax.ppermute(jnp.where(upper, low, high), axis, pairs)  8.17 us
  transfers between devices with their start and end apart: 40, of which 23 were waited for; matrix products, arithmetic and copies ran while one was open for 11% of the time, Pallas kernels for 0%

profile of v2, /device:TPU:56, one launch (start us, length us, event | category | flops | bytes accessed | tf_op | source)
XLA Modules:
  0.0 297.4 jit_solution(12251607706683874262)
XLA Ops:
  1.6 3.5 %collective-permute-start = (bf16[3,512]{0,1:T(8,128)(2,1)S(1)}, bf16[3,512]{0,1:T(8,128)(2,1)S(1)}, u32[]{:S(2)}, u32[]{:S(2)}) collective-permute-start(bf16[3,512]{0,1:T(8,128)(2,1)S(1)} %copy.131), channel_id=1, source_target_pairs={{0,8},{8,16},{16,24},{24,32},{32,40},{40,48},{48,56},{56,64},{64,7... | collective-permute-start | bytes 9224 | tf_op jit(solution)/shard_map/ppermute | solution.py:12
  8.4 1.3 fusion.70
  9.7 2.5 multiply_cosine_fusion.1
  14.5 1.0 fusion.18
  20.7 3.5 %collective-permute-start.1 = (f32[4,512]{1,0:T(4,128)S(1)}, f32[4,512]{1,0:T(4,128)S(1)}, u32[]{:S(2)}, u32[]{:S(2)}) collective-permute-start(f32[4,512]{1,0:T(4,128)S(1)} %fusion.48), channel_id=1, source_target_pairs={{0,8},{8,16},{16,24},{24,32},{32,40},{40,48},{48,56},{56,64},{64,7... | collective-permute-start | bytes 24584 | tf_op jit(solution)/shard_map/ppermute | solution.py:12
  24.2 2.0 collective-permute-done.1
  26.3 5.6 %collective-permute-start.2 = (f32[4,512]{1,0:T(4,128)S(1)}, f32[4,512]{1,0:T(4,128)S(1)}, u32[]{:S(2)}, u32[]{:S(2)}) collective-permute-start(f32[4,512]{1,0:T(4,128)S(1)} %broadcast_select_fusion.11), channel_id=1, source_target_pairs={{0,8},{8,16},{16,24},{24,32},{32,40},{40,48},{48,56},{56,64},{64,7... | collective-permute-start | bytes 24584 | tf_op jit(solution)/shard_map/ppermute | solution.py:12
  31.9 1.3 collective-permute-done.2
  33.2 3.6 %collective-permute-start.3 = (f32[4,512]{1,0:T(4,128)S(1)}, f32[4,512]{1,0:T(4,128)S(1)}, u32[]{:S(2)}, u32[]{:S(2)}) collective-permute-start(f32[4,512]{1,0:T(4,128)S(1)} %maximum_select_fusion.11), channel_id=1, source_target_pairs={{0,16},{8,24},{16,32},{24,40},{32,48},{40,56},{48,64},{56,72},{64,... | collective-permute-start | bytes 24584 | tf_op jit(solution)/shard_map/ppermute | solution.py:12
  36.9 2.8 collective-permute-done.3
  39.8 6.3 %collective-permute-start.4 = (f32[4,512]{1,0:T(4,128)S(1)}, f32[4,512]{1,0:T(4,128)S(1)}, u32[]{:S(2)}, u32[]{:S(2)}) collective-permute-start(f32[4,512]{1,0:T(4,128)S(1)} %maximum_select_fusion.12), channel_id=1, source_target_pairs={{0,32},{8,40},{16,48},{24,56},{32,64},{40,72},{48,80},{56,88},{64,... | collective-permute-start | bytes 24584 | tf_op jit(solution)/shard_map/ppermute | solution.py:12
  46.1 3.1 %collective-permute-done.4 = f32[4,512]{1,0:T(4,128)S(1)} collective-permute-done((f32[4,512]{1,0:T(4,128)S(1)}, f32[4,512]{1,0:T(4,128)S(1)}, u32[]{:S(2)}, u32[]{:S(2)}) %collective-permute-start.4) | collective-permute-done | bytes 8224 | tf_op jit(solution)/shard_map/ppermute | solution.py:12
  49.3 4.3 %collective-permute-start.5 = (f32[4,512]{1,0:T(4,128)S(1)}, f32[4,512]{1,0:T(4,128)S(1)}, u32[]{:S(2)}, u32[]{:S(2)}) collective-permute-start(f32[4,512]{1,0:T(4,128)S(1)} %maximum_select_fusion.13), channel_id=1, source_target_pairs={{0,64},{8,72},{16,80},{24,88},{32,96},{40,104},{48,112},{56,120},{... | collective-permute-start | bytes 24584 | tf_op jit(solution)/shard_map/ppermute | solution.py:12
  53.6 1.3 collective-permute-done.5
  55.1 8.5 %collective-permute-start.6 = (f32[4,512]{1,0:T(4,128)S(1)}, f32[4,512]{1,0:T(4,128)S(1)}, u32[]{:S(2)}, u32[]{:S(2)}) collective-permute-start(f32[4,512]{1,0:T(4,128)S(1)} %maximum_select_fusion.14), channel_id=1, source_target_pairs={{0,128},{8,136},{16,144},{24,152},{32,160},{40,168},{48,176},{56,1... | collective-permute-start | bytes 24584 | tf_op jit(solution)/shard_map/ppermute | solution.py:12
  63.6 1.3 collective-permute-done.6
  66.2 9.7 %collective-permute-start.7 = (f32[4,512]{1,0:T(4,128)}, f32[4,512]{1,0:T(4,128)}, u32[]{:S(2)}, u32[]{:S(2)}) collective-permute-start(f32[4,512]{1,0:T(4,128)} %maximum_select_fusion.15), channel_id=1, source_target_pairs={{0,256},{8,264},{16,272},{24,280},{32,288},{40,296},{48,304},{56,3... | collective-permute-start | bytes 24584 | tf_op jit(solution)/shard_map/ppermute | solution.py:12
  79.3 1.1 sub.392
  90.7 1.1 squeeze.79
  97.4 2.7 subtract_convert_fusion
  101.5 12.6 %all-reduce = (f32[128]{0:T(128)S(1)}, f32[128]{0:T(128)S(1)}) all-reduce(f32[128]{0:T(128)S(1)} %get-tuple-element.185, f32[128]{0:T(128)S(1)} %get-tuple-element.184), channel_id=1, replica_groups=mesh['z'=8,'y'=8,'chan'=8] {'chan'}, use_global_device_ids=true, to_apply=%region_6.7 | all-reduce | flops 256 | bytes 2048 | tf_op jit(solution)/shard_map/psum | solution.py:183
  121.4 5.4 %collective-permute-start.8 = (f32[4,512]{1,0:T(4,128)S(1)}, f32[4,512]{1,0:T(4,128)S(1)}, u32[]{:S(2)}, u32[]{:S(2)}) collective-permute-start(f32[4,512]{1,0:T(4,128)S(1)} %fusion.50), channel_id=1, source_target_pairs={{8,0},{16,8},{24,16},{32,24},{40,32},{48,40},{56,48},{64,56},{72,6... | collective-permute-start | bytes 24584 | tf_op jit(solution)/shard_map/ppermute | solution.py:12
  126.9 7.6 %collective-permute-done.8 = f32[4,512]{1,0:T(4,128)S(1)} collective-permute-done((f32[4,512]{1,0:T(4,128)S(1)}, f32[4,512]{1,0:T(4,128)S(1)}, u32[]{:S(2)}, u32[]{:S(2)}) %collective-permute-start.8) | collective-permute-done | bytes 8224 | tf_op jit(solution)/shard_map/ppermute | solution.py:12
  134.4 1.9 collective-permute-start.9
  136.3 5.7 %collective-permute-done.9 = f32[4,512]{1,0:T(4,128)S(1)} collective-permute-done((f32[4,512]{1,0:T(4,128)S(1)}, f32[4,512]{1,0:T(4,128)S(1)}, u32[]{:S(2)}, u32[]{:S(2)}) %collective-permute-start.9) | collective-permute-done | bytes 8224 | tf_op jit(solution)/shard_map/ppermute | solution.py:12
  142.1 1.9 collective-permute-start.10
  144.0 6.6 %collective-permute-done.10 = f32[4,512]{1,0:T(4,128)S(1)} collective-permute-done((f32[4,512]{1,0:T(4,128)S(1)}, f32[4,512]{1,0:T(4,128)S(1)}, u32[]{:S(2)}, u32[]{:S(2)}) %collective-permute-start.10) | collective-permute-done | bytes 8224 | tf_op jit(solution)/shard_map/ppermute | solution.py:12
  150.7 1.9 collective-permute-start.11
  152.6 8.4 %collective-permute-done.11 = f32[4,512]{1,0:T(4,128)S(1)} collective-permute-done((f32[4,512]{1,0:T(4,128)S(1)}, f32[4,512]{1,0:T(4,128)S(1)}, u32[]{:S(2)}, u32[]{:S(2)}) %collective-permute-start.11) | collective-permute-done | bytes 8224 | tf_op jit(solution)/shard_map/ppermute | solution.py:12
  161.1 1.3 collective-permute-start.12
  163.5 3.2 %collective-permute-done.12 = f32[4,512]{1,0:T(4,128)S(1)} collective-permute-done((f32[4,512]{1,0:T(4,128)S(1)}, f32[4,512]{1,0:T(4,128)S(1)}, u32[]{:S(2)}, u32[]{:S(2)}) %collective-permute-start.12) | collective-permute-done | bytes 8224 | tf_op jit(solution)/shard_map/ppermute | solution.py:12
  166.7 1.3 collective-permute-start.13
  168.3 4.9 %collective-permute-done.13 = f32[4,512]{1,0:T(4,128)S(1)} collective-permute-done((f32[4,512]{1,0:T(4,128)S(1)}, f32[4,512]{1,0:T(4,128)S(1)}, u32[]{:S(2)}, u32[]{:S(2)}) %collective-permute-start.13) | collective-permute-done | bytes 8224 | tf_op jit(solution)/shard_map/ppermute | solution.py:12
  173.2 1.3 collective-permute-start.14
  174.6 1.9 collective-permute-start.28
  176.6 6.1 %collective-permute-done.14 = f32[4,512]{1,0:T(4,128)S(1)} collective-permute-done((f32[4,512]{1,0:T(4,128)S(1)}, f32[4,512]{1,0:T(4,128)S(1)}, u32[]{:S(2)}, u32[]{:S(2)}) %collective-permute-start.14) | collective-permute-done | bytes 8224 | tf_op jit(solution)/shard_map/ppermute | solution.py:12
  183.5 1.1 multiply_subtract_fusion
  188.2 4.9 %collective-permute-start.29 = (f32[16,1024]{1,0:T(8,128)S(1)}, f32[16,1024]{1,0:T(8,128)S(1)}, u32[]{:S(2)}, u32[]{:S(2)}) collective-permute-start(f32[16,1024]{1,0:T(8,128)S(1)} %slice_select_fusion.5), channel_id=1, source_target_pairs={{0,64},{8,72},{16,80},{24,88},{32,96},{40,104},{48,112},{56,120},{... | collective-permute-start | bytes 196616 | tf_op jit(solution)/shard_map/ppermute | solution.py:49
  193.3 1.9 collective-permute-start.16
  195.4 1.9 collective-permute-start.30
  197.6 3.8 %collective-permute-start.15 = (f32[3,512]{0,1:T(8,128)S(1)}, f32[3,512]{0,1:T(8,128)S(1)}, u32[]{:S(2)}, u32[]{:S(2)}) collective-permute-start(f32[3,512]{0,1:T(8,128)S(1)} %bitcast.248), channel_id=1, source_target_pairs={{8,0},{16,8},{24,16},{32,24},{40,32},{48,40},{56,48},{64,56},{72,6... | collective-permute-start | bytes 18440 | tf_op jit(solution)/shard_map/ppermute | solution.py:12
  202.2 6.0 %collective-permute-start.31 = (f32[4,1024]{1,0:T(4,128)S(1)}, f32[4,1024]{1,0:T(4,128)S(1)}, u32[]{:S(2)}, u32[]{:S(2)}) collective-permute-start(f32[4,1024]{1,0:T(4,128)S(1)} %slice_select_fusion.9), channel_id=1, source_target_pairs={{0,128},{8,136},{16,144},{24,152},{32,160},{40,168},{48,176},{56,1... | collective-permute-start | bytes 49160 | tf_op jit(solution)/shard_map/ppermute | solution.py:49
  208.3 3.8 %collective-permute-start.17 = (f32[16,1056]{1,0:T(8,128)S(1)}, f32[16,1056]{1,0:T(8,128)S(1)}, u32[]{:S(2)}, u32[]{:S(2)}) collective-permute-start(f32[16,1056]{1,0:T(8,128)S(1)} %slice_select_fusion.4), channel_id=1, source_target_pairs={{0,64},{8,72},{16,80},{24,88},{32,96},{40,104},{48,112},{56,120},{... | collective-permute-start | bytes 202760 | tf_op jit(solution)/shard_map/ppermute | solution.py:49
  212.1 2.4 collective-permute-done.17
  214.5 4.8 %collective-permute-start.18 = (f32[8,1056]{1,0:T(8,128)S(1)}, f32[8,1056]{1,0:T(8,128)S(1)}, u32[]{:S(2)}, u32[]{:S(2)}) collective-permute-start(f32[8,1056]{1,0:T(8,128)S(1)} %slice_select_fusion.6), channel_id=1, source_target_pairs={{0,16},{8,24},{16,0},{24,8},{32,48},{40,56},{48,32},{56,40},{64,80... | collective-permute-start | bytes 101384 | tf_op jit(solution)/shard_map/ppermute | solution.py:49
  219.4 1.9 collective-permute-start.32
  221.4 1.9 collective-permute-start.19
  223.3 5.6 %collective-permute-done.32 = f32[2,1024]{1,0:T(2,128)S(1)} collective-permute-done((f32[2,1024]{1,0:T(2,128)S(1)}, f32[2,1024]{1,0:T(2,128)S(1)}, u32[]{:S(2)}, u32[]{:S(2)}) %collective-permute-start.32) | collective-permute-done | bytes 8224 | tf_op jit(solution)/shard_map/ppermute | solution.py:49
  228.9 6.9 %collective-permute-start.20 = (f32[2,1056]{1,0:T(2,128)S(1)}, f32[2,1056]{1,0:T(2,128)S(1)}, u32[]{:S(2)}, u32[]{:S(2)}) collective-permute-start(f32[2,1056]{1,0:T(2,128)S(1)} %broadcast_select_fusion.4), channel_id=1, source_target_pairs={{0,32},{8,40},{16,48},{24,56},{32,0},{40,8},{48,16},{56,24},{64,96... | collective-permute-start | bytes 25352 | tf_op jit(solution)/shard_map/ppermute | solution.py:49
  235.8 2.5 collective-permute-start.33
  238.4 7.2 %collective-permute-start.21 = (f32[1,1056]{1,0:T(1,128)S(1)}, f32[1,1056]{1,0:T(1,128)S(1)}, u32[]{:S(2)}, u32[]{:S(2)}) collective-permute-start(f32[1,1056]{1,0:T(1,128)S(1)} %broadcast_select_fusion.5), channel_id=1, source_target_pairs={{0,256},{8,264},{16,272},{24,280},{32,288},{40,296},{48,304},{56,3... | collective-permute-start | bytes 12680 | tf_op jit(solution)/shard_map/ppermute | solution.py:49
  245.6 2.5 collective-permute-start.34
  248.2 7.2 %collective-permute-start.22 = (f32[1,1056]{1,0:T(1,128)S(1)}, f32[1,1056]{1,0:T(1,128)S(1)}, u32[]{:S(2)}, u32[]{:S(2)}) collective-permute-start(f32[1,1056]{1,0:T(1,128)S(1)} %fusion.51), channel_id=1, source_target_pairs={{0,256},{8,264},{16,272},{24,280},{32,288},{40,296},{48,304},{56,3... | collective-permute-start | bytes 12680 | tf_op jit(solution)/shard_map/ppermute | solution.py:54
  255.5 2.9 collective-permute-start.35
  258.4 6.9 %collective-permute-start.23 = (f32[2,1056]{1,0:T(2,128)S(1)}, f32[2,1056]{1,0:T(2,128)S(1)}, u32[]{:S(2)}, u32[]{:S(2)}) collective-permute-start(f32[2,1056]{1,0:T(2,128)S(1)} %maximum_select_fusion.10), channel_id=1, source_target_pairs={{0,32},{8,40},{16,48},{24,56},{32,0},{40,8},{48,16},{56,24},{64,96... | collective-permute-start | bytes 25352 | tf_op jit(solution)/shard_map/ppermute | solution.py:54
  265.3 1.9 collective-permute-start.36
  267.9 4.2 %collective-permute-start.24 = (f32[4,1056]{1,0:T(4,128)S(1)}, f32[4,1056]{1,0:T(4,128)S(1)}, u32[]{:S(2)}, u32[]{:S(2)}) collective-permute-start(f32[4,1056]{1,0:T(4,128)S(1)} %maximum_select_fusion.8), channel_id=1, source_target_pairs={{0,128},{8,136},{16,144},{24,152},{32,160},{40,168},{48,176},{56,1... | collective-permute-start | bytes 50696 | tf_op jit(solution)/shard_map/ppermute | solution.py:54
  272.1 1.9 collective-permute-start.37
  274.5 4.5 %collective-permute-start.25 = (f32[8,1056]{1,0:T(8,128)S(1)}, f32[8,1056]{1,0:T(8,128)S(1)}, u32[]{:S(2)}, u32[]{:S(2)}) collective-permute-start(f32[8,1056]{1,0:T(8,128)S(1)} %maximum_select_fusion.6), channel_id=1, source_target_pairs={{0,16},{8,24},{16,0},{24,8},{32,48},{40,56},{48,32},{56,40},{64,80... | collective-permute-start | bytes 101384 | tf_op jit(solution)/shard_map/ppermute | solution.py:54
  279.0 2.0 collective-permute-start.38
  281.2 3.7 %collective-permute-start.26 = (f32[16,1056]{1,0:T(8,128)S(1)}, f32[16,1056]{1,0:T(8,128)S(1)}, u32[]{:S(2)}, u32[]{:S(2)}) collective-permute-start(f32[16,1056]{1,0:T(8,128)S(1)} %maximum_select_fusion.4), channel_id=1, source_target_pairs={{0,64},{8,72},{16,80},{24,88},{32,96},{40,104},{48,112},{56,120},{... | collective-permute-start | bytes 202760 | tf_op jit(solution)/shard_map/ppermute | solution.py:54
  285.2 3.3 %collective-permute-start.39 = (f32[32,1024]{1,0:T(8,128)S(1)}, f32[32,1024]{1,0:T(8,128)S(1)}, u32[]{:S(2)}, u32[]{:S(2)}) collective-permute-start(f32[32,1024]{1,0:T(8,128)S(1)} %maximum_select_fusion.3), channel_id=1, source_target_pairs={{0,8},{8,0},{16,24},{24,16},{32,40},{40,32},{48,56},{56,48},{64,72... | collective-permute-start | bytes 393224 | tf_op jit(solution)/shard_map/ppermute | solution.py:54
  288.6 2.7 collective-permute-start.27
  293.6 2.0 collective-permute-done.27
  (423 shorter events, 53.8 us)
Async XLA Ops:
  0.6 99.5 %copy-start = (bf16[8,64,128]{2,1,0:T(8,128)(2,1)S(1)}, bf16[8,64,128]{2,1,0:T(8,128)(2,1)}, u32[]{:S(2)}) copy-start(bf16[8,64,128]{2,1,0:T(8,128)(2,1)} %param.19) | copy-start | bytes 393220
  1.6 3.5 %copy-start.87 = (f32[128]{0:T(128)S(1)}, f32[128]{0:T(128)}, u32[]{:S(2)}) copy-start(f32[128]{0:T(128)} %param.22) | copy-start | bytes 1540
  1.6 14.0 %collective-permute-start = (bf16[3,512]{0,1:T(8,128)(2,1)S(1)}, bf16[3,512]{0,1:T(8,128)(2,1)S(1)}, u32[]{:S(2)}, u32[]{:S(2)}) collective-permute-start(bf16[3,512]{0,1:T(8,128)(2,1)S(1)} %copy.131), channel_id=1, source_target_pairs={{0,8},{8,16},{16,24},{24,32},{32,40},{40,48},{48,56},{56,64},{64,7... | collective-permute-start | bytes 9224 | tf_op jit(solution)/shard_map/ppermute | solution.py:12
  7.7 70.4 %copy-start.71 = (f32[2,64]{1,0:T(2,128)}, f32[2,64]{1,0:T(2,128)S(1)}, u32[]{:S(2)}) copy-start(f32[2,64]{1,0:T(2,128)S(1)} %reduce.6) | copy-start | bytes 1540
  9.7 8.4 %copy-start.56 = (f32[512]{0:T(512)}, f32[512]{0:T(512)S(1)}, u32[]{:S(2)}) copy-start(f32[512]{0:T(512)S(1)} %get-tuple-element.356) | copy-start | bytes 6148
  9.7 11.0 %copy-start.58 = (f32[512]{0:T(512)}, f32[512]{0:T(512)S(1)}, u32[]{:S(2)}) copy-start(f32[512]{0:T(512)S(1)} %get-tuple-element.352) | copy-start | bytes 6148
  20.7 5.5 %collective-permute-start.1 = (f32[4,512]{1,0:T(4,128)S(1)}, f32[4,512]{1,0:T(4,128)S(1)}, u32[]{:S(2)}, u32[]{:S(2)}) collective-permute-start(f32[4,512]{1,0:T(4,128)S(1)} %fusion.48), channel_id=1, source_target_pairs={{0,8},{8,16},{16,24},{24,32},{32,40},{40,48},{48,56},{56,64},{64,7... | collective-permute-start | bytes 24584 | tf_op jit(solution)/shard_map/ppermute | solution.py:12
  24.2 2.1 copy-start.15
  26.3 6.9 %collective-permute-start.2 = (f32[4,512]{1,0:T(4,128)S(1)}, f32[4,512]{1,0:T(4,128)S(1)}, u32[]{:S(2)}, u32[]{:S(2)}) collective-permute-start(f32[4,512]{1,0:T(4,128)S(1)} %broadcast_select_fusion.11), channel_id=1, source_target_pairs={{0,8},{8,16},{16,24},{24,32},{32,40},{40,48},{48,56},{56,64},{64,7... | collective-permute-start | bytes 24584 | tf_op jit(solution)/shard_map/ppermute | solution.py:12
  33.2 6.4 %collective-permute-start.3 = (f32[4,512]{1,0:T(4,128)S(1)}, f32[4,512]{1,0:T(4,128)S(1)}, u32[]{:S(2)}, u32[]{:S(2)}) collective-permute-start(f32[4,512]{1,0:T(4,128)S(1)} %maximum_select_fusion.11), channel_id=1, source_target_pairs={{0,16},{8,24},{16,32},{24,40},{32,48},{40,56},{48,64},{56,72},{64,... | collective-permute-start | bytes 24584 | tf_op jit(solution)/shard_map/ppermute | solution.py:12
  39.7 25.3 %copy-start.16 = (f32[1,512]{1,0:T(1,128)}, f32[1,512]{1,0:T(1,128)S(1)}, u32[]{:S(2)}) copy-start(f32[1,512]{1,0:T(1,128)S(1)} %get-tuple-element.319) | copy-start | bytes 6148
  39.7 25.3 %copy-start.18 = (f32[1,512]{1,0:T(1,128)}, f32[1,512]{1,0:T(1,128)S(1)}, u32[]{:S(2)}) copy-start(f32[1,512]{1,0:T(1,128)S(1)} %get-tuple-element.320) | copy-start | bytes 6148
  39.7 25.3 %copy-start.20 = (f32[1,512]{1,0:T(1,128)}, f32[1,512]{1,0:T(1,128)S(1)}, u32[]{:S(2)}) copy-start(f32[1,512]{1,0:T(1,128)S(1)} %get-tuple-element.321) | copy-start | bytes 6148
  39.7 25.3 %copy-start.22 = (f32[1,512]{1,0:T(1,128)}, f32[1,512]{1,0:T(1,128)S(1)}, u32[]{:S(2)}) copy-start(f32[1,512]{1,0:T(1,128)S(1)} %get-tuple-element.322) | copy-start | bytes 6148
  39.8 9.5 %collective-permute-start.4 = (f32[4,512]{1,0:T(4,128)S(1)}, f32[4,512]{1,0:T(4,128)S(1)}, u32[]{:S(2)}, u32[]{:S(2)}) collective-permute-start(f32[4,512]{1,0:T(4,128)S(1)} %maximum_select_fusion.12), channel_id=1, source_target_pairs={{0,32},{8,40},{16,48},{24,56},{32,64},{40,72},{48,80},{56,88},{64,... | collective-permute-start | bytes 24584 | tf_op jit(solution)/shard_map/ppermute | solution.py:12
  49.2 15.8 %copy-start.28 = (f32[1,512]{1,0:T(1,128)}, f32[1,512]{1,0:T(1,128)S(1)}, u32[]{:S(2)}) copy-start(f32[1,512]{1,0:T(1,128)S(1)} %get-tuple-element.315) | copy-start | bytes 6148
  49.3 15.8 %copy-start.30 = (f32[1,512]{1,0:T(1,128)}, f32[1,512]{1,0:T(1,128)S(1)}, u32[]{:S(2)}) copy-start(f32[1,512]{1,0:T(1,128)S(1)} %get-tuple-element.316) | copy-start | bytes 6148
  49.3 15.8 %copy-start.32 = (f32[1,512]{1,0:T(1,128)}, f32[1,512]{1,0:T(1,128)S(1)}, u32[]{:S(2)}) copy-start(f32[1,512]{1,0:T(1,128)S(1)} %get-tuple-element.317) | copy-start | bytes 6148
  49.3 15.8 %copy-start.34 = (f32[1,512]{1,0:T(1,128)}, f32[1,512]{1,0:T(1,128)S(1)}, u32[]{:S(2)}) copy-start(f32[1,512]{1,0:T(1,128)S(1)} %get-tuple-element.318) | copy-start | bytes 6148
  49.3 5.6 %collective-permute-start.5 = (f32[4,512]{1,0:T(4,128)S(1)}, f32[4,512]{1,0:T(4,128)S(1)}, u32[]{:S(2)}, u32[]{:S(2)}) collective-permute-start(f32[4,512]{1,0:T(4,128)S(1)} %maximum_select_fusion.13), channel_id=1, source_target_pairs={{0,64},{8,72},{16,80},{24,88},{32,96},{40,104},{48,112},{56,120},{... | collective-permute-start | bytes 24584 | tf_op jit(solution)/shard_map/ppermute | solution.py:12
  55.0 10.1 %copy-start.40 = (f32[1,512]{1,0:T(1,128)}, f32[1,512]{1,0:T(1,128)S(1)}, u32[]{:S(2)}) copy-start(f32[1,512]{1,0:T(1,128)S(1)} %get-tuple-element.311) | copy-start | bytes 6148
  55.0 10.1 %copy-start.42 = (f32[1,512]{1,0:T(1,128)}, f32[1,512]{1,0:T(1,128)S(1)}, u32[]{:S(2)}) copy-start(f32[1,512]{1,0:T(1,128)S(1)} %get-tuple-element.312) | copy-start | bytes 6148
  55.0 10.1 %copy-start.44 = (f32[1,512]{1,0:T(1,128)}, f32[1,512]{1,0:T(1,128)S(1)}, u32[]{:S(2)}) copy-start(f32[1,512]{1,0:T(1,128)S(1)} %get-tuple-element.313) | copy-start | bytes 6148
  55.0 10.1 %copy-start.46 = (f32[1,512]{1,0:T(1,128)}, f32[1,512]{1,0:T(1,128)S(1)}, u32[]{:S(2)}) copy-start(f32[1,512]{1,0:T(1,128)S(1)} %get-tuple-element.314) | copy-start | bytes 6148
  55.1 9.9 %collective-permute-start.6 = (f32[4,512]{1,0:T(4,128)S(1)}, f32[4,512]{1,0:T(4,128)S(1)}, u32[]{:S(2)}, u32[]{:S(2)}) collective-permute-start(f32[4,512]{1,0:T(4,128)S(1)} %maximum_select_fusion.14), channel_id=1, source_target_pairs={{0,128},{8,136},{16,144},{24,152},{32,160},{40,168},{48,176},{56,1... | collective-permute-start | bytes 24584 | tf_op jit(solution)/shard_map/ppermute | solution.py:12
  66.2 28.6 %collective-permute-start.7 = (f32[4,512]{1,0:T(4,128)}, f32[4,512]{1,0:T(4,128)}, u32[]{:S(2)}, u32[]{:S(2)}) collective-permute-start(f32[4,512]{1,0:T(4,128)} %maximum_select_fusion.15), channel_id=1, source_target_pairs={{0,256},{8,264},{16,272},{24,280},{32,288},{40,296},{48,304},{56,3... | collective-permute-start | bytes 24584 | tf_op jit(solution)/shard_map/ppermute | solution.py:12
  93.6 2.3 copy-start.67
  94.5 2.3 copy-start.6
  94.5 2.3 copy-start.7
  94.5 2.3 copy-start.8
  116.4 2.7 copy-start.11
  116.4 2.7 copy-start.12
  121.4 13.0 %collective-permute-start.8 = (f32[4,512]{1,0:T(4,128)S(1)}, f32[4,512]{1,0:T(4,128)S(1)}, u32[]{:S(2)}, u32[]{:S(2)}) collective-permute-start(f32[4,512]{1,0:T(4,128)S(1)} %fusion.50), channel_id=1, source_target_pairs={{8,0},{16,8},{24,16},{32,24},{40,32},{48,40},{56,48},{64,56},{72,6... | collective-permute-start | bytes 24584 | tf_op jit(solution)/shard_map/ppermute | solution.py:12
  134.4 7.6 %collective-permute-start.9 = (f32[4,512]{1,0:T(4,128)S(1)}, f32[4,512]{1,0:T(4,128)S(1)}, u32[]{:S(2)}, u32[]{:S(2)}) collective-permute-start(f32[4,512]{1,0:T(4,128)S(1)} %broadcast_select_fusion.10), channel_id=1, source_target_pairs={{8,0},{16,8},{24,16},{32,24},{40,32},{48,40},{56,48},{64,56},{72,6... | collective-permute-start | bytes 24584 | tf_op jit(solution)/shard_map/ppermute | solution.py:12
  142.1 8.6 %collective-permute-start.10 = (f32[4,512]{1,0:T(4,128)S(1)}, f32[4,512]{1,0:T(4,128)S(1)}, u32[]{:S(2)}, u32[]{:S(2)}) collective-permute-start(f32[4,512]{1,0:T(4,128)S(1)} %maximum_select_fusion.17), channel_id=1, source_target_pairs={{16,0},{24,8},{32,16},{40,24},{48,32},{56,40},{64,48},{72,56},{80,... | collective-permute-start | bytes 24584 | tf_op jit(solution)/shard_map/ppermute | solution.py:12
  150.7 10.4 %collective-permute-start.11 = (f32[4,512]{1,0:T(4,128)S(1)}, f32[4,512]{1,0:T(4,128)S(1)}, u32[]{:S(2)}, u32[]{:S(2)}) collective-permute-start(f32[4,512]{1,0:T(4,128)S(1)} %maximum_select_fusion.18), channel_id=1, source_target_pairs={{32,0},{40,8},{48,16},{56,24},{64,32},{72,40},{80,48},{88,56},{96,... | collective-permute-start | bytes 24584 | tf_op jit(solution)/shard_map/ppermute | solution.py:12
  161.1 5.5 %collective-permute-start.12 = (f32[4,512]{1,0:T(4,128)S(1)}, f32[4,512]{1,0:T(4,128)S(1)}, u32[]{:S(2)}, u32[]{:S(2)}) collective-permute-start(f32[4,512]{1,0:T(4,128)S(1)} %maximum_select_fusion.19), channel_id=1, source_target_pairs={{64,0},{72,8},{80,16},{88,24},{96,32},{104,40},{112,48},{120,56},{... | collective-permute-start | bytes 24584 | tf_op jit(solution)/shard_map/ppermute | solution.py:12
  166.7 6.4 %collective-permute-start.13 = (f32[4,512]{1,0:T(4,128)S(1)}, f32[4,512]{1,0:T(4,128)S(1)}, u32[]{:S(2)}, u32[]{:S(2)}) collective-permute-start(f32[4,512]{1,0:T(4,128)S(1)} %maximum_select_fusion.20), channel_id=1, source_target_pairs={{128,0},{136,8},{144,16},{152,24},{160,32},{168,40},{176,48},{184,... | collective-permute-start | bytes 24584 | tf_op jit(solution)/shard_map/ppermute | solution.py:12
  173.2 9.5 %collective-permute-start.14 = (f32[4,512]{1,0:T(4,128)S(1)}, f32[4,512]{1,0:T(4,128)S(1)}, u32[]{:S(2)}, u32[]{:S(2)}) collective-permute-start(f32[4,512]{1,0:T(4,128)S(1)} %maximum_select_fusion.21), channel_id=1, source_target_pairs={{256,0},{264,8},{272,16},{280,24},{288,32},{296,40},{304,48},{312,... | collective-permute-start | bytes 24584 | tf_op jit(solution)/shard_map/ppermute | solution.py:12
  174.6 13.6 %collective-permute-start.28 = (f32[32,1024]{1,0:T(8,128)S(1)}, f32[32,1024]{1,0:T(8,128)S(1)}, u32[]{:S(2)}, u32[]{:S(2)}) collective-permute-start(f32[32,1024]{1,0:T(8,128)S(1)} %select_n.509), channel_id=1, source_target_pairs={{0,8},{8,0},{16,24},{24,16},{32,40},{40,32},{48,56},{56,48},{64,72... | collective-permute-start | bytes 393224 | tf_op jit(solution)/shard_map/ppermute | solution.py:49
  188.2 7.1 %collective-permute-start.29 = (f32[16,1024]{1,0:T(8,128)S(1)}, f32[16,1024]{1,0:T(8,128)S(1)}, u32[]{:S(2)}, u32[]{:S(2)}) collective-permute-start(f32[16,1024]{1,0:T(8,128)S(1)} %slice_select_fusion.5), channel_id=1, source_target_pairs={{0,64},{8,72},{16,80},{24,88},{32,96},{40,104},{48,112},{56,120},{... | collective-permute-start | bytes 196616 | tf_op jit(solution)/shard_map/ppermute | solution.py:49
  193.3 8.8 %collective-permute-start.16 = (f32[32,1056]{1,0:T(8,128)S(1)}, f32[32,1056]{1,0:T(8,128)S(1)}, u32[]{:S(2)}, u32[]{:S(2)}) collective-permute-start(f32[32,1056]{1,0:T(8,128)S(1)} %select_n.476), channel_id=1, source_target_pairs={{0,8},{8,0},{16,24},{24,16},{32,40},{40,32},{48,56},{56,48},{64,72... | collective-permute-start | bytes 405512 | tf_op jit(solution)/shard_map/ppermute | solution.py:49
  195.4 6.8 %collective-permute-start.30 = (f32[8,1024]{1,0:T(8,128)S(1)}, f32[8,1024]{1,0:T(8,128)S(1)}, u32[]{:S(2)}, u32[]{:S(2)}) collective-permute-start(f32[8,1024]{1,0:T(8,128)S(1)} %slice_select_fusion.7), channel_id=1, source_target_pairs={{0,16},{8,24},{16,0},{24,8},{32,48},{40,56},{48,32},{56,40},{64,80... | collective-permute-start | bytes 98312 | tf_op jit(solution)/shard_map/ppermute | solution.py:49
  197.6 93.7 %collective-permute-start.15 = (f32[3,512]{0,1:T(8,128)S(1)}, f32[3,512]{0,1:T(8,128)S(1)}, u32[]{:S(2)}, u32[]{:S(2)}) collective-permute-start(f32[3,512]{0,1:T(8,128)S(1)} %bitcast.248), channel_id=1, source_target_pairs={{8,0},{16,8},{24,16},{32,24},{40,32},{48,40},{56,48},{64,56},{72,6... | collective-permute-start | bytes 18440 | tf_op jit(solution)/shard_map/ppermute | solution.py:12
  202.2 9.9 %collective-permute-start.31 = (f32[4,1024]{1,0:T(4,128)S(1)}, f32[4,1024]{1,0:T(4,128)S(1)}, u32[]{:S(2)}, u32[]{:S(2)}) collective-permute-start(f32[4,1024]{1,0:T(4,128)S(1)} %slice_select_fusion.9), channel_id=1, source_target_pairs={{0,128},{8,136},{16,144},{24,152},{32,160},{40,168},{48,176},{56,1... | collective-permute-start | bytes 49160 | tf_op jit(solution)/shard_map/ppermute | solution.py:49
  208.3 6.2 %collective-permute-start.17 = (f32[16,1056]{1,0:T(8,128)S(1)}, f32[16,1056]{1,0:T(8,128)S(1)}, u32[]{:S(2)}, u32[]{:S(2)}) collective-permute-start(f32[16,1056]{1,0:T(8,128)S(1)} %slice_select_fusion.4), channel_id=1, source_target_pairs={{0,64},{8,72},{16,80},{24,88},{32,96},{40,104},{48,112},{56,120},{... | collective-permute-start | bytes 202760 | tf_op jit(solution)/shard_map/ppermute | solution.py:49
  214.5 6.8 %collective-permute-start.18 = (f32[8,1056]{1,0:T(8,128)S(1)}, f32[8,1056]{1,0:T(8,128)S(1)}, u32[]{:S(2)}, u32[]{:S(2)}) collective-permute-start(f32[8,1056]{1,0:T(8,128)S(1)} %slice_select_fusion.6), channel_id=1, source_target_pairs={{0,16},{8,24},{16,0},{24,8},{32,48},{40,56},{48,32},{56,40},{64,80... | collective-permute-start | bytes 101384 | tf_op jit(solution)/shard_map/ppermute | solution.py:49
  219.4 9.5 %collective-permute-start.32 = (f32[2,1024]{1,0:T(2,128)S(1)}, f32[2,1024]{1,0:T(2,128)S(1)}, u32[]{:S(2)}, u32[]{:S(2)}) collective-permute-start(f32[2,1024]{1,0:T(2,128)S(1)} %broadcast_select_fusion.7), channel_id=1, source_target_pairs={{0,32},{8,40},{16,48},{24,56},{32,0},{40,8},{48,16},{56,24},{64,96... | collective-permute-start | bytes 24584 | tf_op jit(solution)/shard_map/ppermute | solution.py:49
  221.4 7.5 %collective-permute-start.19 = (f32[4,1056]{1,0:T(4,128)S(1)}, f32[4,1056]{1,0:T(4,128)S(1)}, u32[]{:S(2)}, u32[]{:S(2)}) collective-permute-start(f32[4,1056]{1,0:T(4,128)S(1)} %slice_select_fusion.8), channel_id=1, source_target_pairs={{0,128},{8,136},{16,144},{24,152},{32,160},{40,168},{48,176},{56,1... | collective-permute-start | bytes 50696 | tf_op jit(solution)/shard_map/ppermute | solution.py:49
  228.9 9.5 %collective-permute-start.20 = (f32[2,1056]{1,0:T(2,128)S(1)}, f32[2,1056]{1,0:T(2,128)S(1)}, u32[]{:S(2)}, u32[]{:S(2)}) collective-permute-start(f32[2,1056]{1,0:T(2,128)S(1)} %broadcast_select_fusion.4), channel_id=1, source_target_pairs={{0,32},{8,40},{16,48},{24,56},{32,0},{40,8},{48,16},{56,24},{64,96... | collective-permute-start | bytes 25352 | tf_op jit(solution)/shard_map/ppermute | solution.py:49
  235.8 9.8 %collective-permute-start.33 = (f32[1,1024]{1,0:T(1,128)S(1)}, f32[1,1024]{1,0:T(1,128)S(1)}, u32[]{:S(2)}, u32[]{:S(2)}) collective-permute-start(f32[1,1024]{1,0:T(1,128)S(1)} %broadcast_select_fusion.8), channel_id=1, source_target_pairs={{0,256},{8,264},{16,272},{24,280},{32,288},{40,296},{48,304},{56,3... | collective-permute-start | bytes 12296 | tf_op jit(solution)/shard_map/ppermute | solution.py:49
  238.4 9.8 %collective-permute-start.21 = (f32[1,1056]{1,0:T(1,128)S(1)}, f32[1,1056]{1,0:T(1,128)S(1)}, u32[]{:S(2)}, u32[]{:S(2)}) collective-permute-start(f32[1,1056]{1,0:T(1,128)S(1)} %broadcast_select_fusion.5), channel_id=1, source_target_pairs={{0,256},{8,264},{16,272},{24,280},{32,288},{40,296},{48,304},{56,3... | collective-permute-start | bytes 12680 | tf_op jit(solution)/shard_map/ppermute | solution.py:49
  245.6 9.8 %collective-permute-start.34 = (f32[1,1024]{1,0:T(1,128)S(1)}, f32[1,1024]{1,0:T(1,128)S(1)}, u32[]{:S(2)}, u32[]{:S(2)}) collective-permute-start(f32[1,1024]{1,0:T(1,128)S(1)} %fusion.52), channel_id=1, source_target_pairs={{0,256},{8,264},{16,272},{24,280},{32,288},{40,296},{48,304},{56,3... | collective-permute-start | bytes 12296 | tf_op jit(solution)/shard_map/ppermute | solution.py:54
  248.2 10.1 %collective-permute-start.22 = (f32[1,1056]{1,0:T(1,128)S(1)}, f32[1,1056]{1,0:T(1,128)S(1)}, u32[]{:S(2)}, u32[]{:S(2)}) collective-permute-start(f32[1,1056]{1,0:T(1,128)S(1)} %fusion.51), channel_id=1, source_target_pairs={{0,256},{8,264},{16,272},{24,280},{32,288},{40,296},{48,304},{56,3... | collective-permute-start | bytes 12680 | tf_op jit(solution)/shard_map/ppermute | solution.py:54
  255.5 9.8 %collective-permute-start.35 = (f32[2,1024]{1,0:T(2,128)S(1)}, f32[2,1024]{1,0:T(2,128)S(1)}, u32[]{:S(2)}, u32[]{:S(2)}) collective-permute-start(f32[2,1024]{1,0:T(2,128)S(1)} %maximum_select_fusion.23), channel_id=1, source_target_pairs={{0,32},{8,40},{16,48},{24,56},{32,0},{40,8},{48,16},{56,24},{64,96... | collective-permute-start | bytes 24584 | tf_op jit(solution)/shard_map/ppermute | solution.py:54
  258.4 9.5 %collective-permute-start.23 = (f32[2,1056]{1,0:T(2,128)S(1)}, f32[2,1056]{1,0:T(2,128)S(1)}, u32[]{:S(2)}, u32[]{:S(2)}) collective-permute-start(f32[2,1056]{1,0:T(2,128)S(1)} %maximum_select_fusion.10), channel_id=1, source_target_pairs={{0,32},{8,40},{16,48},{24,56},{32,0},{40,8},{48,16},{56,24},{64,96... | collective-permute-start | bytes 25352 | tf_op jit(solution)/shard_map/ppermute | solution.py:54
  265.3 6.8 %collective-permute-start.36 = (f32[4,1024]{1,0:T(4,128)S(1)}, f32[4,1024]{1,0:T(4,128)S(1)}, u32[]{:S(2)}, u32[]{:S(2)}) collective-permute-start(f32[4,1024]{1,0:T(4,128)S(1)} %maximum_select_fusion.9), channel_id=1, source_target_pairs={{0,128},{8,136},{16,144},{24,152},{32,160},{40,168},{48,176},{56,1... | collective-permute-start | bytes 49160 | tf_op jit(solution)/shard_map/ppermute | solution.py:54
  267.9 6.6 %collective-permute-start.24 = (f32[4,1056]{1,0:T(4,128)S(1)}, f32[4,1056]{1,0:T(4,128)S(1)}, u32[]{:S(2)}, u32[]{:S(2)}) collective-permute-start(f32[4,1056]{1,0:T(4,128)S(1)} %maximum_select_fusion.8), channel_id=1, source_target_pairs={{0,128},{8,136},{16,144},{24,152},{32,160},{40,168},{48,176},{56,1... | collective-permute-start | bytes 50696 | tf_op jit(solution)/shard_map/ppermute | solution.py:54
  272.1 6.9 %collective-permute-start.37 = (f32[8,1024]{1,0:T(8,128)S(1)}, f32[8,1024]{1,0:T(8,128)S(1)}, u32[]{:S(2)}, u32[]{:S(2)}) collective-permute-start(f32[8,1024]{1,0:T(8,128)S(1)} %maximum_select_fusion.7), channel_id=1, source_target_pairs={{0,16},{8,24},{16,0},{24,8},{32,48},{40,56},{48,32},{56,40},{64,80... | collective-permute-start | bytes 98312 | tf_op jit(solution)/shard_map/ppermute | solution.py:54
  274.5 6.8 %collective-permute-start.25 = (f32[8,1056]{1,0:T(8,128)S(1)}, f32[8,1056]{1,0:T(8,128)S(1)}, u32[]{:S(2)}, u32[]{:S(2)}) collective-permute-start(f32[8,1056]{1,0:T(8,128)S(1)} %maximum_select_fusion.6), channel_id=1, source_target_pairs={{0,16},{8,24},{16,0},{24,8},{32,48},{40,56},{48,32},{56,40},{64,80... | collective-permute-start | bytes 101384 | tf_op jit(solution)/shard_map/ppermute | solution.py:54
  279.0 6.2 %collective-permute-start.38 = (f32[16,1024]{1,0:T(8,128)S(1)}, f32[16,1024]{1,0:T(8,128)S(1)}, u32[]{:S(2)}, u32[]{:S(2)}) collective-permute-start(f32[16,1024]{1,0:T(8,128)S(1)} %maximum_select_fusion.5), channel_id=1, source_target_pairs={{0,64},{8,72},{16,80},{24,88},{32,96},{40,104},{48,112},{56,120},{... | collective-permute-start | bytes 196616 | tf_op jit(solution)/shard_map/ppermute | solution.py:54
  281.2 7.3 %collective-permute-start.26 = (f32[16,1056]{1,0:T(8,128)S(1)}, f32[16,1056]{1,0:T(8,128)S(1)}, u32[]{:S(2)}, u32[]{:S(2)}) collective-permute-start(f32[16,1056]{1,0:T(8,128)S(1)} %maximum_select_fusion.4), channel_id=1, source_target_pairs={{0,64},{8,72},{16,80},{24,88},{32,96},{40,104},{48,112},{56,120},{... | collective-permute-start | bytes 202760 | tf_op jit(solution)/shard_map/ppermute | solution.py:54
  285.2 7.6 %collective-permute-start.39 = (f32[32,1024]{1,0:T(8,128)S(1)}, f32[32,1024]{1,0:T(8,128)S(1)}, u32[]{:S(2)}, u32[]{:S(2)}) collective-permute-start(f32[32,1024]{1,0:T(8,128)S(1)} %maximum_select_fusion.3), channel_id=1, source_target_pairs={{0,8},{8,0},{16,24},{24,16},{32,40},{40,32},{48,56},{56,48},{64,72... | collective-permute-start | bytes 393224 | tf_op jit(solution)/shard_map/ppermute | solution.py:54
  288.6 7.0 %collective-permute-start.27 = (f32[32,1056]{1,0:T(8,128)S(1)}, f32[32,1056]{1,0:T(8,128)S(1)}, u32[]{:S(2)}, u32[]{:S(2)}) collective-permute-start(f32[32,1056]{1,0:T(8,128)S(1)} %maximum_select_fusion.2), channel_id=1, source_target_pairs={{0,8},{8,0},{16,24},{24,16},{32,40},{40,32},{48,56},{56,48},{64,72... | collective-permute-start | bytes 405512 | tf_op jit(solution)/shard_map/ppermute | solution.py:54
  (65 other events, 58.2 us)

commit v3 on v2

--- a/solution.py
+++ b/solution.py
@@ -12,21 +12,32 @@
     return lax.ppermute(value, axis, pairs)
 
 
+def fold(stack, where_at, combine, unit):
+    total = unit
+    prefix = unit
+    for j in range(stack.shape[0]):
+        prefix = jnp.where(j == where_at, total, prefix)
+        total = jnp.stack(combine(tuple(total), tuple(stack[j])))
+    return prefix, total
+
+
 def carried_in(part, axis, combine, identity, reverse):
-    count = lax.axis_size(axis)
-    place = lax.axis_index(axis)
-    ahead = count - 1 - place if reverse else place
-    step = -1 if reverse else 1
+    outer, inner = axis
     packed = jnp.stack(part)
     unit = jnp.stack([jnp.zeros_like(a) + jnp.asarray(e, a.dtype) for a, e in zip(part, identity)])
-    state = jnp.where(ahead >= 1, from_behind(packed, axis, step), unit)
-    reach = 1
-    while reach < count:
-        earlier = from_behind(state, axis, step * reach)
-        joined = jnp.stack(combine(tuple(earlier), tuple(state)))
-        state = jnp.where(ahead >= reach, joined, state)
-        reach *= 2
-    return tuple(state)
+    row_place = lax.axis_index(inner)
+    col_place = lax.axis_index(outer)
+    row = lax.all_gather(packed, inner)
+    if reverse:
+        row = row[::-1]
+        row_place = lax.axis_size(inner) - 1 - row_place
+        col_place = lax.axis_size(outer) - 1 - col_place
+    within, row_total = fold(row, row_place, combine, unit)
+    rows = lax.all_gather(row_total, outer)
+    if reverse:
+        rows = rows[::-1]
+    before, _ = fold(rows, col_place, combine, unit)
+    return combine(tuple(before), tuple(within))
 
 
 def tree_sum(value, axis):
@@ -191,7 +202,6 @@
     grad_bf = mixed_grad.astype(jnp.bfloat16).reshape(seq_len, local_heads, head_width)
     state_grad = jnp.einsum("thc,hck->thk", grad_bf, out_proj, preferred_element_type=jnp.float32)
     out_grad = jnp.einsum("thc,thk->hck", grad_bf, state_bf, preferred_element_type=jnp.float32)
-    out_grad = tree_sum(out_grad, SEQ)
     back_keep = jnp.concatenate([jnp.zeros((1,), jnp.float32), log_keep[::-1][:-1]])
     grad_re = state_grad[:, :, :state_size].reshape(seq_len, num_cols)[::-1]
     grad_im = state_grad[:, :, state_size:].reshape(seq_len, num_cols)[::-1]
@@ -242,10 +252,14 @@
             for offset in range(tap_count)
         ]
     )
-    packed = jnp.concatenate([in_grad.reshape(-1), taps_grad.reshape(-1)])
-    packed = tree_sum(packed, SEQ)
-    in_grad = packed[: in_grad.size].reshape(in_grad.shape)
-    taps_grad = packed[in_grad.size :].reshape(taps_grad.shape)
+    parts = (out_grad, in_grad, taps_grad)
+    packed = tree_sum(jnp.concatenate([p.reshape(-1) for p in parts]), SEQ)
+    ends = [0]
+    for p in parts:
+        ends.append(ends[-1] + p.size)
+    out_grad, in_grad, taps_grad = (
+        packed[a:b].reshape(p.shape) for a, b, p in zip(ends[:-1], ends[1:], parts)
+    )
     return (normed, tokens_grad.astype(jnp.bfloat16), in_grad, out_grad, taps_grad)
 
 

time: 302 us -> 300 us (level)
  blocking collectives: 12.6 us -> 117 us
  starting transfers between devices: 153 us -> 49.6 us
  waiting for transfers between devices: 66.2 us -> 57.1 us
  other arithmetic: 21.3 us -> 26.7 us
  local copies, waits for them, and re-layouts: 38.4 us -> 43 us
    all_gather x0 -> x4, blocking collectives: none -> 104 us  [the longest x2 54.8 us: carried_in(): rows = lax.all_gather(row_total, outer)]
    ppermute x16 -> x2, starting transfers between devices: 63.8 us -> 7.41 us  [from_behind(): return lax.ppermute(value, axis, pairs)]
    ppermute x16 -> x2, waiting for transfers between devices: 54.5 us -> 5.64 us  [from_behind(): return lax.ppermute(value, axis, pairs)]
    ppermute x12 -> x6, starting transfers between devices: 43.7 us -> 19.2 us  [tree_sum(): other = lax.ppermute(block, axis, pairs)]
    ppermute x12 -> x6, starting transfers between devices: 45.7 us -> 23 us  [tree_sum(): sent = lax.ppermute(jnp.where(upper, low, high), axis, pairs)]
    ppermute x12 -> x6, waiting for transfers between devices: 3.56 us -> 25.1 us  [tree_sum(): other = lax.ppermute(block, axis, pairs)]
    ppermute x12 -> x6, waiting for transfers between devices: 8.17 us -> 26.4 us  [tree_sum(): sent = lax.ppermute(jnp.where(upper, low, high), axis, pairs)]
    unnamed x186 -> x232, local copies, waits for them, and re-layouts: 14.6 us -> 17.1 us
  transfers between devices with their start and end apart: 40 -> 14, of which waited for: 23 -> 12; matrix products, arithmetic and copies ran while one was open for 11% -> 8% of each run, Pallas kernels for 0% -> 0%
where the time goes in v3:
time: 300 us; the launch traced here: 298 us
  blocking collectives  117 us (39%)
  waiting for transfers between devices  57.1 us (19%)
  starting transfers between devices  49.6 us (17%)
  local copies, waits for them, and re-layouts  43 us (14%)
  other arithmetic  26.7 us (9%)
    all_gather x2, blocking collectives, carried_in(): rows = lax.all_gather(row_total, outer)  54.8 us
    all_gather x2, blocking collectives, carried_in(): row = lax.all_gather(packed, inner)  49.2 us
    ppermute x6, waiting for transfers between devices, tree_sum(): sent = lax.ppermute(jnp.where(upper, low, high), axis, pairs)  26.4 us
    ppermute x6, waiting for transfers between devices, tree_sum(): other = lax.ppermute(block, axis, pairs)  25.1 us
    ppermute x6, starting transfers between devices, tree_sum(): sent = lax.ppermute(jnp.where(upper, low, high), axis, pairs)  23 us
    ppermute x6, starting transfers between devices, tree_sum(): other = lax.ppermute(block, axis, pairs)  19.2 us
    unnamed x232, local copies, waits for them, and re-layouts  17.1 us
    psum x1, blocking collectives, per_device(): squares = lax.psum(squares, 'chan')  12.6 us
  transfers between devices with their start and end apart: 14, of which 12 were waited for; matrix products, arithmetic and copies ran while one was open for 8% of the time, Pallas kernels for 0%

profile of v3, /device:TPU:56, one launch (start us, length us, event | category | flops | bytes accessed | tf_op | source)
XLA Modules:
  0.0 298.1 jit_solution(2556786549949098203)
XLA Ops:
  0.7 0.8 slice.452
  1.6 3.5 %collective-permute-start = (bf16[3,512]{0,1:T(8,128)(2,1)S(1)}, bf16[3,512]{0,1:T(8,128)(2,1)S(1)}, u32[]{:S(2)}, u32[]{:S(2)}) collective-permute-start(bf16[3,512]{0,1:T(8,128)(2,1)S(1)} %copy.164), channel_id=1, source_target_pairs={{0,8},{8,16},{16,24},{24,32},{32,40},{40,48},{48,56},{56,64},{64,7... | collective-permute-start | bytes 9224 | tf_op jit(solution)/shard_map/ppermute | solution.py:12
  10.6 1.3 fusion.211
  12.7 2.5 multiply_cosine_fusion.1
  15.2 0.9 subtract_exponential_fusion.1
  18.2 0.9 copy.163
  19.2 0.9 copy.169
  20.3 0.9 copy.171
  21.4 0.9 copy.172
  22.5 0.9 copy.173
  23.4 1.0 fusion.18
  24.6 0.9 copy.175
  31.8 0.8 add_multiply_fusion.1
  33.9 0.8 add_multiply_fusion.3
  35.7 0.8 multiply_subtract_fusion.27
  37.2 24.6 %all-gather.4 = f32[8,4,512]{2,1,0:T(4,128)S(1)} all-gather(f32[1,4,512]{2,1,0:T(4,128)S(1)} %fusion.52), channel_id=2, replica_groups=mesh['z'=8,'y'=8,'chan'=8] {'y'}, dimensions={0}, use_global_device_ids=true | all-gather | bytes 73728 | tf_op jit(solution)/shard_map/all_gather | solution.py:30
  63.7 30.2 %all-gather.5 = f32[8,4,512]{2,1,0:T(4,128)S(1)} all-gather(f32[1,4,512]{2,1,0:T(4,128)S(1)} %maximum_bitcast_fusion), channel_id=3, replica_groups=mesh['z'=8,'y'=8,'chan'=8] {'z'}, dimensions={0}, use_global_device_ids=true | all-gather | bytes 73728 | tf_op jit(solution)/shard_map/all_gather | solution.py:36
  95.7 1.1 squeeze.109
  97.5 0.8 multiply_add_fusion.14
  99.2 0.8 maximum_select_fusion.13
  100.9 0.8 maximum_select_fusion.6
  102.3 1.3 mul.7980
  103.6 1.3 mul.7986
  105.0 0.9 copy.174
  105.9 0.9 copy.176
  106.8 0.9 copy.168
  107.9 0.7 copy-done.2
  108.8 2.7 subtract_convert_fusion
  112.3 0.7 multiply_reduce_fusion.4
  113.0 12.6 %all-reduce = (f32[128]{0:T(128)S(1)}, f32[128]{0:T(128)S(1)}) all-reduce(f32[128]{0:T(128)S(1)} %get-tuple-element.190, f32[128]{0:T(128)S(1)} %get-tuple-element.189), channel_id=1, replica_groups=mesh['z'=8,'y'=8,'chan'=8] {'chan'}, use_global_device_ids=true, to_apply=%region_6.7 | all-reduce | flops 256 | bytes 2048 | tf_op jit(solution)/shard_map/psum | solution.py:194
  129.4 0.8 add_multiply_fusion.2
  133.7 24.6 %all-gather.6 = f32[8,4,512]{2,1,0:T(4,128)S(1)} all-gather(f32[1,4,512]{2,1,0:T(4,128)S(1)} %fusion.55), channel_id=4, replica_groups=mesh['z'=8,'y'=8,'chan'=8] {'y'}, dimensions={0}, use_global_device_ids=true | all-gather | bytes 73728 | tf_op jit(solution)/shard_map/all_gather | solution.py:30
  158.4 24.6 %all-gather.7 = f32[8,4,512]{2,1,0:T(4,128)S(1)} all-gather(f32[1,4,512]{2,1,0:T(4,128)S(1)} %maximum_bitcast_fusion.1), channel_id=5, replica_groups=mesh['z'=8,'y'=8,'chan'=8] {'z'}, dimensions={0}, use_global_device_ids=true | all-gather | bytes 73728 | tf_op jit(solution)/shard_map/all_gather | solution.py:36
  184.1 1.1 multiply_subtract_fusion
  188.3 0.7 multiply_reduce_fusion.3
  189.3 2.6 collective-permute-start.2
  192.1 6.4 %collective-permute-done.2 = f32[32,2080]{1,0:T(8,128)S(1)} collective-permute-done((f32[32,2080]{1,0:T(8,128)S(1)}, f32[32,2080]{1,0:T(8,128)S(1)}, u32[]{:S(2)}, u32[]{:S(2)}) %collective-permute-start.2) | collective-permute-done | bytes 266272 | tf_op jit(solution)/shard_map/ppermute | solution.py:60
  198.5 3.4 %collective-permute-start.3 = (f32[16,2080]{1,0:T(8,128)S(1)}, f32[16,2080]{1,0:T(8,128)S(1)}, u32[]{:S(2)}, u32[]{:S(2)}) collective-permute-start(f32[16,2080]{1,0:T(8,128)S(1)} %slice_select_fusion), channel_id=1, source_target_pairs={{0,64},{8,72},{16,80},{24,88},{32,96},{40,104},{48,112},{56,120},{... | collective-permute-start | bytes 399368 | tf_op jit(solution)/shard_map/ppermute | solution.py:60
  201.9 3.5 %collective-permute-done.3 = f32[16,2080]{1,0:T(8,128)S(1)} collective-permute-done((f32[16,2080]{1,0:T(8,128)S(1)}, f32[16,2080]{1,0:T(8,128)S(1)}, u32[]{:S(2)}, u32[]{:S(2)}) %collective-permute-start.3) | collective-permute-done | bytes 133152 | tf_op jit(solution)/shard_map/ppermute | solution.py:60
  205.5 3.8 %collective-permute-start.4 = (f32[8,2080]{1,0:T(8,128)S(1)}, f32[8,2080]{1,0:T(8,128)S(1)}, u32[]{:S(2)}, u32[]{:S(2)}) collective-permute-start(f32[8,2080]{1,0:T(8,128)S(1)} %slice_select_fusion.1), channel_id=1, source_target_pairs={{0,16},{8,24},{16,0},{24,8},{32,48},{40,56},{48,32},{56,40},{64,80... | collective-permute-start | bytes 199688 | tf_op jit(solution)/shard_map/ppermute | solution.py:60
  209.4 4.0 %collective-permute-done.4 = f32[8,2080]{1,0:T(8,128)S(1)} collective-permute-done((f32[8,2080]{1,0:T(8,128)S(1)}, f32[8,2080]{1,0:T(8,128)S(1)}, u32[]{:S(2)}, u32[]{:S(2)}) %collective-permute-start.4) | collective-permute-done | bytes 66592 | tf_op jit(solution)/shard_map/ppermute | solution.py:60
  213.4 2.5 collective-permute-start.5
  215.9 4.3 %collective-permute-done.5 = f32[4,2080]{1,0:T(4,128)S(1)} collective-permute-done((f32[4,2080]{1,0:T(4,128)S(1)}, f32[4,2080]{1,0:T(4,128)S(1)}, u32[]{:S(2)}, u32[]{:S(2)}) %collective-permute-start.5) | collective-permute-done | bytes 33312 | tf_op jit(solution)/shard_map/ppermute | solution.py:60
  220.2 6.2 %collective-permute-start.6 = (f32[2,2080]{1,0:T(2,128)S(1)}, f32[2,2080]{1,0:T(2,128)S(1)}, u32[]{:S(2)}, u32[]{:S(2)}) collective-permute-start(f32[2,2080]{1,0:T(2,128)S(1)} %broadcast_select_fusion.4), channel_id=1, source_target_pairs={{0,32},{8,40},{16,48},{24,56},{32,0},{40,8},{48,16},{56,24},{64,96... | collective-permute-start | bytes 49928 | tf_op jit(solution)/shard_map/ppermute | solution.py:60
  226.4 3.3 %collective-permute-done.6 = f32[2,2080]{1,0:T(2,128)S(1)} collective-permute-done((f32[2,2080]{1,0:T(2,128)S(1)}, f32[2,2080]{1,0:T(2,128)S(1)}, u32[]{:S(2)}, u32[]{:S(2)}) %collective-permute-start.6) | collective-permute-done | bytes 16672 | tf_op jit(solution)/shard_map/ppermute | solution.py:60
  229.8 4.5 %collective-permute-start.7 = (f32[1,2080]{1,0:T(1,128)S(1)}, f32[1,2080]{1,0:T(1,128)S(1)}, u32[]{:S(2)}, u32[]{:S(2)}) collective-permute-start(f32[1,2080]{1,0:T(1,128)S(1)} %broadcast_select_fusion.5), channel_id=1, source_target_pairs={{0,256},{8,264},{16,272},{24,280},{32,288},{40,296},{48,304},{56,3... | collective-permute-start | bytes 24968 | tf_op jit(solution)/shard_map/ppermute | solution.py:60
  234.3 4.9 %collective-permute-done.7 = f32[1,2080]{1,0:T(1,128)S(1)} collective-permute-done((f32[1,2080]{1,0:T(1,128)S(1)}, f32[1,2080]{1,0:T(1,128)S(1)}, u32[]{:S(2)}, u32[]{:S(2)}) %collective-permute-start.7) | collective-permute-done | bytes 8352 | tf_op jit(solution)/shard_map/ppermute | solution.py:60
  239.2 4.5 %collective-permute-start.8 = (f32[1,2080]{1,0:T(1,128)S(1)}, f32[1,2080]{1,0:T(1,128)S(1)}, u32[]{:S(2)}, u32[]{:S(2)}) collective-permute-start(f32[1,2080]{1,0:T(1,128)S(1)} %fusion.49), channel_id=1, source_target_pairs={{0,256},{8,264},{16,272},{24,280},{32,288},{40,296},{48,304},{56,3... | collective-permute-start | bytes 24968 | tf_op jit(solution)/shard_map/ppermute | solution.py:65
  243.8 4.9 %collective-permute-done.8 = f32[1,2080]{1,0:T(1,128)S(1)} collective-permute-done((f32[1,2080]{1,0:T(1,128)S(1)}, f32[1,2080]{1,0:T(1,128)S(1)}, u32[]{:S(2)}, u32[]{:S(2)}) %collective-permute-start.8) | collective-permute-done | bytes 8352 | tf_op jit(solution)/shard_map/ppermute | solution.py:65
  248.7 6.4 %collective-permute-start.9 = (f32[2,2080]{1,0:T(2,128)S(1)}, f32[2,2080]{1,0:T(2,128)S(1)}, u32[]{:S(2)}, u32[]{:S(2)}) collective-permute-start(f32[2,2080]{1,0:T(2,128)S(1)} %maximum_select_fusion.5), channel_id=1, source_target_pairs={{0,32},{8,40},{16,48},{24,56},{32,0},{40,8},{48,16},{56,24},{64,96... | collective-permute-start | bytes 49928 | tf_op jit(solution)/shard_map/ppermute | solution.py:65
  255.1 3.2 %collective-permute-done.9 = f32[2,2080]{1,0:T(2,128)S(1)} collective-permute-done((f32[2,2080]{1,0:T(2,128)S(1)}, f32[2,2080]{1,0:T(2,128)S(1)}, u32[]{:S(2)}, u32[]{:S(2)}) %collective-permute-start.9) | collective-permute-done | bytes 16672 | tf_op jit(solution)/shard_map/ppermute | solution.py:65
  258.3 2.5 collective-permute-start.10
  260.8 6.8 %collective-permute-done.10 = f32[4,2080]{1,0:T(4,128)S(1)} collective-permute-done((f32[4,2080]{1,0:T(4,128)S(1)}, f32[4,2080]{1,0:T(4,128)S(1)}, u32[]{:S(2)}, u32[]{:S(2)}) %collective-permute-start.10) | collective-permute-done | bytes 33312 | tf_op jit(solution)/shard_map/ppermute | solution.py:65
  267.7 1.9 collective-permute-start.11
  269.6 5.2 %collective-permute-done.11 = f32[8,2080]{1,0:T(8,128)S(1)} collective-permute-done((f32[8,2080]{1,0:T(8,128)S(1)}, f32[8,2080]{1,0:T(8,128)S(1)}, u32[]{:S(2)}, u32[]{:S(2)}) %collective-permute-start.11) | collective-permute-done | bytes 66592 | tf_op jit(solution)/shard_map/ppermute | solution.py:65
  274.8 1.9 collective-permute-start.12
  276.7 5.0 %collective-permute-done.12 = f32[16,2080]{1,0:T(8,128)S(1)} collective-permute-done((f32[16,2080]{1,0:T(8,128)S(1)}, f32[16,2080]{1,0:T(8,128)S(1)}, u32[]{:S(2)}, u32[]{:S(2)}) %collective-permute-start.12) | collective-permute-done | bytes 133152 | tf_op jit(solution)/shard_map/ppermute | solution.py:65
  281.8 1.9 collective-permute-start.13
  283.7 3.9 %collective-permute-start.1 = (f32[3,512]{0,1:T(8,128)S(1)}, f32[3,512]{0,1:T(8,128)S(1)}, u32[]{:S(2)}, u32[]{:S(2)}) collective-permute-start(f32[3,512]{0,1:T(8,128)S(1)} %bitcast.1375), channel_id=1, source_target_pairs={{8,0},{16,8},{24,16},{32,24},{40,32},{48,40},{56,48},{64,56},{72,6... | collective-permute-start | bytes 18440 | tf_op jit(solution)/shard_map/ppermute | solution.py:12
  287.7 0.8 copy.195
  288.4 5.6 %collective-permute-done.1 = f32[3,512]{0,1:T(8,128)S(1)} collective-permute-done((f32[3,512]{0,1:T(8,128)S(1)}, f32[3,512]{0,1:T(8,128)S(1)}, u32[]{:S(2)}, u32[]{:S(2)}) %collective-permute-start.1) | collective-permute-done | bytes 6176 | tf_op jit(solution)/shard_map/ppermute | solution.py:12
  294.1 0.7 fusion.28
  294.8 0.8 copy.196
  296.6 0.8 fusion.206
  (392 shorter events, 39.6 us)
Async XLA Ops:
  0.6 110.9 %copy-start = (bf16[8,64,128]{2,1,0:T(8,128)(2,1)S(1)}, bf16[8,64,128]{2,1,0:T(8,128)(2,1)}, u32[]{:S(2)}) copy-start(bf16[8,64,128]{2,1,0:T(8,128)(2,1)} %param.19) | copy-start | bytes 393220
  0.6 4.5 %copy-start.10 = (bf16[128,512]{1,0:T(8,128)(2,1)S(1)}, bf16[128,512]{1,0:T(8,128)(2,1)}, u32[]{:S(2)}) copy-start(bf16[128,512]{1,0:T(8,128)(2,1)} %param.14) | copy-start | bytes 393220
  1.6 27.1 %collective-permute-start = (bf16[3,512]{0,1:T(8,128)(2,1)S(1)}, bf16[3,512]{0,1:T(8,128)(2,1)S(1)}, u32[]{:S(2)}, u32[]{:S(2)}) collective-permute-start(bf16[3,512]{0,1:T(8,128)(2,1)S(1)} %copy.164), channel_id=1, source_target_pairs={{0,8},{8,16},{16,24},{24,32},{32,40},{40,48},{48,56},{56,64},{64,7... | collective-permute-start | bytes 9224 | tf_op jit(solution)/shard_map/ppermute | solution.py:12
  7.6 7.6 %copy-start.54 = (f32[2,64]{1,0:T(2,128)}, f32[2,64]{1,0:T(2,128)S(1)}, u32[]{:S(2)}) copy-start(f32[2,64]{1,0:T(2,128)S(1)} %reduce) | copy-start | bytes 1540
  7.8 7.4 %copy-start.52 = (f32[2,64]{1,0:T(2,128)}, f32[2,64]{1,0:T(2,128)S(1)}, u32[]{:S(2)}) copy-start(f32[2,64]{1,0:T(2,128)S(1)} %reduce.6) | copy-start | bytes 1540
  10.6 1.3 copy-start.99
  11.9 17.0 %copy-start.21 = (f32[1,512]{1,0:T(1,128)}, f32[1,512]{1,0:T(1,128)S(1)}, u32[]{:S(2)}) copy-start(f32[1,512]{1,0:T(1,128)S(1)} %get-tuple-element.410) | copy-start | bytes 6148
  11.9 17.0 %copy-start.24 = (f32[1,512]{1,0:T(1,128)}, f32[1,512]{1,0:T(1,128)S(1)}, u32[]{:S(2)}) copy-start(f32[1,512]{1,0:T(1,128)S(1)} %get-tuple-element.411) | copy-start | bytes 6148
  11.9 17.0 %copy-start.27 = (f32[1,512]{1,0:T(1,128)}, f32[1,512]{1,0:T(1,128)S(1)}, u32[]{:S(2)}) copy-start(f32[1,512]{1,0:T(1,128)S(1)} %get-tuple-element.412) | copy-start | bytes 6148
  11.9 17.0 %copy-start.30 = (f32[1,512]{1,0:T(1,128)}, f32[1,512]{1,0:T(1,128)S(1)}, u32[]{:S(2)}) copy-start(f32[1,512]{1,0:T(1,128)S(1)} %get-tuple-element.413) | copy-start | bytes 6148
  12.0 11.4 %copy-start.109 = (f32[128]{0:T(128)}, f32[128]{0:T(128)S(1)}, u32[]{:S(2)}) copy-start(f32[128]{0:T(128)S(1)} %sub.2460) | copy-start | bytes 1540
  25.6 0.9 copy-start.12
  28.9 0.9 copy-start.5
  33.2 60.8 %copy-start.1 = (f32[1,2,64,512]{3,2,1,0:T(8,128)}, f32[1,2,64,512]{3,2,1,0:T(8,128)S(1)}, u32[]{:S(2)}) copy-start(f32[1,2,64,512]{3,2,1,0:T(8,128)S(1)} %get-tuple-element.388) | copy-start | bytes 786436
  34.7 0.7 copy-start.17
  36.5 0.7 copy-start.70
  94.6 2.2 copy-start.34
  94.6 2.2 copy-start.36
  96.8 1.7 copy-start.94
  98.4 0.7 copy-start.66
  98.4 0.7 copy-start.93
  98.4 0.7 copy-start.11
  98.4 0.7 copy-start.37
  98.5 0.7 copy-start.35
  99.1 1.1 copy-start.88
  99.1 1.1 copy-start.89
  99.1 1.1 copy-start.90
  99.2 1.1 copy-start.91
  100.0 0.7 copy-start.74
  100.0 0.7 copy-start.75
  100.0 0.7 copy-start.76
  100.1 0.7 copy-start.78
  100.1 0.7 copy-start.82
  107.7 0.9 copy-start.2
  107.7 1.0 copy-start.3
  107.7 1.1 copy-start.4
  111.5 0.7 copy-start.25
  111.6 0.7 copy-start.50
  111.6 0.7 copy-start.100
  128.6 2.7 copy-start.7
  128.6 2.7 copy-start.8
  130.3 0.7 copy-start.15
  183.4 0.7 copy-start.20
  186.6 0.9 copy-start.6
  187.6 0.7 copy-start.101
  187.6 0.7 copy-start.105
  187.6 0.7 copy-start.107
  189.3 9.2 %collective-permute-start.2 = (f32[32,2080]{1,0:T(8,128)S(1)}, f32[32,2080]{1,0:T(8,128)S(1)}, u32[]{:S(2)}, u32[]{:S(2)}) collective-permute-start(f32[32,2080]{1,0:T(8,128)S(1)} %select_n.446), channel_id=1, source_target_pairs={{0,8},{8,0},{16,24},{24,16},{32,40},{40,32},{48,56},{56,48},{64,72... | collective-permute-start | bytes 798728 | tf_op jit(solution)/shard_map/ppermute | solution.py:60
  198.5 6.9 %collective-permute-start.3 = (f32[16,2080]{1,0:T(8,128)S(1)}, f32[16,2080]{1,0:T(8,128)S(1)}, u32[]{:S(2)}, u32[]{:S(2)}) collective-permute-start(f32[16,2080]{1,0:T(8,128)S(1)} %slice_select_fusion), channel_id=1, source_target_pairs={{0,64},{8,72},{16,80},{24,88},{32,96},{40,104},{48,112},{56,120},{... | collective-permute-start | bytes 399368 | tf_op jit(solution)/shard_map/ppermute | solution.py:60
  205.5 7.8 %collective-permute-start.4 = (f32[8,2080]{1,0:T(8,128)S(1)}, f32[8,2080]{1,0:T(8,128)S(1)}, u32[]{:S(2)}, u32[]{:S(2)}) collective-permute-start(f32[8,2080]{1,0:T(8,128)S(1)} %slice_select_fusion.1), channel_id=1, source_target_pairs={{0,16},{8,24},{16,0},{24,8},{32,48},{40,56},{48,32},{56,40},{64,80... | collective-permute-start | bytes 199688 | tf_op jit(solution)/shard_map/ppermute | solution.py:60
  213.4 6.8 %collective-permute-start.5 = (f32[4,2080]{1,0:T(4,128)S(1)}, f32[4,2080]{1,0:T(4,128)S(1)}, u32[]{:S(2)}, u32[]{:S(2)}) collective-permute-start(f32[4,2080]{1,0:T(4,128)S(1)} %slice_select_fusion.2), channel_id=1, source_target_pairs={{0,128},{8,136},{16,144},{24,152},{32,160},{40,168},{48,176},{56,1... | collective-permute-start | bytes 99848 | tf_op jit(solution)/shard_map/ppermute | solution.py:60
  220.2 9.6 %collective-permute-start.6 = (f32[2,2080]{1,0:T(2,128)S(1)}, f32[2,2080]{1,0:T(2,128)S(1)}, u32[]{:S(2)}, u32[]{:S(2)}) collective-permute-start(f32[2,2080]{1,0:T(2,128)S(1)} %broadcast_select_fusion.4), channel_id=1, source_target_pairs={{0,32},{8,40},{16,48},{24,56},{32,0},{40,8},{48,16},{56,24},{64,96... | collective-permute-start | bytes 49928 | tf_op jit(solution)/shard_map/ppermute | solution.py:60
  229.8 9.5 %collective-permute-start.7 = (f32[1,2080]{1,0:T(1,128)S(1)}, f32[1,2080]{1,0:T(1,128)S(1)}, u32[]{:S(2)}, u32[]{:S(2)}) collective-permute-start(f32[1,2080]{1,0:T(1,128)S(1)} %broadcast_select_fusion.5), channel_id=1, source_target_pairs={{0,256},{8,264},{16,272},{24,280},{32,288},{40,296},{48,304},{56,3... | collective-permute-start | bytes 24968 | tf_op jit(solution)/shard_map/ppermute | solution.py:60
  239.2 9.5 %collective-permute-start.8 = (f32[1,2080]{1,0:T(1,128)S(1)}, f32[1,2080]{1,0:T(1,128)S(1)}, u32[]{:S(2)}, u32[]{:S(2)}) collective-permute-start(f32[1,2080]{1,0:T(1,128)S(1)} %fusion.49), channel_id=1, source_target_pairs={{0,256},{8,264},{16,272},{24,280},{32,288},{40,296},{48,304},{56,3... | collective-permute-start | bytes 24968 | tf_op jit(solution)/shard_map/ppermute | solution.py:65
  248.7 9.6 %collective-permute-start.9 = (f32[2,2080]{1,0:T(2,128)S(1)}, f32[2,2080]{1,0:T(2,128)S(1)}, u32[]{:S(2)}, u32[]{:S(2)}) collective-permute-start(f32[2,2080]{1,0:T(2,128)S(1)} %maximum_select_fusion.5), channel_id=1, source_target_pairs={{0,32},{8,40},{16,48},{24,56},{32,0},{40,8},{48,16},{56,24},{64,96... | collective-permute-start | bytes 49928 | tf_op jit(solution)/shard_map/ppermute | solution.py:65
  258.3 9.3 %collective-permute-start.10 = (f32[4,2080]{1,0:T(4,128)S(1)}, f32[4,2080]{1,0:T(4,128)S(1)}, u32[]{:S(2)}, u32[]{:S(2)}) collective-permute-start(f32[4,2080]{1,0:T(4,128)S(1)} %maximum_select_fusion.4), channel_id=1, source_target_pairs={{0,128},{8,136},{16,144},{24,152},{32,160},{40,168},{48,176},{56,1... | collective-permute-start | bytes 99848 | tf_op jit(solution)/shard_map/ppermute | solution.py:65
  267.7 7.1 %collective-permute-start.11 = (f32[8,2080]{1,0:T(8,128)S(1)}, f32[8,2080]{1,0:T(8,128)S(1)}, u32[]{:S(2)}, u32[]{:S(2)}) collective-permute-start(f32[8,2080]{1,0:T(8,128)S(1)} %maximum_select_fusion.3), channel_id=1, source_target_pairs={{0,16},{8,24},{16,0},{24,8},{32,48},{40,56},{48,32},{56,40},{64,80... | collective-permute-start | bytes 199688 | tf_op jit(solution)/shard_map/ppermute | solution.py:65
  274.8 6.9 %collective-permute-start.12 = (f32[16,2080]{1,0:T(8,128)S(1)}, f32[16,2080]{1,0:T(8,128)S(1)}, u32[]{:S(2)}, u32[]{:S(2)}) collective-permute-start(f32[16,2080]{1,0:T(8,128)S(1)} %maximum_select_fusion.2), channel_id=1, source_target_pairs={{0,64},{8,72},{16,80},{24,88},{32,96},{40,104},{48,112},{56,120},{... | collective-permute-start | bytes 399368 | tf_op jit(solution)/shard_map/ppermute | solution.py:65
  281.8 13.8 %collective-permute-start.13 = (f32[32,2080]{1,0:T(8,128)S(1)}, f32[32,2080]{1,0:T(8,128)S(1)}, u32[]{:S(2)}, u32[]{:S(2)}) collective-permute-start(f32[32,2080]{1,0:T(8,128)S(1)} %maximum_select_fusion.1), channel_id=1, source_target_pairs={{0,8},{8,0},{16,24},{24,16},{32,40},{40,32},{48,56},{56,48},{64,72... | collective-permute-start | bytes 798728 | tf_op jit(solution)/shard_map/ppermute | solution.py:65
  283.7 10.4 %collective-permute-start.1 = (f32[3,512]{0,1:T(8,128)S(1)}, f32[3,512]{0,1:T(8,128)S(1)}, u32[]{:S(2)}, u32[]{:S(2)}) collective-permute-start(f32[3,512]{0,1:T(8,128)S(1)} %bitcast.1375), channel_id=1, source_target_pairs={{8,0},{16,8},{24,16},{32,24},{40,32},{48,40},{56,48},{64,56},{72,6... | collective-permute-start | bytes 18440 | tf_op jit(solution)/shard_map/ppermute | solution.py:12
  287.6 6.4 %copy-start.23 = (f32[1,512]{1,0:T(1,128)S(1)}, f32[1,512]{1,0:T(1,128)}, u32[]{:S(2)}) copy-start(f32[1,512]{1,0:T(1,128)} %copy-done.21) | copy-start | bytes 6148
  287.6 6.4 %copy-start.26 = (f32[1,512]{1,0:T(1,128)S(1)}, f32[1,512]{1,0:T(1,128)}, u32[]{:S(2)}) copy-start(f32[1,512]{1,0:T(1,128)} %copy-done.24) | copy-start | bytes 6148
  287.6 6.4 %copy-start.29 = (f32[1,512]{1,0:T(1,128)S(1)}, f32[1,512]{1,0:T(1,128)}, u32[]{:S(2)}) copy-start(f32[1,512]{1,0:T(1,128)} %copy-done.27) | copy-start | bytes 6148
  287.6 6.4 %copy-start.32 = (f32[1,512]{1,0:T(1,128)S(1)}, f32[1,512]{1,0:T(1,128)}, u32[]{:S(2)}) copy-start(f32[1,512]{1,0:T(1,128)} %copy-done.30) | copy-start | bytes 6148
  (62 other events, 41.2 us)

commit v4 on v1

--- a/solution.py
+++ b/solution.py
@@ -12,21 +12,40 @@
     return lax.ppermute(value, axis, pairs)
 
 
+def tree_fold(stack, upto, combine, unit):
+    keep = jnp.arange(stack.shape[0])[:, None, None] < upto
+    level = jnp.where(keep, stack, unit[None])
+    while level.shape[0] > 1:
+        joined = combine(tuple(level[0::2].swapaxes(0, 1)), tuple(level[1::2].swapaxes(0, 1)))
+        level = jnp.stack(joined, axis=1)
+    return level[0]
+
+
+def gather_all(value, axis):
+    count = lax.axis_size(axis)
+    spread = jnp.broadcast_to(value[None], (count,) + value.shape)
+    return lax.all_to_all(spread, axis, 0, 0, tiled=True)
+
+
 def carried_in(part, axis, combine, identity, reverse):
-    count = lax.axis_size(axis)
-    place = lax.axis_index(axis)
-    ahead = count - 1 - place if reverse else place
-    step = -1 if reverse else 1
     packed = jnp.stack(part)
     unit = jnp.stack([jnp.zeros_like(a) + jnp.asarray(e, a.dtype) for a, e in zip(part, identity)])
-    state = jnp.where(ahead >= 1, from_behind(packed, axis, step), unit)
-    reach = 1
-    while reach < count:
-        earlier = from_behind(state, axis, step * reach)
-        joined = jnp.stack(combine(tuple(earlier), tuple(state)))
-        state = jnp.where(ahead >= reach, joined, state)
-        reach *= 2
-    return tuple(state)
+    place = lax.axis_index(axis)
+    every = gather_all(packed, axis)
+    if reverse:
+        every = every[::-1]
+        place = lax.axis_size(axis) - 1 - place
+    before = tree_fold(every, place, combine, unit)
+    return tuple(before)
+
+
+def tree_sum(value, axis):
+    count = lax.axis_size(axis)
+    flat = value.reshape(-1)
+    width = -(-flat.size // count)
+    block = jnp.pad(flat, (0, width * count - flat.size)).reshape(count, width)
+    mine = jnp.sum(lax.all_to_all(block, axis, 0, 0, tiled=True), axis=0)
+    return gather_all(mine, axis).reshape(-1)[: flat.size].reshape(value.shape)
 
 
 def linear_run(drive_re, drive_im, decay_rate, turn_rate, log_keep):
@@ -164,7 +183,6 @@
     grad_bf = mixed_grad.astype(jnp.bfloat16).reshape(seq_len, local_heads, head_width)
     state_grad = jnp.einsum("thc,hck->thk", grad_bf, out_proj, preferred_element_type=jnp.float32)
     out_grad = jnp.einsum("thc,thk->hck", grad_bf, state_bf, preferred_element_type=jnp.float32)
-    out_grad = lax.psum(lax.psum(out_grad, "y"), "z")
     back_keep = jnp.concatenate([jnp.zeros((1,), jnp.float32), log_keep[::-1][:-1]])
     grad_re = state_grad[:, :, :state_size].reshape(seq_len, num_cols)[::-1]
     grad_im = state_grad[:, :, state_size:].reshape(seq_len, num_cols)[::-1]
@@ -215,10 +233,14 @@
             for offset in range(tap_count)
         ]
     )
-    packed = jnp.concatenate([in_grad.reshape(-1), taps_grad.reshape(-1)])
-    packed = lax.psum(lax.psum(packed, "y"), "z")
-    in_grad = packed[: in_grad.size].reshape(in_grad.shape)
-    taps_grad = packed[in_grad.size :].reshape(taps_grad.shape)
+    parts = (out_grad, in_grad, taps_grad)
+    packed = tree_sum(jnp.concatenate([p.reshape(-1) for p in parts]), SEQ)
+    ends = [0]
+    for p in parts:
+        ends.append(ends[-1] + p.size)
+    out_grad, in_grad, taps_grad = (
+        packed[a:b].reshape(p.shape) for a, b, p in zip(ends[:-1], ends[1:], parts)
+    )
     return (normed, tokens_grad.astype(jnp.bfloat16), in_grad, out_grad, taps_grad)
 
 

time: 366 us -> 187 us (0.51)
  waiting for transfers between devices: 209 us -> 29 us
  blocking collectives: 12.6 us -> 37.9 us
  starting transfers between devices: 62.6 us -> 41.7 us
  between operations: 15.8 us -> 2.11 us
  local copies, waits for them, and re-layouts: 39.3 us -> 47.1 us
    psum x2 -> x0, waiting for transfers between devices: 146 us -> none  [per_device(): packed = lax.psum(lax.psum(packed, 'y'), 'z')]
    ppermute x16 -> x2, starting transfers between devices: 62.5 us -> 6.85 us  [from_behind(): return lax.ppermute(value, axis, pairs)]
    ppermute x16 -> x2, waiting for transfers between devices: 62.9 us -> 14 us  [from_behind(): return lax.ppermute(value, axis, pairs)]
    all_to_all x0 -> x3, starting transfers between devices: none -> 34.8 us  [gather_all(): return lax.all_to_all(spread, axis, 0, 0, tiled=True)]
    all_to_all x0 -> x1, blocking collectives: none -> 24.1 us  [tree_sum(): mine = jnp.sum(lax.all_to_all(block, axis, 0, 0, tiled=True), axis=0)]
    all_to_all x0 -> x3, waiting for transfers between devices: none -> 15 us  [gather_all(): return lax.all_to_all(spread, axis, 0, 0, tiled=True)]
    unnamed x189 -> x166, local copies, waits for them, and re-layouts: 15.2 us -> 18.1 us
  transfers between devices with their start and end apart: 18 -> 5, of which waited for: 16 -> 2; matrix products, arithmetic and copies ran while one was open for 8% -> 18% of each run, Pallas kernels for 0% -> 0%
where the time goes in v4:
time: 187 us; the launch traced here: 185 us
  local copies, waits for them, and re-layouts  47.1 us (25%)
  starting transfers between devices  41.7 us (22%)
  blocking collectives  37.9 us (20%)
  waiting for transfers between devices  29 us (16%)
  other arithmetic  24.2 us (13%)
  matrix products  2.45 us (1%)
  between operations  2.11 us (1%)
    all_to_all x3, starting transfers between devices, gather_all(): return lax.all_to_all(spread, axis, 0, 0, tiled=True)  34.8 us
    all_to_all x1, blocking collectives, tree_sum(): mine = jnp.sum(lax.all_to_all(block, axis, 0, 0, tiled=True), axis=0)  24.1 us
    unnamed x166, local copies, waits for them, and re-layouts  18.1 us
    all_to_all x3, waiting for transfers between devices, gather_all(): return lax.all_to_all(spread, axis, 0, 0, tiled=True)  15 us
    ppermute x2, waiting for transfers between devices, from_behind(): return lax.ppermute(value, axis, pairs)  14 us
    psum x1, blocking collectives, per_device(): squares = lax.psum(squares, 'chan')  13.8 us
    ppermute x2, starting transfers between devices, from_behind(): return lax.ppermute(value, axis, pairs)  6.85 us
    another operation x8, other arithmetic  5.26 us
  transfers between devices with their start and end apart: 5, of which 2 were waited for; matrix products, arithmetic and copies ran while one was open for 18% of the time, Pallas kernels for 0%

profile of v4, /device:TPU:56, one launch (start us, length us, event | category | flops | bytes accessed | tf_op | source)
XLA Modules:
  0.0 184.6 jit_solution(6154580006702728405)
XLA Ops:
  0.6 0.7 slice.261
  1.6 3.5 %collective-permute-start = (bf16[3,512]{0,1:T(8,128)(2,1)S(1)}, bf16[3,512]{0,1:T(8,128)(2,1)S(1)}, u32[]{:S(2)}, u32[]{:S(2)}) collective-permute-start(bf16[3,512]{0,1:T(8,128)(2,1)S(1)} %copy.233), channel_id=1, source_target_pairs={{0,8},{8,16},{16,24},{24,32},{32,40},{40,48},{48,56},{56,64},{64,7... | collective-permute-start | bytes 9224 | tf_op jit(solution)/shard_map/ppermute | solution.py:12
  5.1 1.1 log_bitcast_fusion
  8.9 1.3 fusion.86
  10.2 2.5 %multiply_cosine_fusion.1 = (f32[64,512]{1,0:T(8,128)}, f32[64,512]{1,0:T(8,128)}, f32[64,512]{1,0:T(8,128)S(1)}, f32[64,512]{1,0:T(8,128)S(1)}, f32[64,512]{1,0...) fusion(f32[512]{0:T(512)S(1)} %get-tuple-element.389, ...), kind=kLoop, calls=%fused_computation.120 | loop fusion | flops 196608 | bytes 1317120 | tf_op jit(solution)/shard_map/cos | solution.py:89
  12.7 0.8 subtract_exponential_fusion.1
  13.5 0.7 fusion.67
  15.7 1.0 fusion.18
  20.6 0.7 copy-done.65
  21.4 0.6 copy-done.31
  22.5 0.6 copy-done.8
  23.2 0.8 multiply_subtract_fusion.3
  23.9 0.7 copy-done.61
  24.6 0.9 broadcast_in_dim.40
  25.5 15.0 %all-to-all-start = ((f32[64,4,512]{2,1,0:T(4,128)}), f32[64,4,512]{2,1,0:T(4,128)S(1)}, u32[]{:S(2)}, u32[]{:S(2)}) async-start(f32[64,4,512]{2,1,0:T(4,128)} %broadcast_in_dim.40), calls=%async_computation | async-start | bytes 1048576 | tf_op jit(solution)/shard_map/all_to_all | solution.py:27
  40.8 0.7 mul.2070
  41.5 0.7 mul.2073
  42.2 0.7 copy-done.54
  43.4 0.7 sub.516
  44.1 1.1 sub.517
  45.2 0.9 copy.232
  46.2 0.9 copy.238
  47.1 0.9 copy.240
  48.2 0.9 copy.241
  49.2 0.9 copy.242
  50.3 0.9 copy.244
  52.2 0.8 copy.255
  55.3 0.8 copy-done.11
  56.3 0.8 copy-done.14
  57.2 1.1 squeeze.81
  58.3 1.0 copy.243
  59.2 0.9 copy.245
  60.2 0.9 copy.237
  61.1 0.9 copy.239
  64.8 2.4 %subtract_convert_fusion = (bf16[128,8,64]{0,2,1:T(8,128)(2,1)S(1)}, bf16[128,8,64]{0,2,1:T(8,128)(2,1)S(1)}) fusion(f32[128,8,64]{0,2,1:T(8,128)S(1)} %copy-done.22, f32[128,8,64]{0,2,1:T(8,128)S(1)} %copy-done.21, f32[128,8,64]{0,2,1:T(8,128)} %copy.239, f32[128,8,64]{0,2,1:T(8,128)S(1)} %copy-done.17, f32[128,8,64]{0,2,1:T(8,128)} %copy.237, ...), kind=kLoop, calls=%fused_computation.105 | loop fusion | flops 2293760 | bytes 2893312 | tf_op jit(solution)/shard_map/convert.4
  67.5 0.6 copy-done.1
  68.2 0.7 multiply_reduce_fusion.4
  68.9 13.8 %all-reduce = (f32[128]{0:T(128)S(1)}, f32[128]{0:T(128)S(1)}) all-reduce(f32[128]{0:T(128)S(1)} %get-tuple-element.200, f32[128]{0:T(128)S(1)} %get-tuple-element.199), channel_id=1, replica_groups=mesh['z'=8,'y'=8,'chan'=8] {'chan'}, use_global_device_ids=true, to_apply=%region_6.7 | all-reduce | flops 256 | bytes 2048 | tf_op jit(solution)/shard_map/psum | solution.py:175
  83.7 0.7 copy-done.3
  85.2 0.7 copy-done.63
  85.9 0.8 add_multiply_fusion.2
  86.7 0.7 copy-done.30
  88.6 0.7 copy-done.60
  89.3 0.6 copy-done.58
  90.0 0.9 broadcast_in_dim.43
  90.9 12.7 %all-to-all-start.1 = ((f32[64,4,512]{2,1,0:T(4,128)}), f32[64,4,512]{2,1,0:T(4,128)S(1)}, u32[]{:S(2)}, u32[]{:S(2)}) async-start(f32[64,4,512]{2,1,0:T(4,128)} %broadcast_in_dim.43), calls=%async_computation.1 | async-start | bytes 1048576 | tf_op jit(solution)/shard_map/all_to_all | solution.py:27
  104.9 15.0 %all-to-all-done.1 = f32[64,4,512]{2,1,0:T(4,128)S(1)} async-done(((f32[64,4,512]{2,1,0:T(4,128)}), f32[64,4,512]{2,1,0:T(4,128)S(1)}, u32[]{:S(2)}, u32[]{:S(2)}) %all-to-all-start.1) | async-done | bytes 524320 | tf_op jit(solution)/shard_map/all_to_all | solution.py:27
  121.7 0.7 copy-done.37
  122.3 1.1 multiply_subtract_fusion
  124.9 0.7 copy-done.7
  125.9 0.6 copy-done.24
  126.9 0.7 multiply_reduce_fusion.3
  127.7 0.8 all_to_all.18
  128.5 24.1 %all_to_all.25 = f32[64,1,2080]{2,1,0:T(1,128)S(1)} all-to-all(f32[64,1,2080]{2,1,0:T(1,128)S(1)} %all_to_all.18), channel_id=1, replica_groups=mesh['z'=8,'y'=8,'chan'=8] {'z','y'}, dimensions={0} | all-to-all | bytes 1064960 | tf_op jit(solution)/shard_map/all_to_all | solution.py:47
  153.0 1.1 broadcast_in_dim.44
  154.1 7.1 %all-to-all-start.3 = ((f32[64,1,2080]{2,1,0:T(1,128)}), f32[64,1,2080]{2,1,0:T(1,128)S(1)}, u32[]{:S(2)}, u32[]{:S(2)}) async-start(f32[64,1,2080]{2,1,0:T(1,128)} %broadcast_in_dim.44), calls=%async_computation.3 | async-start | bytes 1114112 | tf_op jit(solution)/shard_map/all_to_all | solution.py:27
  161.2 3.4 %collective-permute-start.1 = (f32[3,512]{0,1:T(8,128)S(1)}, f32[3,512]{0,1:T(8,128)S(1)}, u32[]{:S(2)}, u32[]{:S(2)}) collective-permute-start(f32[3,512]{0,1:T(8,128)S(1)} %bitcast.355), channel_id=1, source_target_pairs={{8,0},{16,8},{24,16},{32,24},{40,32},{48,40},{56,48},{64,56},{72,6... | collective-permute-start | bytes 18440 | tf_op jit(solution)/shard_map/ppermute | solution.py:12
  164.6 0.8 copy.265
  165.4 14.0 %collective-permute-done.1 = f32[3,512]{0,1:T(8,128)S(1)} collective-permute-done((f32[3,512]{0,1:T(8,128)S(1)}, f32[3,512]{0,1:T(8,128)S(1)}, u32[]{:S(2)}, u32[]{:S(2)}) %collective-permute-start.1) | collective-permute-done | bytes 6176 | tf_op jit(solution)/shard_map/ppermute | solution.py:12
  179.4 0.7 fusion.28
  180.1 0.8 copy.266
  180.9 1.3 reduce.11
  183.2 0.8 fusion.81
  184.0 0.6 slice.379
  (308 shorter events, 26.0 us)
Async XLA Ops:
  0.6 66.6 %copy-start = (bf16[8,64,128]{2,1,0:T(8,128)(2,1)S(1)}, bf16[8,64,128]{2,1,0:T(8,128)(2,1)}, u32[]{:S(2)}) copy-start(bf16[8,64,128]{2,1,0:T(8,128)(2,1)} %param.19) | copy-start | bytes 393220
  1.6 3.5 %copy-start.77 = (f32[128]{0:T(128)S(1)}, f32[128]{0:T(128)}, u32[]{:S(2)}) copy-start(f32[128]{0:T(128)} %param.22) | copy-start | bytes 1540
  1.6 15.1 %collective-permute-start = (bf16[3,512]{0,1:T(8,128)(2,1)S(1)}, bf16[3,512]{0,1:T(8,128)(2,1)S(1)}, u32[]{:S(2)}, u32[]{:S(2)}) collective-permute-start(bf16[3,512]{0,1:T(8,128)(2,1)S(1)} %copy.233), channel_id=1, source_target_pairs={{0,8},{8,16},{16,24},{24,32},{32,40},{40,48},{48,56},{56,64},{64,7... | collective-permute-start | bytes 9224 | tf_op jit(solution)/shard_map/ppermute | solution.py:12
  8.0 6.5 %copy-start.56 = (f32[2,64]{1,0:T(2,128)}, f32[2,64]{1,0:T(2,128)S(1)}, u32[]{:S(2)}) copy-start(f32[2,64]{1,0:T(2,128)S(1)} %reduce.1) | copy-start | bytes 1540
  8.2 4.5 %copy-start.53 = (f32[2,64]{1,0:T(2,128)}, f32[2,64]{1,0:T(2,128)S(1)}, u32[]{:S(2)}) copy-start(f32[2,64]{1,0:T(2,128)S(1)} %reduce.7) | copy-start | bytes 1540
  8.2 0.7 copy-start.35
  12.7 40.2 %copy-start.4 = (f32[64,512]{1,0:T(8,128)}, f32[64,512]{1,0:T(8,128)S(1)}, u32[]{:S(2)}) copy-start(f32[64,512]{1,0:T(8,128)S(1)} %get-tuple-element.393) | copy-start | bytes 393220
  12.7 40.8 %copy-start.2 = (f32[64,512]{1,0:T(8,128)}, f32[64,512]{1,0:T(8,128)S(1)}, u32[]{:S(2)}) copy-start(f32[64,512]{1,0:T(8,128)S(1)} %get-tuple-element.392) | copy-start | bytes 393220
  12.7 1.5 copy-start.27
  13.5 0.7 copy-start.66
  14.2 2.6 %copy-start.38 = (f32[1,512]{1,0:T(1,128)}, f32[1,512]{1,0:T(1,128)S(1)}, u32[]{:S(2)}) copy-start(f32[1,512]{1,0:T(1,128)S(1)} %get-tuple-element.365) | copy-start | bytes 6148
  14.2 2.6 %copy-start.40 = (f32[1,512]{1,0:T(1,128)}, f32[1,512]{1,0:T(1,128)S(1)}, u32[]{:S(2)}) copy-start(f32[1,512]{1,0:T(1,128)S(1)} %get-tuple-element.366) | copy-start | bytes 6148
  14.3 2.6 %copy-start.42 = (f32[1,512]{1,0:T(1,128)}, f32[1,512]{1,0:T(1,128)S(1)}, u32[]{:S(2)}) copy-start(f32[1,512]{1,0:T(1,128)S(1)} %get-tuple-element.367) | copy-start | bytes 6148
  14.3 2.6 %copy-start.44 = (f32[1,512]{1,0:T(1,128)}, f32[1,512]{1,0:T(1,128)S(1)}, u32[]{:S(2)}) copy-start(f32[1,512]{1,0:T(1,128)S(1)} %get-tuple-element.368) | copy-start | bytes 6148
  14.5 1.2 copy-start.70
  16.9 0.9 copy-start.23
  20.5 1.9 %copy-start.12 = (f32[1,2,64,512]{3,2,1,0:T(8,128)}, f32[1,2,64,512]{3,2,1,0:T(8,128)S(1)}, u32[]{:S(2)}) copy-start(f32[1,2,64,512]{3,2,1,0:T(8,128)S(1)} %get-tuple-element.299) | copy-start | bytes 786436
  20.5 1.9 %copy-start.13 = (f32[1,2,64,512]{3,2,1,0:T(8,128)}, f32[1,2,64,512]{3,2,1,0:T(8,128)S(1)}, u32[]{:S(2)}) copy-start(f32[1,2,64,512]{3,2,1,0:T(8,128)S(1)} %get-tuple-element.296) | copy-start | bytes 786436
  20.6 0.7 copy-start.64
  21.3 0.7 copy-start.31
  21.3 0.7 copy-start.32
  22.4 0.7 copy-start.8
  22.4 0.8 copy-start.10
  25.5 36.5 %all-to-all-start = ((f32[64,4,512]{2,1,0:T(4,128)}), f32[64,4,512]{2,1,0:T(4,128)S(1)}, u32[]{:S(2)}, u32[]{:S(2)}) async-start(f32[64,4,512]{2,1,0:T(4,128)} %broadcast_in_dim.40), calls=%async_computation | async-start | bytes 1048576 | tf_op jit(solution)/shard_map/all_to_all | solution.py:27
  50.3 0.9 copy-start.74
  51.3 0.9 copy-start.28
  51.3 3.9 %copy-start.9 = (f32[2,64,512]{2,1,0:T(8,128)S(1)}, f32[2,64,512]{2,1,0:T(8,128)}, u32[]{:S(2)}) copy-start(f32[2,64,512]{2,1,0:T(8,128)} %copy-done.8) | copy-start | bytes 786436
  55.2 1.0 copy-start.11
  56.1 0.9 copy-start.14
  61.1 1.0 copy-start.33
  61.1 1.0 copy-start.76
  63.0 1.1 copy-start.21
  63.0 1.1 copy-start.22
  63.0 1.1 copy-start.20
  63.3 1.0 copy-start.19
  63.4 1.0 copy-start.18
  63.4 1.1 copy-start.17
  63.6 1.1 copy-start.16
  63.7 1.1 copy-start.15
  63.9 0.8 copy-start.52
  64.0 0.8 copy-start.51
  64.0 0.8 copy-start.71
  64.0 0.8 copy-start.72
  64.0 0.8 copy-start.75
  67.2 0.9 copy-start.1
  67.2 0.9 copy-start.39
  67.2 0.9 copy-start.41
  67.3 0.9 copy-start.43
  67.3 0.9 copy-start.45
  67.3 0.9 copy-start.50
  67.3 0.9 copy-start.67
  83.5 0.9 copy-start.3
  83.5 1.0 copy-start.5
  83.7 0.8 copy-start.55
  85.0 2.7 %copy-start.25 = (f32[64,512]{1,0:T(8,128)S(1)}, f32[64,512]{1,0:T(8,128)}, u32[]{:S(2)}) copy-start(f32[64,512]{1,0:T(8,128)} %get-tuple-element.370) | copy-start | bytes 393220
  85.1 2.7 %copy-start.26 = (f32[64,512]{1,0:T(8,128)S(1)}, f32[64,512]{1,0:T(8,128)}, u32[]{:S(2)}) copy-start(f32[64,512]{1,0:T(8,128)} %get-tuple-element.371) | copy-start | bytes 393220
  85.2 0.7 copy-start.62
  86.7 0.7 copy-start.30
  90.9 29.0 %all-to-all-start.1 = ((f32[64,4,512]{2,1,0:T(4,128)}), f32[64,4,512]{2,1,0:T(4,128)S(1)}, u32[]{:S(2)}, u32[]{:S(2)}) async-start(f32[64,4,512]{2,1,0:T(4,128)} %broadcast_in_dim.43), calls=%async_computation.1 | async-start | bytes 1048576 | tf_op jit(solution)/shard_map/all_to_all | solution.py:27
  104.6 15.3 %copy-start.34 = (f32[4,512]{1,0:T(4,128)S(1)}, f32[4,512]{1,0:T(4,128)}, u32[]{:S(2)}) copy-start(f32[4,512]{1,0:T(4,128)} %constant.67.clone.1) | copy-start | bytes 24580
  124.7 0.9 copy-start.7
  125.6 0.9 copy-start.24
  154.1 26.8 %all-to-all-start.3 = ((f32[64,1,2080]{2,1,0:T(1,128)}), f32[64,1,2080]{2,1,0:T(1,128)S(1)}, u32[]{:S(2)}, u32[]{:S(2)}) async-start(f32[64,1,2080]{2,1,0:T(1,128)} %broadcast_in_dim.44), calls=%async_computation.3 | async-start | bytes 1114112 | tf_op jit(solution)/shard_map/all_to_all | solution.py:27
  161.2 18.1 %collective-permute-start.1 = (f32[3,512]{0,1:T(8,128)S(1)}, f32[3,512]{0,1:T(8,128)S(1)}, u32[]{:S(2)}, u32[]{:S(2)}) collective-permute-start(f32[3,512]{0,1:T(8,128)S(1)} %bitcast.355), channel_id=1, source_target_pairs={{8,0},{16,8},{24,16},{32,24},{40,32},{48,40},{56,48},{64,56},{72,6... | collective-permute-start | bytes 18440 | tf_op jit(solution)/shard_map/ppermute | solution.py:12
  (20 other events, 13.2 us)

commit v5 on v4

--- a/solution.py
+++ b/solution.py
@@ -12,11 +12,16 @@
     return lax.ppermute(value, axis, pairs)
 
 
-def tree_fold(stack, upto, combine, unit):
-    keep = jnp.arange(stack.shape[0])[:, None, None] < upto
-    level = jnp.where(keep, stack, unit[None])
+def tree_fold(stack, order, upto, combine, unit):
+    count = len(order)
+    width = count.bit_length() - 1
+    flips = [int(format(r, f"0{width}b")[::-1], 2) for r in range(count)]
+    level = jnp.take(stack, jnp.asarray([order[f] for f in flips]), axis=0)
+    keep = jnp.asarray(flips)[:, None, None] < upto
+    level = jnp.where(keep, level, unit[None])
     while level.shape[0] > 1:
-        joined = combine(tuple(level[0::2].swapaxes(0, 1)), tuple(level[1::2].swapaxes(0, 1)))
+        half = level.shape[0] // 2
+        joined = combine(tuple(level[:half].swapaxes(0, 1)), tuple(level[half:].swapaxes(0, 1)))
         level = jnp.stack(joined, axis=1)
     return level[0]
 
@@ -32,10 +37,11 @@
     unit = jnp.stack([jnp.zeros_like(a) + jnp.asarray(e, a.dtype) for a, e in zip(part, identity)])
     place = lax.axis_index(axis)
     every = gather_all(packed, axis)
+    order = list(range(lax.axis_size(axis)))
     if reverse:
-        every = every[::-1]
+        order = order[::-1]
         place = lax.axis_size(axis) - 1 - place
-    before = tree_fold(every, place, combine, unit)
+    before = tree_fold(every, order, place, combine, unit)
     return tuple(before)
 
 
@@ -172,11 +178,10 @@
     squares = jnp.sum(mixed * mixed, axis=1)
     scaled = cotangent.astype(jnp.float32) * norm_gain
     dots = jnp.sum(scaled * mixed, axis=1)
-    squares = lax.psum(squares, "chan")
+    squares, dots = jnp.sum(gather_all(jnp.stack([squares, dots]), "chan"), axis=0)
     model_width = local_width * lax.axis_size("chan")
     inverse = lax.rsqrt(squares / model_width + 1e-06)
     normed = (mixed * inverse[:, None] * norm_gain).astype(jnp.bfloat16)
-    dots = lax.psum(dots, "chan")
     mixed_grad = inverse[:, None] * (
         scaled - mixed * (inverse * inverse * dots / model_width)[:, None]
     )

time: 187 us -> 188 us (level)
  blocking collectives: 37.9 us -> 24.4 us
  local copies, waits for them, and re-layouts: 47.1 us -> 52.4 us
  starting transfers between devices: 41.7 us -> 46 us
  waiting for transfers between devices: 29 us -> 32.8 us
    psum x1 -> x0, blocking collectives: 13.8 us -> none  [per_device(): squares = lax.psum(squares, 'chan')]
    all_to_all x3 -> x4, starting transfers between devices: 34.8 us -> 39.1 us  [gather_all(): return lax.all_to_all(spread, axis, 0, 0, tiled=True)]
    all_to_all x3 -> x4, waiting for transfers between devices: 15 us -> 18.6 us  [gather_all(): return lax.all_to_all(spread, axis, 0, 0, tiled=True)]
    unnamed x166 -> x180, local copies, waits for them, and re-layouts: 18.1 us -> 20.8 us
    gather x0 -> x2, local copies, waits for them, and re-layouts: none -> 1.98 us  [tree_fold(): level = jnp.take(stack, jnp.asarray([order[f] for f in flips]), axis=0)]
    another operation x8 -> x9, other arithmetic: 5.26 us -> 5.29 us
  transfers between devices with their start and end apart: 5 -> 6, of which waited for: 2 -> 3; matrix products, arithmetic and copies ran while one was open for 18% -> 18% of each run, Pallas kernels for 0% -> 0%
where the time goes in v5:
time: 188 us; the launch traced here: 186 us
  local copies, waits for them, and re-layouts  52.4 us (28%)
  starting transfers between devices  46 us (24%)
  waiting for transfers between devices  32.8 us (17%)
  other arithmetic  25.5 us (14%)
  blocking collectives  24.4 us (13%)
  matrix products  2.44 us (1%)
  between operations  2.18 us (1%)
    all_to_all x4, starting transfers between devices, gather_all(): return lax.all_to_all(spread, axis, 0, 0, tiled=True)  39.1 us
    all_to_all x1, blocking collectives, tree_sum(): mine = jnp.sum(lax.all_to_all(block, axis, 0, 0, tiled=True), axis=0)  24.4 us
    unnamed x180, local copies, waits for them, and re-layouts  20.8 us
    all_to_all x4, waiting for transfers between devices, gather_all(): return lax.all_to_all(spread, axis, 0, 0, tiled=True)  18.6 us
    ppermute x2, waiting for transfers between devices, from_behind(): return lax.ppermute(value, axis, pairs)  14.2 us
    ppermute x2, starting transfers between devices, from_behind(): return lax.ppermute(value, axis, pairs)  6.85 us
    another operation x8, other arithmetic  5.28 us
  transfers between devices with their start and end apart: 6, of which 3 were waited for; matrix products, arithmetic and copies ran while one was open for 18% of the time, Pallas kernels for 0%

profile of v5, /device:TPU:56, one launch (start us, length us, event | category | flops | bytes accessed | tf_op | source)
XLA Modules:
  0.0 185.8 jit_solution(5397142870529725978)
XLA Ops:
  0.6 0.7 slice.257
  1.6 3.5 %collective-permute-start = (bf16[3,512]{0,1:T(8,128)(2,1)S(1)}, bf16[3,512]{0,1:T(8,128)(2,1)S(1)}, u32[]{:S(2)}, u32[]{:S(2)}) collective-permute-start(bf16[3,512]{0,1:T(8,128)(2,1)S(1)} %copy.238), channel_id=1, source_target_pairs={{0,8},{8,16},{16,24},{24,32},{32,40},{40,48},{48,56},{56,64},{64,7... | collective-permute-start | bytes 9224 | tf_op jit(solution)/shard_map/ppermute | solution.py:12
  5.1 1.1 log_bitcast_fusion
  8.8 1.3 fusion.87
  10.1 2.6 %multiply_cosine_fusion.1 = (f32[64,512]{1,0:T(8,128)}, f32[64,512]{1,0:T(8,128)}, f32[64,512]{1,0:T(8,128)}, f32[64,512]{1,0:T(8,128)}, f32[64,512]{1,0:T(8,128...) fusion(f32[512]{0:T(512)S(1)} %get-tuple-element.388, ...), kind=kLoop, calls=%fused_computation.122 | loop fusion | flops 196608 | bytes 1317120 | tf_op jit(solution)/shard_map/cos | solution.py:95
  12.8 0.8 subtract_exponential_fusion.1
  13.6 0.7 fusion.67
  15.8 0.8 fusion.18
  19.1 0.7 copy-done.56
  19.8 0.8 add_multiply_fusion.1
  21.2 0.7 copy-done.62
  23.7 0.7 multiply_subtract_fusion.3
  24.5 0.7 copy-done.60
  25.2 0.9 broadcast_in_dim.51
  26.0 15.0 %all-to-all-start = ((f32[64,4,512]{2,1,0:T(4,128)}), f32[64,4,512]{2,1,0:T(4,128)S(1)}, u32[]{:S(2)}, u32[]{:S(2)}) async-start(f32[64,4,512]{2,1,0:T(4,128)} %broadcast_in_dim.51), calls=%async_computation | async-start | bytes 1048576 | tf_op jit(solution)/shard_map/all_to_all | solution.py:32
  41.4 0.7 mul.2078
  42.0 0.7 mul.2081
  42.7 0.7 sub.516
  43.4 1.1 sub.517
  44.5 0.9 copy.237
  45.4 0.9 copy.243
  46.3 0.9 copy.245
  47.4 0.9 copy.246
  48.5 0.9 copy.247
  49.6 0.9 copy.249
  51.4 0.7 reduce.4
  52.0 0.8 copy.259
  54.8 0.8 copy-done.7
  55.7 0.8 copy-done.10
  56.7 1.1 squeeze.81
  57.8 0.9 copy.248
  58.7 0.9 copy.250
  59.6 0.9 copy.242
  60.5 0.9 copy.244
  61.4 1.1 gather_fusion
  62.6 0.7 copy-done.74
  65.9 2.4 %subtract_convert_fusion = (bf16[128,8,64]{0,2,1:T(8,128)(2,1)S(1)}, bf16[128,8,64]{0,2,1:T(8,128)(2,1)S(1)}) fusion(f32[128,8,64]{0,2,1:T(8,128)S(1)} %copy-done.18, f32[128,8,64]{0,2,1:T(8,128)S(1)} %copy-done.17, f32[128,8,64]{0,2,1:T(8,128)} %copy.244, f32[128,8,64]{0,2,1:T(8,128)S(1)} %copy-done.13, f32[128,8,64]{0,2,1:T(8,128)} %copy.242, ...), kind=kLoop, calls=%fused_computation.108 | loop fusion | flops 2293760 | bytes 2893312 | tf_op jit(solution)/shard_map/convert.4
  69.4 0.7 multiply_reduce_fusion.5
  70.7 4.3 %all-to-all-start.1 = ((f32[8,2,128]{2,1,0:T(2,128)}), f32[8,2,128]{2,1,0:T(2,128)S(1)}, u32[]{:S(2)}, u32[]{:S(2)}) async-start(f32[8,2,128]{2,1,0:T(2,128)} %broadcast_in_dim.59), calls=%async_computation.1 | async-start | bytes 16384 | tf_op jit(solution)/shard_map/all_to_all | solution.py:32
  75.6 0.7 sub.563
  77.5 2.8 %all-to-all-done.1 = f32[8,2,128]{2,1,0:T(2,128)S(1)} async-done(((f32[8,2,128]{2,1,0:T(2,128)}), f32[8,2,128]{2,1,0:T(2,128)S(1)}, u32[]{:S(2)}, u32[]{:S(2)}) %all-to-all-start.1) | async-done | bytes 8224 | tf_op jit(solution)/shard_map/all_to_all | solution.py:32
  82.6 0.7 copy-done.64
  83.3 0.8 add_multiply_fusion.2
  84.2 0.6 copy-done.26
  86.9 0.7 copy-done.57
  87.6 0.9 broadcast_in_dim.61
  88.4 12.7 %all-to-all-start.2 = ((f32[64,4,512]{2,1,0:T(4,128)}), f32[64,4,512]{2,1,0:T(4,128)S(1)}, u32[]{:S(2)}, u32[]{:S(2)}) async-start(f32[64,4,512]{2,1,0:T(4,128)} %broadcast_in_dim.61), calls=%async_computation.2 | async-start | bytes 1048576 | tf_op jit(solution)/shard_map/all_to_all | solution.py:32
  103.0 15.8 %all-to-all-done.2 = f32[64,4,512]{2,1,0:T(4,128)S(1)} async-done(((f32[64,4,512]{2,1,0:T(4,128)}), f32[64,4,512]{2,1,0:T(4,128)S(1)}, u32[]{:S(2)}, u32[]{:S(2)}) %all-to-all-start.2) | async-done | bytes 524320 | tf_op jit(solution)/shard_map/all_to_all | solution.py:32
  118.7 0.9 gather_fusion.1
  122.0 0.7 copy-done.33
  122.7 1.1 multiply_subtract_fusion
  125.3 0.7 copy-done.5
  127.6 0.7 multiply_reduce_fusion.3
  128.4 0.8 all_to_all.22
  129.2 24.4 %all_to_all.30 = f32[64,1,2080]{2,1,0:T(1,128)S(1)} all-to-all(f32[64,1,2080]{2,1,0:T(1,128)S(1)} %all_to_all.22), channel_id=1, replica_groups=mesh['z'=8,'y'=8,'chan'=8] {'z','y'}, dimensions={0} | all-to-all | bytes 1064960 | tf_op jit(solution)/shard_map/all_to_all | solution.py:53
  154.0 1.1 broadcast_in_dim.62
  155.1 7.1 %all-to-all-start.4 = ((f32[64,1,2080]{2,1,0:T(1,128)}), f32[64,1,2080]{2,1,0:T(1,128)S(1)}, u32[]{:S(2)}, u32[]{:S(2)}) async-start(f32[64,1,2080]{2,1,0:T(1,128)} %broadcast_in_dim.62), calls=%async_computation.4 | async-start | bytes 1114112 | tf_op jit(solution)/shard_map/all_to_all | solution.py:32
  162.2 3.4 %collective-permute-start.1 = (f32[3,512]{0,1:T(8,128)S(1)}, f32[3,512]{0,1:T(8,128)S(1)}, u32[]{:S(2)}, u32[]{:S(2)}) collective-permute-start(f32[3,512]{0,1:T(8,128)S(1)} %bitcast.365), channel_id=1, source_target_pairs={{8,0},{16,8},{24,16},{32,24},{40,32},{48,40},{56,48},{64,56},{72,6... | collective-permute-start | bytes 18440 | tf_op jit(solution)/shard_map/ppermute | solution.py:12
  165.6 0.8 copy.271
  166.4 14.2 %collective-permute-done.1 = f32[3,512]{0,1:T(8,128)S(1)} collective-permute-done((f32[3,512]{0,1:T(8,128)S(1)}, f32[3,512]{0,1:T(8,128)S(1)}, u32[]{:S(2)}, u32[]{:S(2)}) %collective-permute-start.1) | collective-permute-done | bytes 6176 | tf_op jit(solution)/shard_map/ppermute | solution.py:12
  180.6 0.7 fusion.28
  181.3 0.8 copy.272
  182.1 1.3 reduce.11
  184.4 0.8 fusion.82
  (330 shorter events, 32.5 us)
Async XLA Ops:
  0.6 67.8 %copy-start = (bf16[8,64,128]{2,1,0:T(8,128)(2,1)S(1)}, bf16[8,64,128]{2,1,0:T(8,128)(2,1)}, u32[]{:S(2)}) copy-start(bf16[8,64,128]{2,1,0:T(8,128)(2,1)} %param.25) | copy-start | bytes 393220
  1.6 3.5 %copy-start.84 = (f32[128]{0:T(128)S(1)}, f32[128]{0:T(128)}, u32[]{:S(2)}) copy-start(f32[128]{0:T(128)} %param.28) | copy-start | bytes 1540
  1.6 15.0 %collective-permute-start = (bf16[3,512]{0,1:T(8,128)(2,1)S(1)}, bf16[3,512]{0,1:T(8,128)(2,1)S(1)}, u32[]{:S(2)}, u32[]{:S(2)}) collective-permute-start(bf16[3,512]{0,1:T(8,128)(2,1)S(1)} %copy.238), channel_id=1, source_target_pairs={{0,8},{8,16},{16,24},{24,32},{32,40},{40,48},{48,56},{56,64},{64,7... | collective-permute-start | bytes 9224 | tf_op jit(solution)/shard_map/ppermute | solution.py:12
  7.9 6.6 %copy-start.55 = (f32[2,64]{1,0:T(2,128)}, f32[2,64]{1,0:T(2,128)S(1)}, u32[]{:S(2)}) copy-start(f32[2,64]{1,0:T(2,128)S(1)} %reduce.1) | copy-start | bytes 1540
  8.1 4.7 %copy-start.53 = (f32[2,64]{1,0:T(2,128)}, f32[2,64]{1,0:T(2,128)S(1)}, u32[]{:S(2)}) copy-start(f32[2,64]{1,0:T(2,128)S(1)} %reduce.7) | copy-start | bytes 1540
  8.1 0.7 copy-start.31
  12.8 1.5 copy-start.23
  13.6 0.7 copy-start.65
  14.3 2.5 %copy-start.34 = (f32[1,512]{1,0:T(1,128)}, f32[1,512]{1,0:T(1,128)S(1)}, u32[]{:S(2)}) copy-start(f32[1,512]{1,0:T(1,128)S(1)} %get-tuple-element.364) | copy-start | bytes 6148
  14.3 2.5 %copy-start.37 = (f32[1,512]{1,0:T(1,128)}, f32[1,512]{1,0:T(1,128)S(1)}, u32[]{:S(2)}) copy-start(f32[1,512]{1,0:T(1,128)S(1)} %get-tuple-element.365) | copy-start | bytes 6148
  14.3 2.5 %copy-start.40 = (f32[1,512]{1,0:T(1,128)}, f32[1,512]{1,0:T(1,128)S(1)}, u32[]{:S(2)}) copy-start(f32[1,512]{1,0:T(1,128)S(1)} %get-tuple-element.366) | copy-start | bytes 6148
  14.3 2.5 %copy-start.43 = (f32[1,512]{1,0:T(1,128)}, f32[1,512]{1,0:T(1,128)S(1)}, u32[]{:S(2)}) copy-start(f32[1,512]{1,0:T(1,128)S(1)} %get-tuple-element.367) | copy-start | bytes 6148
  14.6 1.2 copy-start.70
  16.8 0.9 copy-start.19
  21.1 2.0 %copy-start.8 = (f32[1,2,64,512]{3,2,1,0:T(8,128)}, f32[1,2,64,512]{3,2,1,0:T(8,128)S(1)}, u32[]{:S(2)}) copy-start(f32[1,2,64,512]{3,2,1,0:T(8,128)S(1)} %get-tuple-element.298) | copy-start | bytes 786436
  21.1 2.0 %copy-start.9 = (f32[1,2,64,512]{3,2,1,0:T(8,128)}, f32[1,2,64,512]{3,2,1,0:T(8,128)S(1)}, u32[]{:S(2)}) copy-start(f32[1,2,64,512]{3,2,1,0:T(8,128)S(1)} %get-tuple-element.295) | copy-start | bytes 786436
  21.1 0.7 copy-start.62
  21.2 0.7 copy-start.61
  21.9 0.7 copy-start.28
  23.0 0.7 copy-start.6
  26.0 35.4 %all-to-all-start = ((f32[64,4,512]{2,1,0:T(4,128)}), f32[64,4,512]{2,1,0:T(4,128)S(1)}, u32[]{:S(2)}, u32[]{:S(2)}) async-start(f32[64,4,512]{2,1,0:T(4,128)} %broadcast_in_dim.51), calls=%async_computation | async-start | bytes 1048576 | tf_op jit(solution)/shard_map/all_to_all | solution.py:32
  51.1 0.9 copy-start.24
  54.6 0.9 copy-start.7
  55.6 0.9 copy-start.10
  61.4 1.1 copy-start.29
  64.1 1.1 copy-start.17
  64.2 1.1 copy-start.18
  64.2 1.1 copy-start.16
  64.4 1.0 copy-start.15
  64.6 1.0 copy-start.14
  64.6 1.1 copy-start.13
  64.7 1.1 copy-start.12
  64.8 1.1 copy-start.11
  65.1 0.8 copy-start.52
  65.1 0.8 copy-start.51
  65.2 0.8 copy-start.71
  65.2 0.8 copy-start.72
  65.2 0.8 copy-start.82
  68.4 0.9 copy-start.1
  68.4 0.9 copy-start.35
  68.4 0.9 copy-start.38
  68.4 0.9 copy-start.41
  68.4 0.9 copy-start.44
  68.4 0.9 copy-start.49
  68.5 0.9 copy-start.66
  69.3 7.0 %copy-start.3 = (f32[64,512]{1,0:T(8,128)S(1)}, f32[64,512]{1,0:T(8,128)}, u32[]{:S(2)}) copy-start(f32[64,512]{1,0:T(8,128)} %get-tuple-element.392) | copy-start | bytes 393220
  69.3 7.5 %copy-start.2 = (f32[64,512]{1,0:T(8,128)S(1)}, f32[64,512]{1,0:T(8,128)}, u32[]{:S(2)}) copy-start(f32[64,512]{1,0:T(8,128)} %get-tuple-element.391) | copy-start | bytes 393220
  70.7 9.6 %all-to-all-start.1 = ((f32[8,2,128]{2,1,0:T(2,128)}), f32[8,2,128]{2,1,0:T(2,128)S(1)}, u32[]{:S(2)}, u32[]{:S(2)}) async-start(f32[8,2,128]{2,1,0:T(2,128)} %broadcast_in_dim.59), calls=%async_computation.1 | async-start | bytes 16384 | tf_op jit(solution)/shard_map/all_to_all | solution.py:32
  82.5 2.7 %copy-start.21 = (f32[64,512]{1,0:T(8,128)S(1)}, f32[64,512]{1,0:T(8,128)}, u32[]{:S(2)}) copy-start(f32[64,512]{1,0:T(8,128)} %get-tuple-element.369) | copy-start | bytes 393220
  82.5 2.7 %copy-start.22 = (f32[64,512]{1,0:T(8,128)S(1)}, f32[64,512]{1,0:T(8,128)}, u32[]{:S(2)}) copy-start(f32[64,512]{1,0:T(8,128)} %get-tuple-element.370) | copy-start | bytes 393220
  82.6 0.7 copy-start.63
  88.4 30.3 %all-to-all-start.2 = ((f32[64,4,512]{2,1,0:T(4,128)}), f32[64,4,512]{2,1,0:T(4,128)S(1)}, u32[]{:S(2)}, u32[]{:S(2)}) async-start(f32[64,4,512]{2,1,0:T(4,128)} %broadcast_in_dim.61), calls=%async_computation.2 | async-start | bytes 1048576 | tf_op jit(solution)/shard_map/all_to_all | solution.py:32
  103.0 16.6 %copy-start.30 = (f32[4,512]{1,0:T(4,128)S(1)}, f32[4,512]{1,0:T(4,128)}, u32[]{:S(2)}) copy-start(f32[4,512]{1,0:T(4,128)} %constant.81.clone.1) | copy-start | bytes 24580
  125.1 0.9 copy-start.5
  126.0 0.9 copy-start.20
  126.9 0.7 copy-start.67
  126.9 0.7 copy-start.79
  126.9 0.7 copy-start.81
  155.1 27.0 %all-to-all-start.4 = ((f32[64,1,2080]{2,1,0:T(1,128)}), f32[64,1,2080]{2,1,0:T(1,128)S(1)}, u32[]{:S(2)}, u32[]{:S(2)}) async-start(f32[64,1,2080]{2,1,0:T(1,128)} %broadcast_in_dim.62), calls=%async_computation.4 | async-start | bytes 1114112 | tf_op jit(solution)/shard_map/all_to_all | solution.py:32
  162.2 18.4 %collective-permute-start.1 = (f32[3,512]{0,1:T(8,128)S(1)}, f32[3,512]{0,1:T(8,128)S(1)}, u32[]{:S(2)}, u32[]{:S(2)}) collective-permute-start(f32[3,512]{0,1:T(8,128)S(1)} %bitcast.365), channel_id=1, source_target_pairs={{8,0},{16,8},{24,16},{32,24},{40,32},{48,40},{56,48},{64,56},{72,6... | collective-permute-start | bytes 18440 | tf_op jit(solution)/shard_map/ppermute | solution.py:12
  165.6 15.0 %copy-start.36 = (f32[1,512]{1,0:T(1,128)S(1)}, f32[1,512]{1,0:T(1,128)}, u32[]{:S(2)}) copy-start(f32[1,512]{1,0:T(1,128)} %copy-done.34) | copy-start | bytes 6148
  165.6 15.0 %copy-start.39 = (f32[1,512]{1,0:T(1,128)S(1)}, f32[1,512]{1,0:T(1,128)}, u32[]{:S(2)}) copy-start(f32[1,512]{1,0:T(1,128)} %copy-done.37) | copy-start | bytes 6148
  165.6 15.0 %copy-start.42 = (f32[1,512]{1,0:T(1,128)S(1)}, f32[1,512]{1,0:T(1,128)}, u32[]{:S(2)}) copy-start(f32[1,512]{1,0:T(1,128)} %copy-done.40) | copy-start | bytes 6148
  165.6 15.0 %copy-start.45 = (f32[1,512]{1,0:T(1,128)S(1)}, f32[1,512]{1,0:T(1,128)}, u32[]{:S(2)}) copy-start(f32[1,512]{1,0:T(1,128)} %copy-done.43) | copy-start | bytes 6148
  (28 other events, 18.3 us)

commit v6 on v5

--- a/solution.py
+++ b/solution.py
@@ -32,11 +32,10 @@
     return lax.all_to_all(spread, axis, 0, 0, tiled=True)
 
 
-def carried_in(part, axis, combine, identity, reverse):
-    packed = jnp.stack(part)
-    unit = jnp.stack([jnp.zeros_like(a) + jnp.asarray(e, a.dtype) for a, e in zip(part, identity)])
+def carried_in(mult_re, mult_im, every, axis, combine, identity, reverse):
+    every = jnp.concatenate([jnp.stack([mult_re, mult_im], axis=1), every[:, :2]], axis=1)
+    unit = jnp.stack([jnp.zeros_like(mult_re[0]) + e for e in identity])
     place = lax.axis_index(axis)
-    every = gather_all(packed, axis)
     order = list(range(lax.axis_size(axis)))
     if reverse:
         order = order[::-1]
@@ -144,18 +143,13 @@
     log_keep = jnp.log(retention)
     state_re, state_im = linear_run(drive_re, drive_im, log_rate, rotation, log_keep)
     keep_total = jnp.sum(log_keep)
-    total_mag = jnp.exp(keep_total - seq_len * log_rate)
+    ends = gather_all(
+        jnp.stack([state_re[-1], state_im[-1], jnp.broadcast_to(keep_total, state_re[-1].shape)]), SEQ
+    )
+    total_mag = jnp.exp(ends[:, 2, :1] - seq_len * log_rate)
     total_re = total_mag * jnp.cos(seq_len * rotation)
     total_im = total_mag * jnp.sin(seq_len * rotation)
-    unit_ones = jnp.ones((num_cols,), jnp.float32)
-    zeros_col = jnp.zeros((num_cols,), jnp.float32)
-    chained = carried_in(
-        (total_re, total_im, state_re[-1], state_im[-1]),
-        SEQ,
-        carry_combine,
-        (unit_ones, zeros_col, zeros_col, zeros_col),
-        False,
-    )
+    chained = carried_in(total_re, total_im, ends, SEQ, carry_combine, (1.0, 0.0, 0.0, 0.0), False)
     enter_re, enter_im = (chained[2], chained[3])
     positions = jnp.arange(seq_len, dtype=jnp.float32)
     ahead = positions + 1.0
@@ -197,12 +191,9 @@
     sin_turn = jnp.sin(rotation)
     first_re = first_mag * (cos_turn * adj_re[-1] + sin_turn * adj_im[-1])
     first_im = first_mag * (cos_turn * adj_im[-1] - sin_turn * adj_re[-1])
+    firsts = gather_all(jnp.stack([first_re, first_im]), SEQ)
     back_chained = carried_in(
-        (total_re, -total_im, first_re, first_im),
-        SEQ,
-        carry_combine,
-        (unit_ones, zeros_col, zeros_col, zeros_col),
-        True,
+        total_re, -total_im, firsts, SEQ, carry_combine, (1.0, 0.0, 0.0, 0.0), True
     )
     later_re, later_im = (back_chained[2], back_chained[3])
     back_lift = jnp.exp(jnp.cumsum(back_keep)[:, None] - positions[:, None] * log_rate[None, :])

time: 188 us -> 182 us (0.968)
  waiting for transfers between devices: 32.8 us -> 27.2 us
  local copies, waits for them, and re-layouts: 52.4 us -> 50.4 us
    all_to_all x4, waiting for transfers between devices: 18.6 us -> 12.8 us  [gather_all(): return lax.all_to_all(spread, axis, 0, 0, tiled=True)]
    unnamed x180 -> x157, local copies, waits for them, and re-layouts: 20.8 us -> 16.4 us
    slice x0 -> x2, local copies, waits for them, and re-layouts: none -> 2.6 us  [the longest x1 1.46 us: per_device(): total_mag = jnp.exp(ends[:, 2, :1] - seq_len * log_rate)]
  transfers between devices with their start and end apart: 6 -> 6, of which waited for: 3 -> 3; matrix products, arithmetic and copies ran while one was open for 18% -> 17% of each run, Pallas kernels for 0% -> 0%
where the time goes in v6:
time: 182 us; the launch traced here: 179 us
  local copies, waits for them, and re-layouts  50.4 us (28%)
  starting transfers between devices  46.2 us (25%)
  waiting for transfers between devices  27.2 us (15%)
  other arithmetic  26.3 us (14%)
  blocking collectives  24.5 us (13%)
  matrix products  2.45 us (1%)
  between operations  2.1 us (1%)
    all_to_all x4, starting transfers between devices, gather_all(): return lax.all_to_all(spread, axis, 0, 0, tiled=True)  39.3 us
    all_to_all x1, blocking collectives, tree_sum(): mine = jnp.sum(lax.all_to_all(block, axis, 0, 0, tiled=True), axis=0)  24.5 us
    unnamed x157, local copies, waits for them, and re-layouts  16.4 us
    ppermute x2, waiting for transfers between devices, from_behind(): return lax.ppermute(value, axis, pairs)  14.4 us
    all_to_all x4, waiting for transfers between devices, gather_all(): return lax.all_to_all(spread, axis, 0, 0, tiled=True)  12.8 us
    ppermute x2, starting transfers between devices, from_behind(): return lax.ppermute(value, axis, pairs)  6.85 us
    another operation x8, other arithmetic  4.99 us
  transfers between devices with their start and end apart: 6, of which 3 were waited for; matrix products, arithmetic and copies ran while one was open for 17% of the time, Pallas kernels for 0%

profile of v6, /device:TPU:56, one launch (start us, length us, event | category | flops | bytes accessed | tf_op | source)
XLA Modules:
  0.0 179.3 jit_solution(1836530957703305836)
XLA Ops:
  0.6 0.7 slice.263
  1.6 3.5 %collective-permute-start = (bf16[3,512]{0,1:T(8,128)(2,1)S(1)}, bf16[3,512]{0,1:T(8,128)(2,1)S(1)}, u32[]{:S(2)}, u32[]{:S(2)}) collective-permute-start(bf16[3,512]{0,1:T(8,128)(2,1)S(1)} %copy.239), channel_id=1, source_target_pairs={{0,8},{8,16},{16,24},{24,32},{32,40},{40,48},{48,56},{56,64},{64,7... | collective-permute-start | bytes 9224 | tf_op jit(solution)/shard_map/ppermute | solution.py:12
  6.4 0.7 fusion.81
  9.0 2.5 %multiply_cosine_fusion.1 = (f32[64,512]{1,0:T(8,128)}, f32[64,512]{1,0:T(8,128)}, f32[64,512]{1,0:T(8,128)S(1)}, f32[64,512]{1,0:T(8,128)S(1)}, f32[64,512]{1,0...) fusion(f32[512]{0:T(512)S(1)} %get-tuple-element.418, ...), kind=kLoop, calls=%fused_computation.126 | loop fusion | flops 196608 | bytes 1317120 | tf_op jit(solution)/shard_map/cos | solution.py:94
  11.5 0.8 subtract_exponential_fusion.1
  12.3 0.7 fusion.68
  13.3 0.7 pad.61.clone
  14.0 1.1 fusion.20
  19.5 0.8 multiply_subtract_fusion.3
  20.3 0.9 broadcast_in_dim.51
  21.2 15.2 %all-to-all-start = ((f32[64,3,512]{2,1,0:T(4,128)}), f32[64,3,512]{2,1,0:T(4,128)}, u32[]{:S(2)}, u32[]{:S(2)}) async-start(f32[64,3,512]{2,1,0:T(4,128)} %broadcast_in_dim.51), calls=%async_computation | async-start | bytes 1048576 | tf_op jit(solution)/shard_map/all_to_all | solution.py:32
  36.7 0.7 mul.2106
  37.3 0.7 mul.2109
  38.0 0.7 sub.540
  38.7 1.1 sub.541
  39.8 0.9 copy.238
  40.7 0.9 copy.244
  41.7 0.9 copy.246
  42.7 0.9 copy.247
  43.8 0.9 copy.248
  44.9 0.9 copy.250
  46.1 0.6 reduce.4
  48.9 0.8 copy-done.2
  49.8 0.8 copy-done.5
  50.8 1.1 squeeze.82
  51.9 0.9 copy.249
  52.8 0.9 copy.251
  53.7 0.9 copy.243
  54.6 0.9 copy.245
  55.6 1.5 slice_reduce_fusion
  57.0 0.6 copy-done.48
  57.7 0.8 fusion.59
  58.7 1.1 slice.364
  60.2 1.1 gather_fusion
  61.4 0.6 copy-done.63
  64.7 2.6 %subtract_convert_fusion = (bf16[128,8,64]{0,2,1:T(8,128)(2,1)S(1)}, bf16[128,8,64]{0,2,1:T(8,128)(2,1)S(1)}) fusion(f32[128,8,64]{0,2,1:T(8,128)} %copy.251, f32[128,8,64]{0,2,1:T(8,128)} %copy.249, f32[128,8,64]{0,2,1:T(8,128)} %copy.245, f32[128,8,64]{0,2,1:T(8,128)S(1)} %copy-done.8, f32[128,8,64]{0,2,1:T(8,128)} %copy.243, ...), kind=kLoop, calls=%fused_computation.112 | loop fusion | flops 2293760 | bytes 2893312 | tf_op jit(solution)/shard_map/convert.4
  68.0 0.7 multiply_reduce_fusion.5
  69.4 4.3 %all-to-all-start.1 = ((f32[8,2,128]{2,1,0:T(2,128)}), f32[8,2,128]{2,1,0:T(2,128)S(1)}, u32[]{:S(2)}, u32[]{:S(2)}) async-start(f32[8,2,128]{2,1,0:T(2,128)} %broadcast_in_dim.53), calls=%async_computation.1 | async-start | bytes 16384 | tf_op jit(solution)/shard_map/all_to_all | solution.py:32
  73.7 0.7 copy-done.46
  76.1 2.9 %all-to-all-done.1 = f32[8,2,128]{2,1,0:T(2,128)S(1)} async-done(((f32[8,2,128]{2,1,0:T(2,128)}), f32[8,2,128]{2,1,0:T(2,128)S(1)}, u32[]{:S(2)}, u32[]{:S(2)}) %all-to-all-start.1) | async-done | bytes 8224 | tf_op jit(solution)/shard_map/all_to_all | solution.py:32
  81.3 0.7 copy-done.53
  82.0 0.8 add_multiply_fusion.2
  82.8 0.6 copy-done.20
  85.0 1.0 fusion.15
  86.7 0.8 broadcast_in_dim.55
  87.5 12.7 %all-to-all-start.2 = ((f32[64,2,512]{2,1,0:T(2,128)}), f32[64,2,512]{2,1,0:T(2,128)S(1)}, u32[]{:S(2)}, u32[]{:S(2)}) async-start(f32[64,2,512]{2,1,0:T(2,128)} %broadcast_in_dim.55), calls=%async_computation.2 | async-start | bytes 524288 | tf_op jit(solution)/shard_map/all_to_all | solution.py:32
  100.2 0.7 copy-done.64
  102.3 10.0 %all-to-all-done.2 = f32[64,2,512]{2,1,0:T(2,128)S(1)} async-done(((f32[64,2,512]{2,1,0:T(2,128)}), f32[64,2,512]{2,1,0:T(2,128)S(1)}, u32[]{:S(2)}, u32[]{:S(2)}) %all-to-all-start.2) | async-done | bytes 262176 | tf_op jit(solution)/shard_map/all_to_all | solution.py:32
  112.6 0.9 gather_fusion.1
  113.5 0.6 copy-done.62
  115.9 0.7 copy-done.24
  116.6 1.1 multiply_subtract_fusion
  120.8 0.7 multiply_reduce_fusion.3
  121.6 0.8 all_to_all.22
  122.3 24.5 %all_to_all.30 = f32[64,1,2080]{2,1,0:T(1,128)S(1)} all-to-all(f32[64,1,2080]{2,1,0:T(1,128)S(1)} %all_to_all.22), channel_id=1, replica_groups=mesh['z'=8,'y'=8,'chan'=8] {'z','y'}, dimensions={0} | all-to-all | bytes 1064960 | tf_op jit(solution)/shard_map/all_to_all | solution.py:52
  147.2 1.1 broadcast_in_dim.62
  148.4 7.1 %all-to-all-start.4 = ((f32[64,1,2080]{2,1,0:T(1,128)}), f32[64,1,2080]{2,1,0:T(1,128)S(1)}, u32[]{:S(2)}, u32[]{:S(2)}) async-start(f32[64,1,2080]{2,1,0:T(1,128)} %broadcast_in_dim.62), calls=%async_computation.4 | async-start | bytes 1114112 | tf_op jit(solution)/shard_map/all_to_all | solution.py:32
  155.5 3.4 %collective-permute-start.1 = (f32[3,512]{0,1:T(8,128)S(1)}, f32[3,512]{0,1:T(8,128)S(1)}, u32[]{:S(2)}, u32[]{:S(2)}) collective-permute-start(f32[3,512]{0,1:T(8,128)S(1)} %bitcast.365), channel_id=1, source_target_pairs={{8,0},{16,8},{24,16},{32,24},{40,32},{48,40},{56,48},{64,56},{72,6... | collective-permute-start | bytes 18440 | tf_op jit(solution)/shard_map/ppermute | solution.py:12
  158.9 0.8 copy.276
  159.7 14.4 %collective-permute-done.1 = f32[3,512]{0,1:T(8,128)S(1)} collective-permute-done((f32[3,512]{0,1:T(8,128)S(1)}, f32[3,512]{0,1:T(8,128)S(1)}, u32[]{:S(2)}, u32[]{:S(2)}) %collective-permute-start.1) | collective-permute-done | bytes 6176 | tf_op jit(solution)/shard_map/ppermute | solution.py:12
  174.0 0.7 fusion.30
  174.8 0.8 copy.277
  175.6 1.3 reduce.12
  177.9 0.8 fusion.82
  (316 shorter events, 30.8 us)
Async XLA Ops:
  0.6 66.7 %copy-start = (bf16[8,64,128]{2,1,0:T(8,128)(2,1)S(1)}, bf16[8,64,128]{2,1,0:T(8,128)(2,1)}, u32[]{:S(2)}) copy-start(bf16[8,64,128]{2,1,0:T(8,128)(2,1)} %param.25) | copy-start | bytes 393220
  1.6 3.5 %copy-start.72 = (f32[128]{0:T(128)S(1)}, f32[128]{0:T(128)}, u32[]{:S(2)}) copy-start(f32[128]{0:T(128)} %param.28) | copy-start | bytes 1540
  1.6 13.5 %collective-permute-start = (bf16[3,512]{0,1:T(8,128)(2,1)S(1)}, bf16[3,512]{0,1:T(8,128)(2,1)S(1)}, u32[]{:S(2)}, u32[]{:S(2)}) collective-permute-start(bf16[3,512]{0,1:T(8,128)(2,1)S(1)} %copy.239), channel_id=1, source_target_pairs={{0,8},{8,16},{16,24},{24,32},{32,40},{40,48},{48,56},{56,64},{64,7... | collective-permute-start | bytes 9224 | tf_op jit(solution)/shard_map/ppermute | solution.py:12
  7.5 0.7 copy-start.23
  7.6 3.9 %copy-start.45 = (f32[2,64]{1,0:T(2,128)}, f32[2,64]{1,0:T(2,128)S(1)}, u32[]{:S(2)}) copy-start(f32[2,64]{1,0:T(2,128)S(1)} %reduce.8) | copy-start | bytes 1540
  7.6 0.7 copy-start.19
  9.0 8.6 %copy-start.37 = (f32[512]{0:T(512)}, f32[512]{0:T(512)S(1)}, u32[]{:S(2)}) copy-start(f32[512]{0:T(512)S(1)} %get-tuple-element.398) | copy-start | bytes 6148
  11.5 1.5 copy-start.17
  12.3 0.7 copy-start.54
  13.0 2.2 %copy-start.25 = (f32[1,512]{1,0:T(1,128)}, f32[1,512]{1,0:T(1,128)S(1)}, u32[]{:S(2)}) copy-start(f32[1,512]{1,0:T(1,128)S(1)} %get-tuple-element.362) | copy-start | bytes 6148
  13.0 2.2 %copy-start.28 = (f32[1,512]{1,0:T(1,128)}, f32[1,512]{1,0:T(1,128)S(1)}, u32[]{:S(2)}) copy-start(f32[1,512]{1,0:T(1,128)S(1)} %get-tuple-element.363) | copy-start | bytes 6148
  13.0 2.2 %copy-start.31 = (f32[1,512]{1,0:T(1,128)}, f32[1,512]{1,0:T(1,128)S(1)}, u32[]{:S(2)}) copy-start(f32[1,512]{1,0:T(1,128)S(1)} %get-tuple-element.364) | copy-start | bytes 6148
  13.0 2.2 %copy-start.34 = (f32[1,512]{1,0:T(1,128)}, f32[1,512]{1,0:T(1,128)S(1)}, u32[]{:S(2)}) copy-start(f32[1,512]{1,0:T(1,128)S(1)} %get-tuple-element.365) | copy-start | bytes 6148
  13.3 0.7 copy-start.59
  15.3 0.9 copy-start.12
  18.3 0.7 copy-start.3
  18.3 0.8 copy-start.4
  18.8 0.7 copy-start.1
  21.2 34.4 %all-to-all-start = ((f32[64,3,512]{2,1,0:T(4,128)}), f32[64,3,512]{2,1,0:T(4,128)}, u32[]{:S(2)}, u32[]{:S(2)}) async-start(f32[64,3,512]{2,1,0:T(4,128)} %broadcast_in_dim.51), calls=%async_computation | async-start | bytes 1048576 | tf_op jit(solution)/shard_map/all_to_all | solution.py:32
  45.8 0.9 copy-start.18
  48.7 0.9 copy-start.2
  49.7 0.9 copy-start.5
  54.6 2.4 %copy-start.49 = (f32[512]{0:T(512)S(1)}, f32[512]{0:T(512)}, u32[]{:S(2)}) copy-start(f32[512]{0:T(512)} %get-tuple-element.419) | copy-start | bytes 6148
  60.2 1.1 copy-start.21
  63.0 1.0 copy-start.11
  63.2 1.0 copy-start.10
  63.4 1.0 copy-start.9
  63.4 1.0 copy-start.8
  63.5 1.0 copy-start.7
  63.6 1.0 copy-start.6
  63.8 0.8 copy-start.42
  63.9 0.8 copy-start.41
  63.9 0.8 copy-start.60
  63.9 0.8 copy-start.61
  63.9 0.8 copy-start.70
  67.3 0.7 copy-start.32
  67.3 0.7 copy-start.35
  67.3 0.7 copy-start.39
  67.4 0.7 copy-start.55
  69.4 9.6 %all-to-all-start.1 = ((f32[8,2,128]{2,1,0:T(2,128)}), f32[8,2,128]{2,1,0:T(2,128)S(1)}, u32[]{:S(2)}, u32[]{:S(2)}) async-start(f32[8,2,128]{2,1,0:T(2,128)} %broadcast_in_dim.53), calls=%async_computation.1 | async-start | bytes 16384 | tf_op jit(solution)/shard_map/all_to_all | solution.py:32
  81.1 3.3 %copy-start.15 = (f32[64,512]{1,0:T(8,128)S(1)}, f32[64,512]{1,0:T(8,128)}, u32[]{:S(2)}) copy-start(f32[64,512]{1,0:T(8,128)} %get-tuple-element.369) | copy-start | bytes 393220
  81.1 3.3 %copy-start.16 = (f32[64,512]{1,0:T(8,128)S(1)}, f32[64,512]{1,0:T(8,128)}, u32[]{:S(2)}) copy-start(f32[64,512]{1,0:T(8,128)} %get-tuple-element.370) | copy-start | bytes 393220
  81.3 0.7 copy-start.53
  81.3 0.7 copy-start.52
  82.8 0.7 copy-start.20
  86.0 0.7 copy-start.50
  86.0 0.7 copy-start.58
  87.5 24.7 %all-to-all-start.2 = ((f32[64,2,512]{2,1,0:T(2,128)}), f32[64,2,512]{2,1,0:T(2,128)S(1)}, u32[]{:S(2)}, u32[]{:S(2)}) async-start(f32[64,2,512]{2,1,0:T(2,128)} %broadcast_in_dim.55), calls=%async_computation.2 | async-start | bytes 524288 | tf_op jit(solution)/shard_map/all_to_all | solution.py:32
  100.2 0.7 copy-start.64
  100.9 0.9 copy-start.14
  112.6 0.9 copy-start.22
  115.9 0.7 copy-start.24
  117.8 0.7 copy-start.38
  119.2 0.9 copy-start.13
  120.1 0.7 copy-start.40
  120.1 0.7 copy-start.56
  120.1 0.7 copy-start.67
  120.1 0.7 copy-start.69
  148.4 27.2 %all-to-all-start.4 = ((f32[64,1,2080]{2,1,0:T(1,128)}), f32[64,1,2080]{2,1,0:T(1,128)S(1)}, u32[]{:S(2)}, u32[]{:S(2)}) async-start(f32[64,1,2080]{2,1,0:T(1,128)} %broadcast_in_dim.62), calls=%async_computation.4 | async-start | bytes 1114112 | tf_op jit(solution)/shard_map/all_to_all | solution.py:32
  155.5 18.5 %collective-permute-start.1 = (f32[3,512]{0,1:T(8,128)S(1)}, f32[3,512]{0,1:T(8,128)S(1)}, u32[]{:S(2)}, u32[]{:S(2)}) collective-permute-start(f32[3,512]{0,1:T(8,128)S(1)} %bitcast.365), channel_id=1, source_target_pairs={{8,0},{16,8},{24,16},{32,24},{40,32},{48,40},{56,48},{64,56},{72,6... | collective-permute-start | bytes 18440 | tf_op jit(solution)/shard_map/ppermute | solution.py:12
  158.9 15.2 %copy-start.27 = (f32[1,512]{1,0:T(1,128)S(1)}, f32[1,512]{1,0:T(1,128)}, u32[]{:S(2)}) copy-start(f32[1,512]{1,0:T(1,128)} %copy-done.25) | copy-start | bytes 6148
  158.9 15.2 %copy-start.30 = (f32[1,512]{1,0:T(1,128)S(1)}, f32[1,512]{1,0:T(1,128)}, u32[]{:S(2)}) copy-start(f32[1,512]{1,0:T(1,128)} %copy-done.28) | copy-start | bytes 6148
  158.9 15.2 %copy-start.33 = (f32[1,512]{1,0:T(1,128)S(1)}, f32[1,512]{1,0:T(1,128)}, u32[]{:S(2)}) copy-start(f32[1,512]{1,0:T(1,128)} %copy-done.31) | copy-start | bytes 6148
  158.9 15.1 %copy-start.36 = (f32[1,512]{1,0:T(1,128)S(1)}, f32[1,512]{1,0:T(1,128)}, u32[]{:S(2)}) copy-start(f32[1,512]{1,0:T(1,128)} %copy-done.34) | copy-start | bytes 6148
  (16 other events, 10.0 us)

commit v7 on v6

--- a/solution.py
+++ b/solution.py
@@ -50,7 +50,8 @@
     width = -(-flat.size // count)
     block = jnp.pad(flat, (0, width * count - flat.size)).reshape(count, width)
     mine = jnp.sum(lax.all_to_all(block, axis, 0, 0, tiled=True), axis=0)
-    return gather_all(mine, axis).reshape(-1)[: flat.size].reshape(value.shape)
+    spread = gather_all(mine.astype(jnp.bfloat16), axis).astype(jnp.float32)
+    return spread.reshape(-1)[: flat.size].reshape(value.shape)
 
 
 def linear_run(drive_re, drive_im, decay_rate, turn_rate, log_keep):

time: 182 us -> 182 us (level)
  waiting for transfers between devices: 27.2 us -> 22 us
  other arithmetic: 26.3 us -> 31.2 us
    ppermute x2, waiting for transfers between devices: 14.4 us -> 9.02 us  [from_behind(): return lax.ppermute(value, axis, pairs)]
    broadcast_in_dim x0 -> x1, other arithmetic: none -> 2.34 us  [gather_all(): spread = jnp.broadcast_to(value[None], (count,) + value.shape)]
    unnamed x157 -> x159, local copies, waits for them, and re-layouts: 16.4 us -> 17.7 us
where the time goes in v7:
time: 182 us; the launch traced here: 180 us
  local copies, waits for them, and re-layouts  50.9 us (28%)
  starting transfers between devices  46.4 us (25%)
  other arithmetic  31.2 us (17%)
  blocking collectives  24.5 us (13%)
  waiting for transfers between devices  22 us (12%)
  matrix products  2.45 us (1%)
  between operations  2.13 us (1%)
    all_to_all x4, starting transfers between devices, gather_all(): return lax.all_to_all(spread, axis, 0, 0, tiled=True)  39.3 us
    all_to_all x1, blocking collectives, tree_sum(): mine = jnp.sum(lax.all_to_all(block, axis, 0, 0, tiled=True), axis=0)  24.5 us
    unnamed x159, local copies, waits for them, and re-layouts  17.7 us
    all_to_all x4, waiting for transfers between devices, gather_all(): return lax.all_to_all(spread, axis, 0, 0, tiled=True)  13 us
    ppermute x2, waiting for transfers between devices, from_behind(): return lax.ppermute(value, axis, pairs)  9.02 us
    ppermute x2, starting transfers between devices, from_behind(): return lax.ppermute(value, axis, pairs)  7.12 us
    another operation x8, other arithmetic  4.95 us
  transfers between devices with their start and end apart: 6, of which 3 were waited for; matrix products, arithmetic and copies ran while one was open for 17% of the time, Pallas kernels for 0%

profile of v7, /device:TPU:56, one launch (start us, length us, event | category | flops | bytes accessed | tf_op | source)
XLA Modules:
  0.0 179.8 jit_solution(10497432209763719656)
XLA Ops:
  0.6 0.7 slice.264
  1.6 3.5 %collective-permute-start = (bf16[3,512]{0,1:T(8,128)(2,1)S(1)}, bf16[3,512]{0,1:T(8,128)(2,1)S(1)}, u32[]{:S(2)}, u32[]{:S(2)}) collective-permute-start(bf16[3,512]{0,1:T(8,128)(2,1)S(1)} %copy.272), channel_id=1, source_target_pairs={{0,8},{8,16},{16,24},{24,32},{32,40},{40,48},{48,56},{56,64},{64,7... | collective-permute-start | bytes 9224 | tf_op jit(solution)/shard_map/ppermute | solution.py:12
  8.3 0.7 broadcast_multiply_fusion.1
  9.0 2.5 %multiply_cosine_fusion.1 = (f32[64,512]{1,0:T(8,128)}, f32[64,512]{1,0:T(8,128)}, f32[64,512]{1,0:T(8,128)S(1)}, f32[64,512]{1,0:T(8,128)S(1)}, f32[64,512]{1,0...) fusion(f32[512]{0:T(512)S(1)} %get-tuple-element.423, ...), kind=kLoop, calls=%fused_computation.127 | loop fusion | flops 196608 | bytes 1317120 | tf_op jit(solution)/shard_map/cos | solution.py:95
  11.5 0.8 subtract_exponential_fusion.1
  12.3 0.7 fusion.68
  13.3 0.7 pad.61.clone
  14.0 1.1 fusion.20
  19.5 0.8 multiply_subtract_fusion.3
  20.3 0.9 broadcast_in_dim.51
  21.2 15.2 %all-to-all-start = ((f32[64,3,512]{2,1,0:T(4,128)}), f32[64,3,512]{2,1,0:T(4,128)}, u32[]{:S(2)}, u32[]{:S(2)}) async-start(f32[64,3,512]{2,1,0:T(4,128)} %broadcast_in_dim.51), calls=%async_computation | async-start | bytes 1048576 | tf_op jit(solution)/shard_map/all_to_all | solution.py:32
  36.7 0.7 mul.2106
  37.3 0.7 mul.2109
  38.0 0.7 sub.540
  38.7 1.1 sub.541
  39.8 0.9 copy.271
  40.7 0.9 copy.277
  41.6 0.9 copy.279
  42.7 0.9 copy.280
  43.8 0.9 copy.281
  44.9 0.9 copy.283
  46.1 0.7 reduce.4
  48.9 0.8 copy-done.2
  49.9 0.8 copy-done.5
  50.8 1.1 squeeze.82
  51.9 0.9 copy.282
  52.8 0.9 copy.284
  53.8 0.9 copy.276
  54.7 0.9 copy.278
  55.6 1.5 slice_reduce_fusion
  57.8 0.8 fusion.59
  58.8 1.1 slice.365
  60.3 1.1 gather_fusion
  61.4 0.7 copy-done.63
  64.8 2.6 %subtract_convert_fusion = (bf16[128,8,64]{0,2,1:T(8,128)(2,1)S(1)}, bf16[128,8,64]{0,2,1:T(8,128)(2,1)S(1)}) fusion(f32[128,8,64]{0,2,1:T(8,128)} %copy.284, f32[128,8,64]{0,2,1:T(8,128)} %copy.282, f32[128,8,64]{0,2,1:T(8,128)} %copy.278, f32[128,8,64]{0,2,1:T(8,128)S(1)} %copy-done.8, f32[128,8,64]{0,2,1:T(8,128)} %copy.276, ...), kind=kLoop, calls=%fused_computation.113 | loop fusion | flops 2293760 | bytes 2893312 | tf_op jit(solution)/shard_map/convert.7
  68.1 0.7 multiply_reduce_fusion.5
  69.4 4.3 %all-to-all-start.1 = ((f32[8,2,128]{2,1,0:T(2,128)}), f32[8,2,128]{2,1,0:T(2,128)S(1)}, u32[]{:S(2)}, u32[]{:S(2)}) async-start(f32[8,2,128]{2,1,0:T(2,128)} %broadcast_in_dim.53), calls=%async_computation.1 | async-start | bytes 16384 | tf_op jit(solution)/shard_map/all_to_all | solution.py:32
  73.7 0.7 copy-done.46
  76.1 2.9 %all-to-all-done.1 = f32[8,2,128]{2,1,0:T(2,128)S(1)} async-done(((f32[8,2,128]{2,1,0:T(2,128)}), f32[8,2,128]{2,1,0:T(2,128)S(1)}, u32[]{:S(2)}, u32[]{:S(2)}) %all-to-all-start.1) | async-done | bytes 8224 | tf_op jit(solution)/shard_map/all_to_all | solution.py:32
  81.4 0.7 copy-done.53
  82.1 0.8 add_multiply_fusion.2
  82.9 0.7 copy-done.20
  85.1 1.0 fusion.15
  86.1 0.7 copy-done.51
  86.8 0.8 broadcast_in_dim.55
  87.6 12.7 %all-to-all-start.2 = ((f32[64,2,512]{2,1,0:T(2,128)}), f32[64,2,512]{2,1,0:T(2,128)S(1)}, u32[]{:S(2)}, u32[]{:S(2)}) async-start(f32[64,2,512]{2,1,0:T(2,128)} %broadcast_in_dim.55), calls=%async_computation.2 | async-start | bytes 524288 | tf_op jit(solution)/shard_map/all_to_all | solution.py:32
  102.3 10.0 %all-to-all-done.2 = f32[64,2,512]{2,1,0:T(2,128)S(1)} async-done(((f32[64,2,512]{2,1,0:T(2,128)}), f32[64,2,512]{2,1,0:T(2,128)S(1)}, u32[]{:S(2)}, u32[]{:S(2)}) %all-to-all-start.2) | async-done | bytes 262176 | tf_op jit(solution)/shard_map/all_to_all | solution.py:32
  112.7 0.9 gather_fusion.1
  115.9 0.7 copy-done.24
  116.6 1.1 multiply_subtract_fusion
  120.8 0.7 multiply_reduce_fusion.3
  121.6 0.8 all_to_all.22
  122.4 24.5 %all_to_all.30 = f32[64,1,2080]{2,1,0:T(1,128)S(1)} all-to-all(f32[64,1,2080]{2,1,0:T(1,128)S(1)} %all_to_all.22), channel_id=1, replica_groups=mesh['z'=8,'y'=8,'chan'=8] {'z','y'}, dimensions={0} | all-to-all | bytes 1064960 | tf_op jit(solution)/shard_map/all_to_all | solution.py:52
  148.2 2.3 %reduce.24 = bf16[64,2080]{1,0:T(8,128)(2,1)S(1)} reduce(bf16[64,1,2080]{2,1,0:T(2,128)(2,1)S(1)} %broadcast_in_dim.62, bf16[]{:T(256)} %broadcast.683), dimensions={1}, to_apply=%broadcast_in_dim.62.reduce_sub_computation | reduce | bytes 532482 | tf_op jit(solution)/shard_map/broadcast_in_dim | solution.py:31
  150.6 1.0 reshape.2980
  151.6 7.1 %all-to-all-start.4 = ((bf16[64,2,1040]{2,1,0:T(2,128)(2,1)}), bf16[64,2,1040]{2,1,0:T(2,128)(2,1)S(1)}, u32[]{:S(2)}, u32[]{:S(2)}) async-start(bf16[64,2,1040]{2,1,0:T(2,128)(2,1)} %reshape.2980), calls=%async_computation.4 | async-start | bytes 589824 | tf_op jit(solution)/shard_map/all_to_all | solution.py:32
  158.7 3.6 %collective-permute-start.1 = (f32[3,512]{0,1:T(8,128)S(1)}, f32[3,512]{0,1:T(8,128)S(1)}, u32[]{:S(2)}, u32[]{:S(2)}) collective-permute-start(f32[3,512]{0,1:T(8,128)S(1)} %bitcast.365), channel_id=1, source_target_pairs={{8,0},{16,8},{24,16},{32,24},{40,32},{48,40},{56,48},{64,56},{72,6... | collective-permute-start | bytes 18440 | tf_op jit(solution)/shard_map/ppermute | solution.py:12
  162.4 0.8 copy.309
  163.1 9.0 %collective-permute-done.1 = f32[3,512]{0,1:T(8,128)S(1)} collective-permute-done((f32[3,512]{0,1:T(8,128)S(1)}, f32[3,512]{0,1:T(8,128)S(1)}, u32[]{:S(2)}, u32[]{:S(2)}) %collective-permute-start.1) | collective-permute-done | bytes 6176 | tf_op jit(solution)/shard_map/ppermute | solution.py:12
  172.2 0.7 fusion.30
  172.9 0.8 copy.310
  174.0 1.6 convert_reduce_fusion
  175.6 1.7 reduce.13
  177.8 0.8 fusion.82
  (321 shorter events, 33.3 us)
Async XLA Ops:
  0.6 66.7 %copy-start = (bf16[8,64,128]{2,1,0:T(8,128)(2,1)S(1)}, bf16[8,64,128]{2,1,0:T(8,128)(2,1)}, u32[]{:S(2)}) copy-start(bf16[8,64,128]{2,1,0:T(8,128)(2,1)} %param.25) | copy-start | bytes 393220
  1.6 3.5 %copy-start.72 = (f32[128]{0:T(128)S(1)}, f32[128]{0:T(128)}, u32[]{:S(2)}) copy-start(f32[128]{0:T(128)} %param.28) | copy-start | bytes 1540
  1.6 13.5 %collective-permute-start = (bf16[3,512]{0,1:T(8,128)(2,1)S(1)}, bf16[3,512]{0,1:T(8,128)(2,1)S(1)}, u32[]{:S(2)}, u32[]{:S(2)}) collective-permute-start(bf16[3,512]{0,1:T(8,128)(2,1)S(1)} %copy.272), channel_id=1, source_target_pairs={{0,8},{8,16},{16,24},{24,32},{32,40},{40,48},{48,56},{56,64},{64,7... | collective-permute-start | bytes 9224 | tf_op jit(solution)/shard_map/ppermute | solution.py:12
  7.5 0.7 copy-start.23
  7.6 3.9 %copy-start.45 = (f32[2,64]{1,0:T(2,128)}, f32[2,64]{1,0:T(2,128)S(1)}, u32[]{:S(2)}) copy-start(f32[2,64]{1,0:T(2,128)S(1)} %reduce.8) | copy-start | bytes 1540
  7.6 0.7 copy-start.19
  9.0 8.6 %copy-start.37 = (f32[512]{0:T(512)}, f32[512]{0:T(512)S(1)}, u32[]{:S(2)}) copy-start(f32[512]{0:T(512)S(1)} %get-tuple-element.403) | copy-start | bytes 6148
  11.5 1.5 copy-start.17
  12.3 0.7 copy-start.54
  13.0 2.2 %copy-start.25 = (f32[1,512]{1,0:T(1,128)}, f32[1,512]{1,0:T(1,128)S(1)}, u32[]{:S(2)}) copy-start(f32[1,512]{1,0:T(1,128)S(1)} %get-tuple-element.367) | copy-start | bytes 6148
  13.0 2.2 %copy-start.28 = (f32[1,512]{1,0:T(1,128)}, f32[1,512]{1,0:T(1,128)S(1)}, u32[]{:S(2)}) copy-start(f32[1,512]{1,0:T(1,128)S(1)} %get-tuple-element.368) | copy-start | bytes 6148
  13.0 2.2 %copy-start.31 = (f32[1,512]{1,0:T(1,128)}, f32[1,512]{1,0:T(1,128)S(1)}, u32[]{:S(2)}) copy-start(f32[1,512]{1,0:T(1,128)S(1)} %get-tuple-element.369) | copy-start | bytes 6148
  13.1 2.2 %copy-start.34 = (f32[1,512]{1,0:T(1,128)}, f32[1,512]{1,0:T(1,128)S(1)}, u32[]{:S(2)}) copy-start(f32[1,512]{1,0:T(1,128)S(1)} %get-tuple-element.370) | copy-start | bytes 6148
  13.3 0.7 copy-start.59
  15.3 0.9 copy-start.12
  18.2 0.7 copy-start.3
  18.3 0.8 copy-start.4
  18.8 0.7 copy-start.1
  21.2 34.4 %all-to-all-start = ((f32[64,3,512]{2,1,0:T(4,128)}), f32[64,3,512]{2,1,0:T(4,128)}, u32[]{:S(2)}, u32[]{:S(2)}) async-start(f32[64,3,512]{2,1,0:T(4,128)} %broadcast_in_dim.51), calls=%async_computation | async-start | bytes 1048576 | tf_op jit(solution)/shard_map/all_to_all | solution.py:32
  45.8 1.0 copy-start.18
  48.8 0.9 copy-start.2
  49.7 0.9 copy-start.5
  54.7 2.4 %copy-start.49 = (f32[512]{0:T(512)S(1)}, f32[512]{0:T(512)}, u32[]{:S(2)}) copy-start(f32[512]{0:T(512)} %get-tuple-element.424) | copy-start | bytes 6148
  57.1 0.7 copy-start.47
  60.3 1.1 copy-start.21
  61.4 0.7 copy-start.63
  63.0 1.0 copy-start.11
  63.3 1.0 copy-start.10
  63.4 1.0 copy-start.9
  63.5 1.0 copy-start.8
  63.6 1.0 copy-start.7
  63.7 1.0 copy-start.6
  63.9 0.8 copy-start.42
  64.0 0.8 copy-start.41
  64.0 0.8 copy-start.60
  64.0 0.8 copy-start.61
  64.0 0.8 copy-start.70
  67.4 0.7 copy-start.32
  67.4 0.7 copy-start.35
  67.4 0.7 copy-start.39
  67.4 0.7 copy-start.55
  69.4 9.6 %all-to-all-start.1 = ((f32[8,2,128]{2,1,0:T(2,128)}), f32[8,2,128]{2,1,0:T(2,128)S(1)}, u32[]{:S(2)}, u32[]{:S(2)}) async-start(f32[8,2,128]{2,1,0:T(2,128)} %broadcast_in_dim.53), calls=%async_computation.1 | async-start | bytes 16384 | tf_op jit(solution)/shard_map/all_to_all | solution.py:32
  81.2 3.3 %copy-start.15 = (f32[64,512]{1,0:T(8,128)S(1)}, f32[64,512]{1,0:T(8,128)}, u32[]{:S(2)}) copy-start(f32[64,512]{1,0:T(8,128)} %get-tuple-element.374) | copy-start | bytes 393220
  81.3 3.3 %copy-start.16 = (f32[64,512]{1,0:T(8,128)S(1)}, f32[64,512]{1,0:T(8,128)}, u32[]{:S(2)}) copy-start(f32[64,512]{1,0:T(8,128)} %get-tuple-element.375) | copy-start | bytes 393220
  81.4 0.7 copy-start.53
  81.4 0.7 copy-start.52
  82.9 0.7 copy-start.20
  86.1 0.7 copy-start.51
  86.1 0.7 copy-start.50
  87.6 24.7 %all-to-all-start.2 = ((f32[64,2,512]{2,1,0:T(2,128)}), f32[64,2,512]{2,1,0:T(2,128)S(1)}, u32[]{:S(2)}, u32[]{:S(2)}) async-start(f32[64,2,512]{2,1,0:T(2,128)} %broadcast_in_dim.55), calls=%async_computation.2 | async-start | bytes 524288 | tf_op jit(solution)/shard_map/all_to_all | solution.py:32
  100.9 0.9 copy-start.14
  112.7 0.9 copy-start.22
  115.9 0.7 copy-start.24
  119.2 0.9 copy-start.13
  120.1 0.7 copy-start.40
  120.1 0.7 copy-start.56
  120.1 0.7 copy-start.67
  120.1 0.7 copy-start.69
  151.6 22.1 %all-to-all-start.4 = ((bf16[64,2,1040]{2,1,0:T(2,128)(2,1)}), bf16[64,2,1040]{2,1,0:T(2,128)(2,1)S(1)}, u32[]{:S(2)}, u32[]{:S(2)}) async-start(bf16[64,2,1040]{2,1,0:T(2,128)(2,1)} %reshape.2980), calls=%async_computation.4 | async-start | bytes 589824 | tf_op jit(solution)/shard_map/all_to_all | solution.py:32
  158.7 13.5 %collective-permute-start.1 = (f32[3,512]{0,1:T(8,128)S(1)}, f32[3,512]{0,1:T(8,128)S(1)}, u32[]{:S(2)}, u32[]{:S(2)}) collective-permute-start(f32[3,512]{0,1:T(8,128)S(1)} %bitcast.365), channel_id=1, source_target_pairs={{8,0},{16,8},{24,16},{32,24},{40,32},{48,40},{56,48},{64,56},{72,6... | collective-permute-start | bytes 18440 | tf_op jit(solution)/shard_map/ppermute | solution.py:12
  162.3 9.8 %copy-start.27 = (f32[1,512]{1,0:T(1,128)S(1)}, f32[1,512]{1,0:T(1,128)}, u32[]{:S(2)}) copy-start(f32[1,512]{1,0:T(1,128)} %copy-done.25) | copy-start | bytes 6148
  162.3 9.8 %copy-start.30 = (f32[1,512]{1,0:T(1,128)S(1)}, f32[1,512]{1,0:T(1,128)}, u32[]{:S(2)}) copy-start(f32[1,512]{1,0:T(1,128)} %copy-done.28) | copy-start | bytes 6148
  162.3 9.8 %copy-start.33 = (f32[1,512]{1,0:T(1,128)S(1)}, f32[1,512]{1,0:T(1,128)}, u32[]{:S(2)}) copy-start(f32[1,512]{1,0:T(1,128)} %copy-done.31) | copy-start | bytes 6148
  162.4 9.8 %copy-start.36 = (f32[1,512]{1,0:T(1,128)S(1)}, f32[1,512]{1,0:T(1,128)}, u32[]{:S(2)}) copy-start(f32[1,512]{1,0:T(1,128)} %copy-done.34) | copy-start | bytes 6148
  (16 other events, 10.0 us)

commit v8 on v6

--- a/solution.py
+++ b/solution.py
@@ -165,6 +165,7 @@
         ],
         axis=2,
     ).astype(jnp.bfloat16)
+    state_bf = lax.optimization_barrier(state_bf)
     mixed = jnp.einsum(
         "thk,hck->thc", state_bf, out_proj, preferred_element_type=jnp.float32
     ).reshape(seq_len, local_width)
@@ -210,6 +211,7 @@
         ],
         axis=2,
     ).astype(jnp.bfloat16)
+    drive_grad = lax.optimization_barrier(drive_grad)
     in_grad = jnp.einsum("thc,thk->hck", by_head, drive_grad, preferred_element_type=jnp.float32)
     input_grad = jnp.einsum(
         "thk,hck->thc", drive_grad, in_proj, preferred_element_type=jnp.float32

time: 182 us -> 199 us (1.093)
  local copies, waits for them, and re-layouts: 50.4 us -> 59.8 us
  other arithmetic: 26.3 us -> 33.7 us
    another operation x8, other arithmetic: 4.99 us -> 9.84 us
    unnamed x157 -> x163, local copies, waits for them, and re-layouts: 16.4 us -> 19.4 us
    sub x5 -> x4, local copies, waits for them, and re-layouts: 3.42 us -> 0.83 us  [linear_run(): keep_cum - offsets[None, :, None] * decay_rate[None, None, :]]
    mul x3 -> x2, local copies, waits for them, and re-layouts: 1.07 us -> 3.54 us  [linear_run(): lift_im = lift * jnp.sin(ahead[:, None] * turn_rate[None, :])]
  transfers between devices with their start and end apart: 6 -> 6, of which waited for: 3 -> 3; matrix products, arithmetic and copies ran while one was open for 17% -> 19% of each run, Pallas kernels for 0% -> 0%
where the time goes in v8:
time: 199 us; the launch traced here: 196 us
  local copies, waits for them, and re-layouts  59.8 us (30%)
  starting transfers between devices  46.2 us (23%)
  other arithmetic  33.7 us (17%)
  waiting for transfers between devices  27.3 us (14%)
  blocking collectives  24.6 us (12%)
  matrix products  2.29 us (1%)
  between operations  2.13 us (1%)
    all_to_all x4, starting transfers between devices, gather_all(): return lax.all_to_all(spread, axis, 0, 0, tiled=True)  39.3 us
    all_to_all x1, blocking collectives, tree_sum(): mine = jnp.sum(lax.all_to_all(block, axis, 0, 0, tiled=True), axis=0)  24.6 us
    unnamed x163, local copies, waits for them, and re-layouts  19.4 us
    ppermute x2, waiting for transfers between devices, from_behind(): return lax.ppermute(value, axis, pairs)  14.3 us
    all_to_all x4, waiting for transfers between devices, gather_all(): return lax.all_to_all(spread, axis, 0, 0, tiled=True)  13 us
    another operation x8, other arithmetic  9.84 us
    ppermute x2, starting transfers between devices, from_behind(): return lax.ppermute(value, axis, pairs)  6.85 us
  transfers between devices with their start and end apart: 6, of which 3 were waited for; matrix products, arithmetic and copies ran while one was open for 19% of the time, Pallas kernels for 0%

profile of v8, /device:TPU:56, one launch (start us, length us, event | category | flops | bytes accessed | tf_op | source)
XLA Modules:
  0.0 196.1 jit_solution(12123363634060997540)
XLA Ops:
  0.6 0.7 slice.263
  1.6 3.5 %collective-permute-start = (bf16[3,512]{0,1:T(8,128)(2,1)S(1)}, bf16[3,512]{0,1:T(8,128)(2,1)S(1)}, u32[]{:S(2)}, u32[]{:S(2)}) collective-permute-start(bf16[3,512]{0,1:T(8,128)(2,1)S(1)} %copy.168), channel_id=1, source_target_pairs={{0,8},{8,16},{16,24},{24,32},{32,40},{40,48},{48,56},{56,64},{64,7... | collective-permute-start | bytes 9224 | tf_op jit(solution)/shard_map/ppermute | solution.py:12
  5.1 1.1 log_bitcast_fusion
  6.9 0.7 fusion.77
  8.9 0.6 broadcast_multiply_fusion.1
  9.5 2.6 %multiply_cosine_fusion.1 = (f32[64,512]{1,0:T(8,128)}, f32[64,512]{1,0:T(8,128)}, f32[64,512]{1,0:T(8,128)}, f32[64,512]{1,0:T(8,128)}, f32[64,512]{1,0:T(8,128...) fusion(f32[512]{0:T(512)S(1)} %get-tuple-element.418, ...), kind=kLoop, calls=%fused_computation.130 | loop fusion | flops 196608 | bytes 1317120 | tf_op jit(solution)/shard_map/cos | solution.py:94
  12.2 0.8 subtract_exponential_fusion.4
  13.0 0.7 fusion.68
  15.2 1.2 pad.61.clone
  16.3 1.1 fusion.22
  21.2 0.7 copy-done.55
  23.8 0.8 multiply_subtract_fusion.3
  25.3 0.9 broadcast_in_dim.51
  26.1 15.2 %all-to-all-start = ((f32[64,3,512]{2,1,0:T(4,128)}), f32[64,3,512]{2,1,0:T(4,128)}, u32[]{:S(2)}, u32[]{:S(2)}) async-start(f32[64,3,512]{2,1,0:T(4,128)} %broadcast_in_dim.51), calls=%async_computation | async-start | bytes 1048576 | tf_op jit(solution)/shard_map/all_to_all | solution.py:32
  41.6 0.7 mul.2106
  42.3 0.7 mul.2109
  43.3 0.7 mul.2081
  44.0 1.1 mul.2082
  45.1 1.6 mul.2099
  46.8 1.9 mul.2100
  49.3 0.7 copy.172
  50.0 1.6 reduce-window.16
  51.6 1.5 reduce.4
  53.1 1.7 copy.176
  56.6 1.9 mul.2097
  58.4 1.9 mul.2103
  60.3 1.9 squeeze.81
  62.2 1.9 squeeze.82
  64.1 1.5 slice_reduce_fusion
  65.6 0.7 copy-done.51
  66.2 1.4 fusion.59
  68.0 1.1 slice.364
  69.1 1.1 fusion
  70.2 2.8 %gather_fusion = f32[64,4,512]{2,1,0:T(4,128)} fusion(f32[64,4,512]{2,1,0:T(4,128)} %fusion, s32[1024]{0:T(1024)} %pad_clamp_fusion.1), kind=kCustom, calls=%fused_computation.clone | custom fusion | bytes 1048832 | tf_op jit(solution)/shard_map/jit(_take)/gather | solution.py:19
  73.7 1.2 broadcast_select_fusion.5
  77.0 1.3 mul.2180
  78.4 1.3 mul.2186
  79.7 4.7 %subtract_convert_fusion = (bf16[128,8,64]{2,1,0:T(8,128)(2,1)S(1)}, bf16[128,8,64]{2,1,0:T(8,128)(2,1)S(1)}) fusion(f32[128,8,64]{2,1,0:T(8,128)} %mul.2103, f32[128,8,64]{2,1,0:T(8,128)} %mul.2097, f32[128,8,64]{2,1,0:T(8,128)} %squeeze.82, f32[128,8,64]{2,1,0:T(8,128)S(1)} %mul.2075, f32[128,8,64]{2,1,0:T(8,128)} %squeeze.81, ...), kind=kLoop, calls=%fused_computation.42 | loop fusion | flops 2293760 | bytes 2893312 | tf_op jit(solution)/shard_map/convert.4
  85.5 0.7 multiply_reduce_fusion.5
  86.8 4.3 %all-to-all-start.1 = ((f32[8,2,128]{2,1,0:T(2,128)}), f32[8,2,128]{2,1,0:T(2,128)S(1)}, u32[]{:S(2)}, u32[]{:S(2)}) async-start(f32[8,2,128]{2,1,0:T(2,128)} %broadcast_in_dim.53), calls=%async_computation.1 | async-start | bytes 16384 | tf_op jit(solution)/shard_map/all_to_all | solution.py:32
  93.5 2.9 %all-to-all-done.1 = f32[8,2,128]{2,1,0:T(2,128)S(1)} async-done(((f32[8,2,128]{2,1,0:T(2,128)}), f32[8,2,128]{2,1,0:T(2,128)S(1)}, u32[]{:S(2)}, u32[]{:S(2)}) %all-to-all-start.1) | async-done | bytes 8224 | tf_op jit(solution)/shard_map/all_to_all | solution.py:32
  98.8 0.7 copy-done.57
  99.5 0.8 add_multiply_fusion.2
  100.3 0.6 copy-done.20
  103.0 0.8 broadcast_in_dim.55
  103.7 12.7 %all-to-all-start.2 = ((f32[64,2,512]{2,1,0:T(2,128)}), f32[64,2,512]{2,1,0:T(2,128)S(1)}, u32[]{:S(2)}, u32[]{:S(2)}) async-start(f32[64,2,512]{2,1,0:T(2,128)} %broadcast_in_dim.55), calls=%async_computation.2 | async-start | bytes 524288 | tf_op jit(solution)/shard_map/all_to_all | solution.py:32
  116.5 0.7 copy-done.66
  118.4 10.0 %all-to-all-done.2 = f32[64,2,512]{2,1,0:T(2,128)S(1)} async-done(((f32[64,2,512]{2,1,0:T(2,128)}), f32[64,2,512]{2,1,0:T(2,128)S(1)}, u32[]{:S(2)}, u32[]{:S(2)}) %all-to-all-start.2) | async-done | bytes 262176 | tf_op jit(solution)/shard_map/all_to_all | solution.py:32
  128.8 0.9 gather_fusion.1
  132.1 0.7 copy-done.27
  132.8 1.1 multiply_subtract_fusion
  135.0 0.9 copy-done.6
  137.5 0.7 multiply_reduce_fusion.3
  138.3 0.8 all_to_all.22
  139.1 24.6 %all_to_all.30 = f32[64,1,2080]{2,1,0:T(1,128)S(1)} all-to-all(f32[64,1,2080]{2,1,0:T(1,128)S(1)} %all_to_all.22), channel_id=1, replica_groups=mesh['z'=8,'y'=8,'chan'=8] {'z','y'}, dimensions={0} | all-to-all | bytes 1064960 | tf_op jit(solution)/shard_map/all_to_all | solution.py:52
  164.0 1.1 broadcast_in_dim.62
  165.1 7.1 %all-to-all-start.4 = ((f32[64,1,2080]{2,1,0:T(1,128)}), f32[64,1,2080]{2,1,0:T(1,128)S(1)}, u32[]{:S(2)}, u32[]{:S(2)}) async-start(f32[64,1,2080]{2,1,0:T(1,128)} %broadcast_in_dim.62), calls=%async_computation.4 | async-start | bytes 1114112 | tf_op jit(solution)/shard_map/all_to_all | solution.py:32
  172.3 3.4 %collective-permute-start.1 = (f32[3,512]{0,1:T(8,128)S(1)}, f32[3,512]{0,1:T(8,128)S(1)}, u32[]{:S(2)}, u32[]{:S(2)}) collective-permute-start(f32[3,512]{0,1:T(8,128)S(1)} %bitcast.367), channel_id=1, source_target_pairs={{8,0},{16,8},{24,16},{32,24},{40,32},{48,40},{56,48},{64,56},{72,6... | collective-permute-start | bytes 18440 | tf_op jit(solution)/shard_map/ppermute | solution.py:12
  175.7 0.8 copy.190
  176.4 14.3 %collective-permute-done.1 = f32[3,512]{0,1:T(8,128)S(1)} collective-permute-done((f32[3,512]{0,1:T(8,128)S(1)}, f32[3,512]{0,1:T(8,128)S(1)}, u32[]{:S(2)}, u32[]{:S(2)}) %collective-permute-start.1) | collective-permute-done | bytes 6176 | tf_op jit(solution)/shard_map/ppermute | solution.py:12
  190.8 0.7 fusion.32
  191.5 0.8 copy.191
  192.3 1.3 reduce.12
  194.6 0.8 fusion.78
  (312 shorter events, 33.0 us)
Async XLA Ops:
  0.6 83.9 %copy-start = (bf16[8,64,128]{2,1,0:T(8,128)(2,1)S(1)}, bf16[8,64,128]{2,1,0:T(8,128)(2,1)}, u32[]{:S(2)}) copy-start(bf16[8,64,128]{2,1,0:T(8,128)(2,1)} %param.25) | copy-start | bytes 393220
  1.6 3.5 %copy-start.75 = (f32[128]{0:T(128)S(1)}, f32[128]{0:T(128)}, u32[]{:S(2)}) copy-start(f32[128]{0:T(128)} %param.28) | copy-start | bytes 1540
  1.6 15.8 %collective-permute-start = (bf16[3,512]{0,1:T(8,128)(2,1)S(1)}, bf16[3,512]{0,1:T(8,128)(2,1)S(1)}, u32[]{:S(2)}, u32[]{:S(2)}) collective-permute-start(bf16[3,512]{0,1:T(8,128)(2,1)S(1)} %copy.168), channel_id=1, source_target_pairs={{0,8},{8,16},{16,24},{24,32},{32,40},{40,48},{48,56},{56,64},{64,7... | collective-permute-start | bytes 9224 | tf_op jit(solution)/shard_map/ppermute | solution.py:12
  8.0 5.9 %copy-start.48 = (f32[2,64]{1,0:T(2,128)}, f32[2,64]{1,0:T(2,128)S(1)}, u32[]{:S(2)}) copy-start(f32[2,64]{1,0:T(2,128)S(1)} %reduce.1) | copy-start | bytes 1540
  8.1 0.7 copy-start.25
  8.2 4.0 %copy-start.46 = (f32[2,64]{1,0:T(2,128)}, f32[2,64]{1,0:T(2,128)S(1)}, u32[]{:S(2)}) copy-start(f32[2,64]{1,0:T(2,128)S(1)} %reduce.8) | copy-start | bytes 1540
  8.2 0.7 copy-start.19
  12.2 4.1 %copy-start.4 = (f32[64,512]{1,0:T(8,128)}, f32[64,512]{1,0:T(8,128)S(1)}, u32[]{:S(2)}) copy-start(f32[64,512]{1,0:T(8,128)S(1)} %get-tuple-element.405) | copy-start | bytes 393220
  12.2 1.5 copy-start.18
  13.0 0.7 copy-start.58
  13.7 3.8 %copy-start.28 = (f32[1,512]{1,0:T(1,128)}, f32[1,512]{1,0:T(1,128)S(1)}, u32[]{:S(2)}) copy-start(f32[1,512]{1,0:T(1,128)S(1)} %get-tuple-element.362) | copy-start | bytes 6148
  13.7 3.8 %copy-start.31 = (f32[1,512]{1,0:T(1,128)}, f32[1,512]{1,0:T(1,128)S(1)}, u32[]{:S(2)}) copy-start(f32[1,512]{1,0:T(1,128)S(1)} %get-tuple-element.363) | copy-start | bytes 6148
  13.7 3.8 %copy-start.34 = (f32[1,512]{1,0:T(1,128)}, f32[1,512]{1,0:T(1,128)S(1)}, u32[]{:S(2)}) copy-start(f32[1,512]{1,0:T(1,128)S(1)} %get-tuple-element.364) | copy-start | bytes 6148
  13.7 3.8 %copy-start.37 = (f32[1,512]{1,0:T(1,128)}, f32[1,512]{1,0:T(1,128)S(1)}, u32[]{:S(2)}) copy-start(f32[1,512]{1,0:T(1,128)S(1)} %get-tuple-element.365) | copy-start | bytes 6148
  14.0 2.3 %copy-start.63 = (f32[128]{0:T(128)}, f32[128]{0:T(128)S(1)}, u32[]{:S(2)}) copy-start(f32[128]{0:T(128)S(1)} %sub.538) | copy-start | bytes 1540
  17.6 0.9 copy-start.13
  21.2 1.9 copy-start.11
  21.2 1.9 copy-start.12
  21.2 0.7 copy-start.55
  21.2 0.7 copy-start.54
  22.0 0.7 copy-start.21
  22.0 0.7 copy-start.22
  23.0 0.7 copy-start.9
  23.1 0.8 copy-start.10
  26.1 38.0 %all-to-all-start = ((f32[64,3,512]{2,1,0:T(4,128)}), f32[64,3,512]{2,1,0:T(4,128)}, u32[]{:S(2)}, u32[]{:S(2)}) async-start(f32[64,3,512]{2,1,0:T(4,128)} %broadcast_in_dim.51), calls=%async_computation | async-start | bytes 1048576 | tf_op jit(solution)/shard_map/all_to_all | solution.py:32
  41.6 0.7 copy-start.26
  65.6 0.7 copy-start.50
  67.8 1.3 copy-start.7
  70.2 2.8 %copy-start.23 = (f32[4,512]{1,0:T(4,128)S(1)}, f32[4,512]{1,0:T(4,128)}, u32[]{:S(2)}) copy-start(f32[4,512]{1,0:T(4,128)} %constant.81.clone.1) | copy-start | bytes 24580
  77.0 2.7 %copy-start.45 = (f32[8,64]{1,0:T(8,128)S(1)}, f32[8,64]{1,0:T(8,128)}, u32[]{:S(2)}) copy-start(f32[8,64]{1,0:T(8,128)} %mul.2109) | copy-start | bytes 6148
  78.4 1.3 copy-start.44
  84.5 0.9 copy-start.1
  84.5 0.9 copy-start.29
  84.6 0.9 copy-start.32
  84.6 0.9 copy-start.35
  84.6 0.9 copy-start.38
  84.6 0.9 copy-start.42
  84.6 0.9 copy-start.59
  85.5 6.9 %copy-start.3 = (f32[64,512]{1,0:T(8,128)S(1)}, f32[64,512]{1,0:T(8,128)}, u32[]{:S(2)}) copy-start(f32[64,512]{1,0:T(8,128)} %get-tuple-element.389) | copy-start | bytes 393220
  85.5 7.4 %copy-start.2 = (f32[64,512]{1,0:T(8,128)S(1)}, f32[64,512]{1,0:T(8,128)}, u32[]{:S(2)}) copy-start(f32[64,512]{1,0:T(8,128)} %get-tuple-element.388) | copy-start | bytes 393220
  86.8 9.6 %all-to-all-start.1 = ((f32[8,2,128]{2,1,0:T(2,128)}), f32[8,2,128]{2,1,0:T(2,128)S(1)}, u32[]{:S(2)}, u32[]{:S(2)}) async-start(f32[8,2,128]{2,1,0:T(2,128)} %broadcast_in_dim.53), calls=%async_computation.1 | async-start | bytes 16384 | tf_op jit(solution)/shard_map/all_to_all | solution.py:32
  98.7 2.7 %copy-start.16 = (f32[64,512]{1,0:T(8,128)S(1)}, f32[64,512]{1,0:T(8,128)}, u32[]{:S(2)}) copy-start(f32[64,512]{1,0:T(8,128)} %get-tuple-element.369) | copy-start | bytes 393220
  98.7 2.7 %copy-start.17 = (f32[64,512]{1,0:T(8,128)S(1)}, f32[64,512]{1,0:T(8,128)}, u32[]{:S(2)}) copy-start(f32[64,512]{1,0:T(8,128)} %get-tuple-element.370) | copy-start | bytes 393220
  98.8 0.7 copy-start.57
  98.8 0.7 copy-start.56
  100.3 0.7 copy-start.20
  102.2 0.7 copy-start.52
  103.7 24.7 %all-to-all-start.2 = ((f32[64,2,512]{2,1,0:T(2,128)}), f32[64,2,512]{2,1,0:T(2,128)S(1)}, u32[]{:S(2)}, u32[]{:S(2)}) async-start(f32[64,2,512]{2,1,0:T(2,128)} %broadcast_in_dim.55), calls=%async_computation.2 | async-start | bytes 524288 | tf_op jit(solution)/shard_map/all_to_all | solution.py:32
  117.1 0.9 copy-start.15
  118.2 10.2 %copy-start.8 = (f32[64,1,512]{2,1,0:T(1,128)S(1)}, f32[64,1,512]{2,1,0:T(1,128)}, u32[]{:S(2)}) copy-start(f32[64,1,512]{2,1,0:T(1,128)} %copy-done.7) | copy-start | bytes 393220
  128.8 0.9 copy-start.24
  132.1 0.7 copy-start.27
  135.0 0.9 copy-start.6
  135.9 0.9 copy-start.14
  136.8 0.7 copy-start.43
  136.8 0.7 copy-start.60
  136.8 0.7 copy-start.70
  136.8 0.7 copy-start.72
  165.1 27.2 %all-to-all-start.4 = ((f32[64,1,2080]{2,1,0:T(1,128)}), f32[64,1,2080]{2,1,0:T(1,128)S(1)}, u32[]{:S(2)}, u32[]{:S(2)}) async-start(f32[64,1,2080]{2,1,0:T(1,128)} %broadcast_in_dim.62), calls=%async_computation.4 | async-start | bytes 1114112 | tf_op jit(solution)/shard_map/all_to_all | solution.py:32
  172.3 18.5 %collective-permute-start.1 = (f32[3,512]{0,1:T(8,128)S(1)}, f32[3,512]{0,1:T(8,128)S(1)}, u32[]{:S(2)}, u32[]{:S(2)}) collective-permute-start(f32[3,512]{0,1:T(8,128)S(1)} %bitcast.367), channel_id=1, source_target_pairs={{8,0},{16,8},{24,16},{32,24},{40,32},{48,40},{56,48},{64,56},{72,6... | collective-permute-start | bytes 18440 | tf_op jit(solution)/shard_map/ppermute | solution.py:12
  175.6 15.1 %copy-start.30 = (f32[1,512]{1,0:T(1,128)S(1)}, f32[1,512]{1,0:T(1,128)}, u32[]{:S(2)}) copy-start(f32[1,512]{1,0:T(1,128)} %copy-done.28) | copy-start | bytes 6148
  175.6 15.1 %copy-start.33 = (f32[1,512]{1,0:T(1,128)S(1)}, f32[1,512]{1,0:T(1,128)}, u32[]{:S(2)}) copy-start(f32[1,512]{1,0:T(1,128)} %copy-done.31) | copy-start | bytes 6148
  175.7 15.1 %copy-start.36 = (f32[1,512]{1,0:T(1,128)S(1)}, f32[1,512]{1,0:T(1,128)}, u32[]{:S(2)}) copy-start(f32[1,512]{1,0:T(1,128)} %copy-done.34) | copy-start | bytes 6148
  175.7 15.1 %copy-start.39 = (f32[1,512]{1,0:T(1,128)S(1)}, f32[1,512]{1,0:T(1,128)}, u32[]{:S(2)}) copy-start(f32[1,512]{1,0:T(1,128)} %copy-done.37) | copy-start | bytes 6148
  (19 other events, 11.9 us)

commit v9 on v5

--- a/solution.py
+++ b/solution.py
@@ -32,17 +32,32 @@
     return lax.all_to_all(spread, axis, 0, 0, tiled=True)
 
 
+def fold(stack, where_at, combine, unit):
+    total = unit
+    prefix = unit
+    for j in range(stack.shape[0]):
+        prefix = jnp.where(j == where_at, total, prefix)
+        total = jnp.stack(combine(tuple(total), tuple(stack[j])))
+    return prefix, total
+
+
 def carried_in(part, axis, combine, identity, reverse):
+    outer, inner = axis
     packed = jnp.stack(part)
-    unit = jnp.stack([jnp.zeros_like(a) + jnp.asarray(e, a.dtype) for a, e in zip(part, identity)])
-    place = lax.axis_index(axis)
-    every = gather_all(packed, axis)
-    order = list(range(lax.axis_size(axis)))
+    unit = jnp.stack([jnp.zeros_like(part[0]) + e for e in identity])
+    row_place = lax.axis_index(inner)
+    col_place = lax.axis_index(outer)
+    row = gather_all(packed, inner)
     if reverse:
-        order = order[::-1]
-        place = lax.axis_size(axis) - 1 - place
-    before = tree_fold(every, order, place, combine, unit)
-    return tuple(before)
+        row = row[::-1]
+        row_place = lax.axis_size(inner) - 1 - row_place
+        col_place = lax.axis_size(outer) - 1 - col_place
+    within, row_total = fold(row, row_place, combine, unit)
+    rows = gather_all(row_total, outer)
+    if reverse:
+        rows = rows[::-1]
+    before, _ = fold(rows, col_place, combine, unit)
+    return combine(tuple(before), tuple(within))
 
 
 def tree_sum(value, axis):
@@ -147,14 +162,8 @@
     total_mag = jnp.exp(keep_total - seq_len * log_rate)
     total_re = total_mag * jnp.cos(seq_len * rotation)
     total_im = total_mag * jnp.sin(seq_len * rotation)
-    unit_ones = jnp.ones((num_cols,), jnp.float32)
-    zeros_col = jnp.zeros((num_cols,), jnp.float32)
     chained = carried_in(
-        (total_re, total_im, state_re[-1], state_im[-1]),
-        SEQ,
-        carry_combine,
-        (unit_ones, zeros_col, zeros_col, zeros_col),
-        False,
+        (total_re, total_im, state_re[-1], state_im[-1]), SEQ, carry_combine, (1.0, 0.0, 0.0, 0.0), False
     )
     enter_re, enter_im = (chained[2], chained[3])
     positions = jnp.arange(seq_len, dtype=jnp.float32)
@@ -198,11 +207,7 @@
     first_re = first_mag * (cos_turn * adj_re[-1] + sin_turn * adj_im[-1])
     first_im = first_mag * (cos_turn * adj_im[-1] - sin_turn * adj_re[-1])
     back_chained = carried_in(
-        (total_re, -total_im, first_re, first_im),
-        SEQ,
-        carry_combine,
-        (unit_ones, zeros_col, zeros_col, zeros_col),
-        True,
+        (total_re, -total_im, first_re, first_im), SEQ, carry_combine, (1.0, 0.0, 0.0, 0.0), True
     )
     later_re, later_im = (back_chained[2], back_chained[3])
     back_lift = jnp.exp(jnp.cumsum(back_keep)[:, None] - positions[:, None] * log_rate[None, :])

time: 188 us -> 176 us (0.936)
  local copies, waits for them, and re-layouts: 52.4 us -> 39.6 us
  waiting for transfers between devices: 32.8 us -> 38.3 us
  blocking collectives: 24.4 us -> 22.4 us
    unnamed x180 -> x112, local copies, waits for them, and re-layouts: 20.8 us -> 12.1 us
    all_to_all x4 -> x6, waiting for transfers between devices: 18.6 us -> 26.1 us  [gather_all(): return lax.all_to_all(spread, axis, 0, 0, tiled=True)]
    slice x4, local copies, waits for them, and re-layouts: 2.34 us -> 0.02 us  [linear_run(): state_re[:, -1]]
    all_to_all x1, blocking collectives: 24.4 us -> 22.4 us  [tree_sum(): mine = jnp.sum(lax.all_to_all(block, axis, 0, 0, tiled=True), axis=0)]
    gather x2 -> x0, local copies, waits for them, and re-layouts: 1.98 us -> none  [tree_fold(): level = jnp.take(stack, jnp.asarray([order[f] for f in flips]), axis=0)]
    ppermute x2, waiting for transfers between devices: 14.2 us -> 12.3 us  [from_behind(): return lax.ppermute(value, axis, pairs)]
    another operation x16 -> x10, other arithmetic: 6.26 us -> 4.97 us
    broadcast_in_dim x4 -> x6, local copies, waits for them, and re-layouts: 3.46 us -> 4.23 us  [gather_all(): spread = jnp.broadcast_to(value[None], (count,) + value.shape)]
  transfers between devices with their start and end apart: 6 -> 8, of which waited for: 3 -> 6; matrix products, arithmetic and copies ran while one was open for 18% -> 16% of each run, Pallas kernels for 0% -> 0%
where the time goes in v9:
time: 176 us; the launch traced here: 174 us
  starting transfers between devices  45.3 us (26%)
  local copies, waits for them, and re-layouts  39.6 us (22%)
  waiting for transfers between devices  38.3 us (22%)
  other arithmetic  23.8 us (14%)
  blocking collectives  22.4 us (13%)
  matrix products  2.45 us (1%)
    all_to_all x6, starting transfers between devices, gather_all(): return lax.all_to_all(spread, axis, 0, 0, tiled=True)  38.4 us
    all_to_all x6, waiting for transfers between devices, gather_all(): return lax.all_to_all(spread, axis, 0, 0, tiled=True)  26.1 us
    all_to_all x1, blocking collectives, tree_sum(): mine = jnp.sum(lax.all_to_all(block, axis, 0, 0, tiled=True), axis=0)  22.4 us
    ppermute x2, waiting for transfers between devices, from_behind(): return lax.ppermute(value, axis, pairs)  12.3 us
    unnamed x112, local copies, waits for them, and re-layouts  12.1 us
    ppermute x2, starting transfers between devices, from_behind(): return lax.ppermute(value, axis, pairs)  6.85 us
    another operation x8, other arithmetic  4.94 us
    broadcast_in_dim x6, local copies, waits for them, and re-layouts, gather_all(): spread = jnp.broadcast_to(value[None], (count,) + value.shape)  4.23 us
  transfers between devices with their start and end apart: 8, of which 6 were waited for; matrix products, arithmetic and copies ran while one was open for 16% of the time, Pallas kernels for 0%

profile of v9, /device:TPU:56, one launch (start us, length us, event | category | flops | bytes accessed | tf_op | source)
XLA Modules:
  0.0 173.8 jit_solution(6953170555336644672)
XLA Ops:
  0.6 0.7 slice.414
  1.6 3.5 %collective-permute-start = (bf16[3,512]{0,1:T(8,128)(2,1)S(1)}, bf16[3,512]{0,1:T(8,128)(2,1)S(1)}, u32[]{:S(2)}, u32[]{:S(2)}) collective-permute-start(bf16[3,512]{0,1:T(8,128)(2,1)S(1)} %copy.234), channel_id=1, source_target_pairs={{0,8},{8,16},{16,24},{24,32},{32,40},{40,48},{48,56},{56,64},{64,7... | collective-permute-start | bytes 9224 | tf_op jit(solution)/shard_map/ppermute | solution.py:12
  8.4 1.3 fusion.207
  9.6 2.5 %multiply_cosine_fusion.1 = (f32[64,512]{1,0:T(8,128)}, f32[64,512]{1,0:T(8,128)}, f32[64,512]{1,0:T(8,128)S(1)}, f32[64,512]{1,0:T(8,128)S(1)}, f32[64,512]{1,0...) fusion(f32[512]{0:T(512)S(1)} %get-tuple-element.440, ...), kind=kLoop, calls=%fused_computation.112 | loop fusion | flops 196608 | bytes 1317120 | tf_op jit(solution)/shard_map/cos | solution.py:110
  12.2 0.8 subtract_exponential_fusion.1
  13.0 0.7 fusion.51
  14.5 1.1 fusion.18
  19.9 0.8 multiply_subtract_fusion.27
  20.7 0.6 broadcast_in_dim.25
  21.3 6.8 %all-to-all-start = ((f32[8,4,512]{2,1,0:T(4,128)}), f32[8,4,512]{2,1,0:T(4,128)}, u32[]{:S(2)}, u32[]{:S(2)}) async-start(f32[8,4,512]{2,1,0:T(4,128)} %broadcast_in_dim.25), calls=%async_computation | async-start | bytes 131072 | tf_op jit(solution)/shard_map/all_to_all | solution.py:32
  28.4 0.7 mul.7850
  29.1 0.7 mul.7853
  29.7 0.7 sub.2439
  30.5 1.1 sub.2440
  31.5 0.9 copy.233
  32.5 0.9 copy.239
  33.4 1.0 copy.241
  34.5 0.9 copy.242
  35.6 0.9 copy.243
  36.7 0.9 copy.245
  39.3 0.8 copy-done.2
  40.3 0.8 copy-done.5
  41.2 1.1 squeeze.109
  42.3 0.9 copy.244
  43.2 0.9 copy.246
  44.1 0.9 copy.238
  45.1 0.9 copy.240
  46.0 0.9 multiply_subtract_fusion.20
  46.9 1.1 fusion.102
  48.0 0.8 multiply_add_fusion.20
  48.8 0.6 broadcast_in_dim.26
  49.5 9.6 %all-to-all-start.1 = ((f32[8,4,512]{2,1,0:T(4,128)}), f32[8,4,512]{2,1,0:T(4,128)S(1)}, u32[]{:S(2)}, u32[]{:S(2)}) async-start(f32[8,4,512]{2,1,0:T(4,128)} %broadcast_in_dim.26), calls=%async_computation.1 | async-start | bytes 131072 | tf_op jit(solution)/shard_map/all_to_all | solution.py:32
  59.2 8.3 %all-to-all-done.1 = f32[8,4,512]{2,1,0:T(4,128)S(1)} async-done(((f32[8,4,512]{2,1,0:T(4,128)}), f32[8,4,512]{2,1,0:T(4,128)S(1)}, u32[]{:S(2)}, u32[]{:S(2)}) %all-to-all-start.1) | async-done | bytes 65568 | tf_op jit(solution)/shard_map/all_to_all | solution.py:32
  68.5 2.6 %subtract_convert_fusion = (bf16[128,8,64]{0,2,1:T(8,128)(2,1)S(1)}, bf16[128,8,64]{0,2,1:T(8,128)(2,1)S(1)}) fusion(f32[128,8,64]{0,2,1:T(8,128)} %copy.246, f32[128,8,64]{0,2,1:T(8,128)} %copy.244, f32[128,8,64]{0,2,1:T(8,128)} %copy.240, f32[128,8,64]{0,2,1:T(8,128)S(1)} %copy-done.8, f32[128,8,64]{0,2,1:T(8,128)} %copy.238, ...), kind=kLoop, calls=%fused_computation.100 | loop fusion | flops 2293760 | bytes 2893312 | tf_op jit(solution)/shard_map/convert.4
  71.9 0.7 multiply_reduce_fusion.5
  73.2 4.3 %all-to-all-start.2 = ((f32[8,2,128]{2,1,0:T(2,128)}), f32[8,2,128]{2,1,0:T(2,128)S(1)}, u32[]{:S(2)}, u32[]{:S(2)}) async-start(f32[8,2,128]{2,1,0:T(2,128)} %broadcast_in_dim.27), calls=%async_computation.2 | async-start | bytes 16384 | tf_op jit(solution)/shard_map/all_to_all | solution.py:32
  77.5 0.7 copy-done.38
  79.3 3.5 %all-to-all-done.2 = f32[8,2,128]{2,1,0:T(2,128)S(1)} async-done(((f32[8,2,128]{2,1,0:T(2,128)}), f32[8,2,128]{2,1,0:T(2,128)S(1)}, u32[]{:S(2)}, u32[]{:S(2)}) %all-to-all-start.2) | async-done | bytes 8224 | tf_op jit(solution)/shard_map/all_to_all | solution.py:32
  84.6 0.8 add_multiply_fusion.2
  85.4 0.6 copy-done.19
  86.8 0.6 copy-done.41
  87.5 0.6 copy-done.39
  88.2 0.6 broadcast_in_dim.28
  88.8 7.2 %all-to-all-start.3 = ((f32[8,4,512]{2,1,0:T(4,128)}), f32[8,4,512]{2,1,0:T(4,128)S(1)}, u32[]{:S(2)}, u32[]{:S(2)}) async-start(f32[8,4,512]{2,1,0:T(4,128)} %broadcast_in_dim.28), calls=%async_computation.3 | async-start | bytes 131072 | tf_op jit(solution)/shard_map/all_to_all | solution.py:32
  96.3 5.1 %all-to-all-done.3 = f32[8,4,512]{2,1,0:T(4,128)S(1)} async-done(((f32[8,4,512]{2,1,0:T(4,128)}), f32[8,4,512]{2,1,0:T(4,128)S(1)}, u32[]{:S(2)}, u32[]{:S(2)}) %all-to-all-start.3) | async-done | bytes 65568 | tf_op jit(solution)/shard_map/all_to_all | solution.py:32
  101.5 0.6 broadcast_in_dim.29
  102.2 3.4 %all-to-all-start.4 = ((f32[8,4,512]{2,1,0:T(4,128)}), f32[8,4,512]{2,1,0:T(4,128)S(1)}, u32[]{:S(2)}, u32[]{:S(2)}) async-start(f32[8,4,512]{2,1,0:T(4,128)} %broadcast_in_dim.29), calls=%async_computation.4 | async-start | bytes 131072 | tf_op jit(solution)/shard_map/all_to_all | solution.py:32
  105.6 8.2 %all-to-all-done.4 = f32[8,4,512]{2,1,0:T(4,128)S(1)} async-done(((f32[8,4,512]{2,1,0:T(4,128)}), f32[8,4,512]{2,1,0:T(4,128)S(1)}, u32[]{:S(2)}, u32[]{:S(2)}) %all-to-all-start.4) | async-done | bytes 65568 | tf_op jit(solution)/shard_map/all_to_all | solution.py:32
  114.1 0.7 copy-done.21
  114.8 1.1 multiply_subtract_fusion
  117.6 0.6 copy-done.12
  118.6 0.7 multiply_reduce_fusion.3
  119.4 0.8 all_to_all.30
  120.2 22.4 %all_to_all.40 = f32[64,1,2080]{2,1,0:T(1,128)S(1)} all-to-all(f32[64,1,2080]{2,1,0:T(1,128)S(1)} %all_to_all.30), channel_id=1, replica_groups=mesh['z'=8,'y'=8,'chan'=8] {'z','y'}, dimensions={0} | all-to-all | bytes 1064960 | tf_op jit(solution)/shard_map/all_to_all | solution.py:68
  142.9 1.1 broadcast_in_dim.30
  144.0 7.2 %all-to-all-start.6 = ((f32[64,1,2080]{2,1,0:T(1,128)}), f32[64,1,2080]{2,1,0:T(1,128)S(1)}, u32[]{:S(2)}, u32[]{:S(2)}) async-start(f32[64,1,2080]{2,1,0:T(1,128)} %broadcast_in_dim.30), calls=%async_computation.6 | async-start | bytes 1114112 | tf_op jit(solution)/shard_map/all_to_all | solution.py:32
  151.2 3.4 %collective-permute-start.1 = (f32[3,512]{0,1:T(8,128)S(1)}, f32[3,512]{0,1:T(8,128)S(1)}, u32[]{:S(2)}, u32[]{:S(2)}) collective-permute-start(f32[3,512]{0,1:T(8,128)S(1)} %bitcast.1377), channel_id=1, source_target_pairs={{8,0},{16,8},{24,16},{32,24},{40,32},{48,40},{56,48},{64,56},{72,6... | collective-permute-start | bytes 18440 | tf_op jit(solution)/shard_map/ppermute | solution.py:12
  154.6 0.8 copy.267
  155.3 12.3 %collective-permute-done.1 = f32[3,512]{0,1:T(8,128)S(1)} collective-permute-done((f32[3,512]{0,1:T(8,128)S(1)}, f32[3,512]{0,1:T(8,128)S(1)}, u32[]{:S(2)}, u32[]{:S(2)}) %collective-permute-start.1) | collective-permute-done | bytes 6176 | tf_op jit(solution)/shard_map/ppermute | solution.py:12
  167.6 0.7 fusion.28
  168.3 0.8 copy.268
  169.1 1.0 all-to-all-done.6
  170.1 1.3 reduce.11
  172.4 0.8 fusion.202
  (249 shorter events, 22.2 us)
Async XLA Ops:
  0.6 70.5 %copy-start = (bf16[8,64,128]{2,1,0:T(8,128)(2,1)S(1)}, bf16[8,64,128]{2,1,0:T(8,128)(2,1)}, u32[]{:S(2)}) copy-start(bf16[8,64,128]{2,1,0:T(8,128)(2,1)} %param.19) | copy-start | bytes 393220
  1.6 3.5 %copy-start.51 = (f32[128]{0:T(128)S(1)}, f32[128]{0:T(128)}, u32[]{:S(2)}) copy-start(f32[128]{0:T(128)} %param.22) | copy-start | bytes 1540
  1.6 13.9 %collective-permute-start = (bf16[3,512]{0,1:T(8,128)(2,1)S(1)}, bf16[3,512]{0,1:T(8,128)(2,1)S(1)}, u32[]{:S(2)}, u32[]{:S(2)}) collective-permute-start(bf16[3,512]{0,1:T(8,128)(2,1)S(1)} %copy.234), channel_id=1, source_target_pairs={{0,8},{8,16},{16,24},{24,32},{32,40},{40,48},{48,56},{56,64},{64,7... | collective-permute-start | bytes 9224 | tf_op jit(solution)/shard_map/ppermute | solution.py:12
  5.7 0.6 copy-start.44
  7.7 4.5 %copy-start.37 = (f32[2,64]{1,0:T(2,128)}, f32[2,64]{1,0:T(2,128)S(1)}, u32[]{:S(2)}) copy-start(f32[2,64]{1,0:T(2,128)S(1)} %reduce.7) | copy-start | bytes 1540
  7.7 0.7 copy-start.18
  7.7 0.7 copy-start.20
  9.6 8.4 %copy-start.30 = (f32[512]{0:T(512)}, f32[512]{0:T(512)S(1)}, u32[]{:S(2)}) copy-start(f32[512]{0:T(512)S(1)} %get-tuple-element.439) | copy-start | bytes 6148
  9.6 11.0 %copy-start.32 = (f32[512]{0:T(512)}, f32[512]{0:T(512)S(1)}, u32[]{:S(2)}) copy-start(f32[512]{0:T(512)S(1)} %get-tuple-element.435) | copy-start | bytes 6148
  12.2 1.5 copy-start.15
  13.0 0.7 copy-start.42
  13.7 2.0 %copy-start.22 = (f32[1,512]{1,0:T(1,128)}, f32[1,512]{1,0:T(1,128)S(1)}, u32[]{:S(2)}) copy-start(f32[1,512]{1,0:T(1,128)S(1)} %get-tuple-element.416) | copy-start | bytes 6148
  13.7 2.0 %copy-start.24 = (f32[1,512]{1,0:T(1,128)}, f32[1,512]{1,0:T(1,128)S(1)}, u32[]{:S(2)}) copy-start(f32[1,512]{1,0:T(1,128)S(1)} %get-tuple-element.417) | copy-start | bytes 6148
  13.7 2.0 %copy-start.26 = (f32[1,512]{1,0:T(1,128)}, f32[1,512]{1,0:T(1,128)S(1)}, u32[]{:S(2)}) copy-start(f32[1,512]{1,0:T(1,128)S(1)} %get-tuple-element.418) | copy-start | bytes 6148
  13.7 2.0 %copy-start.28 = (f32[1,512]{1,0:T(1,128)}, f32[1,512]{1,0:T(1,128)S(1)}, u32[]{:S(2)}) copy-start(f32[1,512]{1,0:T(1,128)S(1)} %get-tuple-element.419) | copy-start | bytes 6148
  14.0 0.5 copy-start.46
  15.7 0.9 copy-start.11
  18.7 0.7 copy-start.3
  18.7 0.8 copy-start.4
  19.2 0.7 copy-start.1
  21.3 24.7 %all-to-all-start = ((f32[8,4,512]{2,1,0:T(4,128)}), f32[8,4,512]{2,1,0:T(4,128)}, u32[]{:S(2)}, u32[]{:S(2)}) async-start(f32[8,4,512]{2,1,0:T(4,128)} %broadcast_in_dim.25), calls=%async_computation | async-start | bytes 131072 | tf_op jit(solution)/shard_map/all_to_all | solution.py:32
  37.7 0.9 copy-start.17
  39.2 0.9 copy-start.2
  40.1 0.9 copy-start.5
  45.1 14.0 %copy-start.16 = (f32[4,512]{1,0:T(4,128)S(1)}, f32[4,512]{1,0:T(4,128)}, u32[]{:S(2)}) copy-start(f32[4,512]{1,0:T(4,128)} %constant.76.clone.1) | copy-start | bytes 24580
  45.1 22.8 %copy-start.9 = (f32[128,8,64]{0,2,1:T(8,128)S(1)}, f32[128,8,64]{0,2,1:T(8,128)}, u32[]{:S(2)}) copy-start(f32[128,8,64]{0,2,1:T(8,128)} %copy.242) | copy-start | bytes 786436
  45.1 22.8 %copy-start.10 = (f32[128,8,64]{0,2,1:T(8,128)S(1)}, f32[128,8,64]{0,2,1:T(8,128)}, u32[]{:S(2)}) copy-start(f32[128,8,64]{0,2,1:T(8,128)} %copy.243) | copy-start | bytes 786436
  46.0 21.9 %copy-start.36 = (f32[8,64]{1,0:T(8,128)S(1)}, f32[8,64]{1,0:T(8,128)}, u32[]{:S(2)}) copy-start(f32[8,64]{1,0:T(8,128)} %mul.7853) | copy-start | bytes 6148
  46.9 21.0 %copy-start.8 = (f32[128,8,64]{0,2,1:T(8,128)S(1)}, f32[128,8,64]{0,2,1:T(8,128)}, u32[]{:S(2)}) copy-start(f32[128,8,64]{0,2,1:T(8,128)} %copy.241) | copy-start | bytes 786436
  49.5 18.4 %copy-start.6 = (f32[128,8,64]{0,2,1:T(8,128)S(1)}, f32[128,8,64]{0,2,1:T(8,128)}, u32[]{:S(2)}) copy-start(f32[128,8,64]{0,2,1:T(8,128)} %copy.233) | copy-start | bytes 786436
  49.5 18.4 %copy-start.7 = (f32[128,8,64]{0,2,1:T(8,128)S(1)}, f32[128,8,64]{0,2,1:T(8,128)}, u32[]{:S(2)}) copy-start(f32[128,8,64]{0,2,1:T(8,128)} %copy.239) | copy-start | bytes 786436
  49.5 18.0 %all-to-all-start.1 = ((f32[8,4,512]{2,1,0:T(4,128)}), f32[8,4,512]{2,1,0:T(4,128)S(1)}, u32[]{:S(2)}, u32[]{:S(2)}) async-start(f32[8,4,512]{2,1,0:T(4,128)} %broadcast_in_dim.26), calls=%async_computation.1 | async-start | bytes 131072 | tf_op jit(solution)/shard_map/all_to_all | solution.py:32
  67.8 0.7 copy-start.35
  67.8 0.7 copy-start.47
  67.8 0.7 copy-start.48
  67.8 0.7 copy-start.50
  71.1 0.7 copy-start.23
  71.2 0.7 copy-start.25
  71.2 0.7 copy-start.27
  71.2 0.7 copy-start.29
  71.2 0.7 copy-start.34
  71.2 0.7 copy-start.43
  73.2 9.6 %all-to-all-start.2 = ((f32[8,2,128]{2,1,0:T(2,128)}), f32[8,2,128]{2,1,0:T(2,128)S(1)}, u32[]{:S(2)}, u32[]{:S(2)}) async-start(f32[8,2,128]{2,1,0:T(2,128)} %broadcast_in_dim.27), calls=%async_computation.2 | async-start | bytes 16384 | tf_op jit(solution)/shard_map/all_to_all | solution.py:32
  77.5 0.7 copy-start.38
  78.3 0.6 copy-start.49
  84.4 2.0 %copy-start.13 = (f32[64,512]{1,0:T(8,128)S(1)}, f32[64,512]{1,0:T(8,128)}, u32[]{:S(2)}) copy-start(f32[64,512]{1,0:T(8,128)} %get-tuple-element.421) | copy-start | bytes 393220
  84.5 2.0 %copy-start.14 = (f32[64,512]{1,0:T(8,128)S(1)}, f32[64,512]{1,0:T(8,128)}, u32[]{:S(2)}) copy-start(f32[64,512]{1,0:T(8,128)} %get-tuple-element.422) | copy-start | bytes 393220
  85.4 0.7 copy-start.19
  86.7 0.7 copy-start.41
  86.7 0.7 copy-start.40
  86.7 0.7 copy-start.45
  87.5 0.7 copy-start.39
  87.5 0.7 copy-start.33
  88.8 12.6 %all-to-all-start.3 = ((f32[8,4,512]{2,1,0:T(4,128)}), f32[8,4,512]{2,1,0:T(4,128)S(1)}, u32[]{:S(2)}, u32[]{:S(2)}) async-start(f32[8,4,512]{2,1,0:T(4,128)} %broadcast_in_dim.28), calls=%async_computation.3 | async-start | bytes 131072 | tf_op jit(solution)/shard_map/all_to_all | solution.py:32
  102.2 11.7 %all-to-all-start.4 = ((f32[8,4,512]{2,1,0:T(4,128)}), f32[8,4,512]{2,1,0:T(4,128)S(1)}, u32[]{:S(2)}, u32[]{:S(2)}) async-start(f32[8,4,512]{2,1,0:T(4,128)} %broadcast_in_dim.29), calls=%async_computation.4 | async-start | bytes 131072 | tf_op jit(solution)/shard_map/all_to_all | solution.py:32
  114.1 0.7 copy-start.21
  116.0 0.7 copy-start.31
  117.4 0.9 copy-start.12
  144.0 26.1 %all-to-all-start.6 = ((f32[64,1,2080]{2,1,0:T(1,128)}), f32[64,1,2080]{2,1,0:T(1,128)S(1)}, u32[]{:S(2)}, u32[]{:S(2)}) async-start(f32[64,1,2080]{2,1,0:T(1,128)} %broadcast_in_dim.30), calls=%async_computation.6 | async-start | bytes 1114112 | tf_op jit(solution)/shard_map/all_to_all | solution.py:32
  151.2 16.4 %collective-permute-start.1 = (f32[3,512]{0,1:T(8,128)S(1)}, f32[3,512]{0,1:T(8,128)S(1)}, u32[]{:S(2)}, u32[]{:S(2)}) collective-permute-start(f32[3,512]{0,1:T(8,128)S(1)} %bitcast.1377), channel_id=1, source_target_pairs={{8,0},{16,8},{24,16},{32,24},{40,32},{48,40},{56,48},{64,56},{72,6... | collective-permute-start | bytes 18440 | tf_op jit(solution)/shard_map/ppermute | solution.py:12

commit v10 on v9

--- a/solution.py
+++ b/solution.py
@@ -61,12 +61,18 @@
 
 
 def tree_sum(value, axis):
-    count = lax.axis_size(axis)
     flat = value.reshape(-1)
+    count = 1
+    for name in axis:
+        count *= lax.axis_size(name)
     width = -(-flat.size // count)
-    block = jnp.pad(flat, (0, width * count - flat.size)).reshape(count, width)
-    mine = jnp.sum(lax.all_to_all(block, axis, 0, 0, tiled=True), axis=0)
-    return gather_all(mine, axis).reshape(-1)[: flat.size].reshape(value.shape)
+    block = jnp.pad(flat, (0, width * count - flat.size))
+    for name in axis[::-1]:
+        block = block.reshape(lax.axis_size(name), -1)
+        block = jnp.sum(lax.all_to_all(block, name, 0, 0, tiled=True), axis=0)
+    for name in axis:
+        block = gather_all(block, name).reshape(-1)
+    return block[: flat.size].reshape(value.shape)
 
 
 def linear_run(drive_re, drive_im, decay_rate, turn_rate, log_keep):

time: 176 us -> 188 us (1.068)
  blocking collectives: 22.4 us -> 39.7 us
  waiting for transfers between devices: 38.3 us -> 34.1 us
    all_to_all x1 -> x3, blocking collectives: 22.4 us -> 39.7 us  [the longest x2 28.9 us: tree_sum(): block = jnp.sum(lax.all_to_all(block, name, 0, 0, tiled=True), axis=0)]
    ppermute x2, waiting for transfers between devices: 12.3 us -> 9.04 us  [from_behind(): return lax.ppermute(value, axis, pairs)]
    broadcast_in_dim x6 -> x8, local copies, waits for them, and re-layouts: 4.23 us -> 4.35 us  [gather_all(): spread = jnp.broadcast_to(value[None], (count,) + value.shape)]
  transfers between devices with their start and end apart: 8 -> 8, of which waited for: 6 -> 5; matrix products, arithmetic and copies ran while one was open for 16% -> 15% of each run, Pallas kernels for 0% -> 0%
where the time goes in v10:
time: 188 us; the launch traced here: 185 us
  starting transfers between devices  44.3 us (24%)
  blocking collectives  39.7 us (21%)
  local copies, waits for them, and re-layouts  38.2 us (20%)
  waiting for transfers between devices  34.1 us (18%)
  other arithmetic  24.2 us (13%)
  matrix products  2.45 us (1%)
    all_to_all x6, starting transfers between devices, gather_all(): return lax.all_to_all(spread, axis, 0, 0, tiled=True)  37.5 us
    all_to_all x2, blocking collectives, tree_sum(): block = jnp.sum(lax.all_to_all(block, name, 0, 0, tiled=True), axis=0)  28.9 us
    all_to_all x6, waiting for transfers between devices, gather_all(): return lax.all_to_all(spread, axis, 0, 0, tiled=True)  25 us
    unnamed x112, local copies, waits for them, and re-layouts  12.1 us
    all_to_all x1, blocking collectives, gather_all(): return lax.all_to_all(spread, axis, 0, 0, tiled=True)  10.8 us
    ppermute x2, waiting for transfers between devices, from_behind(): return lax.ppermute(value, axis, pairs)  9.04 us
    ppermute x2, starting transfers between devices, from_behind(): return lax.ppermute(value, axis, pairs)  6.84 us
    another operation x8, other arithmetic  5.02 us
  transfers between devices with their start and end apart: 8, of which 5 were waited for; matrix products, arithmetic and copies ran while one was open for 15% of the time, Pallas kernels for 0%

profile of v10, /device:TPU:56, one launch (start us, length us, event | category | flops | bytes accessed | tf_op | source)
XLA Modules:
  0.0 184.8 jit_solution(1040406391710996156)
XLA Ops:
  0.6 0.7 slice.414
  1.6 3.5 %collective-permute-start = (bf16[3,512]{0,1:T(8,128)(2,1)S(1)}, bf16[3,512]{0,1:T(8,128)(2,1)S(1)}, u32[]{:S(2)}, u32[]{:S(2)}) collective-permute-start(bf16[3,512]{0,1:T(8,128)(2,1)S(1)} %copy.235), channel_id=1, source_target_pairs={{0,8},{8,16},{16,24},{24,32},{32,40},{40,48},{48,56},{56,64},{64,7... | collective-permute-start | bytes 9224 | tf_op jit(solution)/shard_map/ppermute | solution.py:12
  6.4 0.7 fusion.140
  8.4 1.3 fusion.207
  9.6 2.5 %multiply_cosine_fusion.1 = (f32[64,512]{1,0:T(8,128)}, f32[64,512]{1,0:T(8,128)}, f32[64,512]{1,0:T(8,128)S(1)}, f32[64,512]{1,0:T(8,128)S(1)}, f32[64,512]{1,0...) fusion(f32[512]{0:T(512)S(1)} %get-tuple-element.440, ...), kind=kLoop, calls=%fused_computation.112 | loop fusion | flops 196608 | bytes 1317120 | tf_op jit(solution)/shard_map/cos | solution.py:116
  12.2 0.8 subtract_exponential_fusion.1
  13.0 0.7 fusion.51
  14.5 1.1 fusion.18
  20.0 0.8 multiply_subtract_fusion.27
  20.8 0.6 broadcast_in_dim.29
  21.4 6.8 %all-to-all-start = ((f32[8,4,512]{2,1,0:T(4,128)}), f32[8,4,512]{2,1,0:T(4,128)}, u32[]{:S(2)}, u32[]{:S(2)}) async-start(f32[8,4,512]{2,1,0:T(4,128)} %broadcast_in_dim.29), calls=%async_computation | async-start | bytes 131072 | tf_op jit(solution)/shard_map/all_to_all | solution.py:32
  28.5 0.6 mul.7850
  29.1 0.7 mul.7853
  29.8 0.7 sub.2439
  30.5 1.1 sub.2440
  31.6 0.9 copy.234
  32.5 0.9 copy.240
  33.5 0.9 copy.242
  34.6 0.9 copy.243
  35.6 0.9 copy.244
  36.7 0.9 copy.246
  39.4 0.8 copy-done.2
  40.4 0.8 copy-done.5
  41.3 1.1 squeeze.109
  42.4 0.9 copy.245
  43.3 0.9 copy.247
  44.2 0.9 copy.239
  45.1 0.9 copy.241
  46.1 0.9 multiply_subtract_fusion.20
  47.0 1.1 fusion.102
  48.0 0.8 multiply_add_fusion.20
  48.9 0.6 broadcast_in_dim.30
  49.5 9.6 %all-to-all-start.1 = ((f32[8,4,512]{2,1,0:T(4,128)}), f32[8,4,512]{2,1,0:T(4,128)S(1)}, u32[]{:S(2)}, u32[]{:S(2)}) async-start(f32[8,4,512]{2,1,0:T(4,128)} %broadcast_in_dim.30), calls=%async_computation.1 | async-start | bytes 131072 | tf_op jit(solution)/shard_map/all_to_all | solution.py:32
  59.2 8.3 %all-to-all-done.1 = f32[8,4,512]{2,1,0:T(4,128)S(1)} async-done(((f32[8,4,512]{2,1,0:T(4,128)}), f32[8,4,512]{2,1,0:T(4,128)S(1)}, u32[]{:S(2)}, u32[]{:S(2)}) %all-to-all-start.1) | async-done | bytes 65568 | tf_op jit(solution)/shard_map/all_to_all | solution.py:32
  68.5 2.6 %subtract_convert_fusion = (bf16[128,8,64]{0,2,1:T(8,128)(2,1)S(1)}, bf16[128,8,64]{0,2,1:T(8,128)(2,1)S(1)}) fusion(f32[128,8,64]{0,2,1:T(8,128)} %copy.247, f32[128,8,64]{0,2,1:T(8,128)} %copy.245, f32[128,8,64]{0,2,1:T(8,128)} %copy.241, f32[128,8,64]{0,2,1:T(8,128)S(1)} %copy-done.8, f32[128,8,64]{0,2,1:T(8,128)} %copy.239, ...), kind=kLoop, calls=%fused_computation.100 | loop fusion | flops 2293760 | bytes 2893312 | tf_op jit(solution)/shard_map/convert.4
  71.9 0.7 multiply_reduce_fusion.5
  73.2 4.3 %all-to-all-start.2 = ((f32[8,2,128]{2,1,0:T(2,128)}), f32[8,2,128]{2,1,0:T(2,128)S(1)}, u32[]{:S(2)}, u32[]{:S(2)}) async-start(f32[8,2,128]{2,1,0:T(2,128)} %broadcast_in_dim.31), calls=%async_computation.2 | async-start | bytes 16384 | tf_op jit(solution)/shard_map/all_to_all | solution.py:32
  77.5 0.6 copy-done.38
  78.3 0.7 copy-done.49
  79.4 3.5 %all-to-all-done.2 = f32[8,2,128]{2,1,0:T(2,128)S(1)} async-done(((f32[8,2,128]{2,1,0:T(2,128)}), f32[8,2,128]{2,1,0:T(2,128)S(1)}, u32[]{:S(2)}, u32[]{:S(2)}) %all-to-all-start.2) | async-done | bytes 8224 | tf_op jit(solution)/shard_map/all_to_all | solution.py:32
  84.6 0.8 add_multiply_fusion.2
  85.4 0.7 copy-done.19
  87.5 0.7 copy-done.39
  88.1 0.6 broadcast_in_dim.32
  88.8 7.2 %all-to-all-start.3 = ((f32[8,4,512]{2,1,0:T(4,128)}), f32[8,4,512]{2,1,0:T(4,128)S(1)}, u32[]{:S(2)}, u32[]{:S(2)}) async-start(f32[8,4,512]{2,1,0:T(4,128)} %broadcast_in_dim.32), calls=%async_computation.3 | async-start | bytes 131072 | tf_op jit(solution)/shard_map/all_to_all | solution.py:32
  96.2 5.1 %all-to-all-done.3 = f32[8,4,512]{2,1,0:T(4,128)S(1)} async-done(((f32[8,4,512]{2,1,0:T(4,128)}), f32[8,4,512]{2,1,0:T(4,128)S(1)}, u32[]{:S(2)}, u32[]{:S(2)}) %all-to-all-start.3) | async-done | bytes 65568 | tf_op jit(solution)/shard_map/all_to_all | solution.py:32
  101.5 0.6 broadcast_in_dim.33
  102.1 3.4 %all-to-all-start.4 = ((f32[8,4,512]{2,1,0:T(4,128)}), f32[8,4,512]{2,1,0:T(4,128)S(1)}, u32[]{:S(2)}, u32[]{:S(2)}) async-start(f32[8,4,512]{2,1,0:T(4,128)} %broadcast_in_dim.33), calls=%async_computation.4 | async-start | bytes 131072 | tf_op jit(solution)/shard_map/all_to_all | solution.py:32
  105.6 8.2 %all-to-all-done.4 = f32[8,4,512]{2,1,0:T(4,128)S(1)} async-done(((f32[8,4,512]{2,1,0:T(4,128)}), f32[8,4,512]{2,1,0:T(4,128)S(1)}, u32[]{:S(2)}, u32[]{:S(2)}) %all-to-all-start.4) | async-done | bytes 65568 | tf_op jit(solution)/shard_map/all_to_all | solution.py:32
  114.0 0.7 copy-done.21
  114.7 1.1 multiply_subtract_fusion
  118.6 0.7 multiply_reduce_fusion.3
  119.4 18.1 %all_to_all.56 = f32[8,1,16640]{2,1,0:T(1,128)S(1)} all-to-all(f32[8,1,16640]{2,1,0:T(1,128)S(1)} %bitcast.1364), channel_id=1, replica_groups=mesh['z'=8,'y'=8,'chan'=8] {'y'}, dimensions={0} | all-to-all | bytes 1064960 | tf_op jit(solution)/shard_map/all_to_all | solution.py:72
  138.0 10.8 %all_to_all.57 = f32[8,1,2080]{2,1,0:T(1,128)S(1)} all-to-all(f32[8,1,2080]{2,1,0:T(1,128)S(1)} %all_to_all.42), channel_id=1, replica_groups=mesh['z'=8,'y'=8,'chan'=8] {'z'}, dimensions={0} | all-to-all | bytes 133120 | tf_op jit(solution)/shard_map/all_to_all | solution.py:72
  148.9 10.8 %all_to_all.55 = f32[8,1,2080]{2,1,0:T(1,128)S(1)} all-to-all(f32[8,1,2080]{2,1,0:T(1,128)S(1)} %broadcast_in_dim.34), channel_id=1, replica_groups=mesh['z'=8,'y'=8,'chan'=8] {'z'}, dimensions={0} | all-to-all | bytes 133120 | tf_op jit(solution)/shard_map/all_to_all | solution.py:32
  159.9 1.1 broadcast_in_dim.36
  161.0 6.2 %all-to-all-start.8 = ((f32[8,1,16640]{2,1,0:T(1,128)}), f32[8,1,16640]{2,1,0:T(1,128)S(1)}, u32[]{:S(2)}, u32[]{:S(2)}) async-start(f32[8,1,16640]{2,1,0:T(1,128)} %broadcast_in_dim.36), calls=%async_computation.8 | async-start | bytes 1064960 | tf_op jit(solution)/shard_map/all_to_all | solution.py:32
  167.2 3.4 %collective-permute-start.1 = (f32[3,512]{0,1:T(8,128)S(1)}, f32[3,512]{0,1:T(8,128)S(1)}, u32[]{:S(2)}, u32[]{:S(2)}) collective-permute-start(f32[3,512]{0,1:T(8,128)S(1)} %bitcast.1381), channel_id=1, source_target_pairs={{8,0},{16,8},{24,16},{32,24},{40,32},{48,40},{56,48},{64,56},{72,6... | collective-permute-start | bytes 18440 | tf_op jit(solution)/shard_map/ppermute | solution.py:12
  170.6 0.8 copy.269
  171.4 9.0 %collective-permute-done.1 = f32[3,512]{0,1:T(8,128)S(1)} collective-permute-done((f32[3,512]{0,1:T(8,128)S(1)}, f32[3,512]{0,1:T(8,128)S(1)}, u32[]{:S(2)}, u32[]{:S(2)}) %collective-permute-start.1) | collective-permute-done | bytes 6176 | tf_op jit(solution)/shard_map/ppermute | solution.py:12
  180.4 0.7 fusion.28
  181.1 0.8 copy.270
  181.9 1.3 reduce.13
  184.0 0.8 fusion.202
  (254 shorter events, 22.0 us)
Async XLA Ops:
  0.6 70.5 %copy-start = (bf16[8,64,128]{2,1,0:T(8,128)(2,1)S(1)}, bf16[8,64,128]{2,1,0:T(8,128)(2,1)}, u32[]{:S(2)}) copy-start(bf16[8,64,128]{2,1,0:T(8,128)(2,1)} %param.19) | copy-start | bytes 393220
  1.6 3.5 %copy-start.51 = (f32[128]{0:T(128)S(1)}, f32[128]{0:T(128)}, u32[]{:S(2)}) copy-start(f32[128]{0:T(128)} %param.22) | copy-start | bytes 1540
  1.6 14.0 %collective-permute-start = (bf16[3,512]{0,1:T(8,128)(2,1)S(1)}, bf16[3,512]{0,1:T(8,128)(2,1)S(1)}, u32[]{:S(2)}, u32[]{:S(2)}) collective-permute-start(bf16[3,512]{0,1:T(8,128)(2,1)S(1)} %copy.235), channel_id=1, source_target_pairs={{0,8},{8,16},{16,24},{24,32},{32,40},{40,48},{48,56},{56,64},{64,7... | collective-permute-start | bytes 9224 | tf_op jit(solution)/shard_map/ppermute | solution.py:12
  5.7 0.5 copy-start.44
  7.6 4.5 %copy-start.37 = (f32[2,64]{1,0:T(2,128)}, f32[2,64]{1,0:T(2,128)S(1)}, u32[]{:S(2)}) copy-start(f32[2,64]{1,0:T(2,128)S(1)} %reduce.8) | copy-start | bytes 1540
  7.7 0.7 copy-start.18
  7.7 0.7 copy-start.20
  9.6 8.5 %copy-start.30 = (f32[512]{0:T(512)}, f32[512]{0:T(512)S(1)}, u32[]{:S(2)}) copy-start(f32[512]{0:T(512)S(1)} %get-tuple-element.439) | copy-start | bytes 6148
  9.6 11.1 %copy-start.32 = (f32[512]{0:T(512)}, f32[512]{0:T(512)S(1)}, u32[]{:S(2)}) copy-start(f32[512]{0:T(512)S(1)} %get-tuple-element.435) | copy-start | bytes 6148
  12.2 1.5 copy-start.15
  13.0 0.7 copy-start.42
  13.7 2.1 %copy-start.22 = (f32[1,512]{1,0:T(1,128)}, f32[1,512]{1,0:T(1,128)S(1)}, u32[]{:S(2)}) copy-start(f32[1,512]{1,0:T(1,128)S(1)} %get-tuple-element.416) | copy-start | bytes 6148
  13.7 2.1 %copy-start.24 = (f32[1,512]{1,0:T(1,128)}, f32[1,512]{1,0:T(1,128)S(1)}, u32[]{:S(2)}) copy-start(f32[1,512]{1,0:T(1,128)S(1)} %get-tuple-element.417) | copy-start | bytes 6148
  13.7 2.1 %copy-start.26 = (f32[1,512]{1,0:T(1,128)}, f32[1,512]{1,0:T(1,128)S(1)}, u32[]{:S(2)}) copy-start(f32[1,512]{1,0:T(1,128)S(1)} %get-tuple-element.418) | copy-start | bytes 6148
  13.7 2.1 %copy-start.28 = (f32[1,512]{1,0:T(1,128)}, f32[1,512]{1,0:T(1,128)S(1)}, u32[]{:S(2)}) copy-start(f32[1,512]{1,0:T(1,128)S(1)} %get-tuple-element.419) | copy-start | bytes 6148
  13.9 0.6 copy-start.46
  15.8 0.9 copy-start.11
  18.8 0.7 copy-start.3
  18.8 0.8 copy-start.4
  19.3 0.7 copy-start.1
  21.4 24.7 %all-to-all-start = ((f32[8,4,512]{2,1,0:T(4,128)}), f32[8,4,512]{2,1,0:T(4,128)}, u32[]{:S(2)}, u32[]{:S(2)}) async-start(f32[8,4,512]{2,1,0:T(4,128)} %broadcast_in_dim.29), calls=%async_computation | async-start | bytes 131072 | tf_op jit(solution)/shard_map/all_to_all | solution.py:32
  37.6 0.9 copy-start.17
  39.3 0.9 copy-start.2
  40.2 0.9 copy-start.5
  45.1 14.0 %copy-start.16 = (f32[4,512]{1,0:T(4,128)S(1)}, f32[4,512]{1,0:T(4,128)}, u32[]{:S(2)}) copy-start(f32[4,512]{1,0:T(4,128)} %constant.76.clone.1) | copy-start | bytes 24580
  45.1 22.8 %copy-start.9 = (f32[128,8,64]{0,2,1:T(8,128)S(1)}, f32[128,8,64]{0,2,1:T(8,128)}, u32[]{:S(2)}) copy-start(f32[128,8,64]{0,2,1:T(8,128)} %copy.243) | copy-start | bytes 786436
  45.1 22.8 %copy-start.10 = (f32[128,8,64]{0,2,1:T(8,128)S(1)}, f32[128,8,64]{0,2,1:T(8,128)}, u32[]{:S(2)}) copy-start(f32[128,8,64]{0,2,1:T(8,128)} %copy.244) | copy-start | bytes 786436
  46.1 21.8 %copy-start.36 = (f32[8,64]{1,0:T(8,128)S(1)}, f32[8,64]{1,0:T(8,128)}, u32[]{:S(2)}) copy-start(f32[8,64]{1,0:T(8,128)} %mul.7853) | copy-start | bytes 6148
  47.0 21.0 %copy-start.8 = (f32[128,8,64]{0,2,1:T(8,128)S(1)}, f32[128,8,64]{0,2,1:T(8,128)}, u32[]{:S(2)}) copy-start(f32[128,8,64]{0,2,1:T(8,128)} %copy.242) | copy-start | bytes 786436
  49.5 18.4 %copy-start.6 = (f32[128,8,64]{0,2,1:T(8,128)S(1)}, f32[128,8,64]{0,2,1:T(8,128)}, u32[]{:S(2)}) copy-start(f32[128,8,64]{0,2,1:T(8,128)} %copy.234) | copy-start | bytes 786436
  49.5 18.4 %copy-start.7 = (f32[128,8,64]{0,2,1:T(8,128)S(1)}, f32[128,8,64]{0,2,1:T(8,128)}, u32[]{:S(2)}) copy-start(f32[128,8,64]{0,2,1:T(8,128)} %copy.240) | copy-start | bytes 786436
  49.5 18.0 %all-to-all-start.1 = ((f32[8,4,512]{2,1,0:T(4,128)}), f32[8,4,512]{2,1,0:T(4,128)S(1)}, u32[]{:S(2)}, u32[]{:S(2)}) async-start(f32[8,4,512]{2,1,0:T(4,128)} %broadcast_in_dim.30), calls=%async_computation.1 | async-start | bytes 131072 | tf_op jit(solution)/shard_map/all_to_all | solution.py:32
  67.8 0.7 copy-start.35
  67.8 0.7 copy-start.47
  67.8 0.7 copy-start.48
  67.8 0.7 copy-start.50
  71.2 0.6 copy-start.23
  71.2 0.7 copy-start.25
  71.2 0.7 copy-start.27
  71.2 0.7 copy-start.29
  71.2 0.7 copy-start.34
  71.2 0.7 copy-start.43
  73.2 9.6 %all-to-all-start.2 = ((f32[8,2,128]{2,1,0:T(2,128)}), f32[8,2,128]{2,1,0:T(2,128)S(1)}, u32[]{:S(2)}, u32[]{:S(2)}) async-start(f32[8,2,128]{2,1,0:T(2,128)} %broadcast_in_dim.31), calls=%async_computation.2 | async-start | bytes 16384 | tf_op jit(solution)/shard_map/all_to_all | solution.py:32
  77.5 0.7 copy-start.38
  78.3 0.7 copy-start.49
  84.5 2.0 %copy-start.13 = (f32[64,512]{1,0:T(8,128)S(1)}, f32[64,512]{1,0:T(8,128)}, u32[]{:S(2)}) copy-start(f32[64,512]{1,0:T(8,128)} %get-tuple-element.421) | copy-start | bytes 393220
  84.5 2.0 %copy-start.14 = (f32[64,512]{1,0:T(8,128)S(1)}, f32[64,512]{1,0:T(8,128)}, u32[]{:S(2)}) copy-start(f32[64,512]{1,0:T(8,128)} %get-tuple-element.422) | copy-start | bytes 393220
  85.4 0.7 copy-start.19
  86.7 0.6 copy-start.41
  86.8 0.6 copy-start.40
  86.8 0.6 copy-start.45
  87.4 0.7 copy-start.39
  87.4 0.7 copy-start.33
  88.8 12.6 %all-to-all-start.3 = ((f32[8,4,512]{2,1,0:T(4,128)}), f32[8,4,512]{2,1,0:T(4,128)S(1)}, u32[]{:S(2)}, u32[]{:S(2)}) async-start(f32[8,4,512]{2,1,0:T(4,128)} %broadcast_in_dim.32), calls=%async_computation.3 | async-start | bytes 131072 | tf_op jit(solution)/shard_map/all_to_all | solution.py:32
  102.1 11.7 %all-to-all-start.4 = ((f32[8,4,512]{2,1,0:T(4,128)}), f32[8,4,512]{2,1,0:T(4,128)S(1)}, u32[]{:S(2)}, u32[]{:S(2)}) async-start(f32[8,4,512]{2,1,0:T(4,128)} %broadcast_in_dim.33), calls=%async_computation.4 | async-start | bytes 131072 | tf_op jit(solution)/shard_map/all_to_all | solution.py:32
  114.0 0.7 copy-start.21
  116.0 0.7 copy-start.31
  117.3 0.9 copy-start.12
  161.0 20.9 %all-to-all-start.8 = ((f32[8,1,16640]{2,1,0:T(1,128)}), f32[8,1,16640]{2,1,0:T(1,128)S(1)}, u32[]{:S(2)}, u32[]{:S(2)}) async-start(f32[8,1,16640]{2,1,0:T(1,128)} %broadcast_in_dim.36), calls=%async_computation.8 | async-start | bytes 1064960 | tf_op jit(solution)/shard_map/all_to_all | solution.py:32
  167.2 13.2 %collective-permute-start.1 = (f32[3,512]{0,1:T(8,128)S(1)}, f32[3,512]{0,1:T(8,128)S(1)}, u32[]{:S(2)}, u32[]{:S(2)}) collective-permute-start(f32[3,512]{0,1:T(8,128)S(1)} %bitcast.1381), channel_id=1, source_target_pairs={{8,0},{16,8},{24,16},{32,24},{40,32},{48,40},{56,48},{64,56},{72,6... | collective-permute-start | bytes 18440 | tf_op jit(solution)/shard_map/ppermute | solution.py:12
